TPU v7x, 128 devices: a whole 4x4x4 slice. The times are simulated.
128 devices in a mesh: elem: 32 (over y, z, core), sub: 4 (over x).
Axes of the slice: x: 4, y: 4, z: 4, core: 2. Of those that a mesh axis runs over, the one named last changes fastest.
Arguments:
- tracers: bfloat16 [1024, 128, 1024], P('elem', 'sub'), may hold values from -6 to 6
- metric_x: float32 [1024, 128], P('elem', 'sub'), may hold values from 0.5 to 2
- metric_y: float32 [1024, 128], P('elem', 'sub'), may hold values from 0.5 to 2
- mass_weight: float32 [1024, 128], P('elem', 'sub'), may hold values from 0.5 to 2
- mass_inverse: float32 [1024, 128], P('elem', 'sub'), may hold values from 0.25 to 1
- phys_slot: int32 [32768], P(('elem', 'sub')), may hold values from 0 to 32767, as said below
- diff_inverse: bfloat16 [2048, 128, 128], P(('elem', 'sub')), may hold values from -0.1 to 0.8
- span_cost: int32 [2048], P(('elem', 'sub')), may hold values from 1 to 4, as said below
Outputs:
- tracers_out: bfloat16 [1024, 128, 1024], P('elem', 'sub')
Inputs may be any that keep to these rules, and one draw needn't show every extreme that they name: `phys_slot`: A permutation of the columns. Every device sends exactly 4 of its columns to each of 64 devices (slot // 256 is the device of a slot) and none to the others, and every device receives exactly 256 columns. `span_cost`: 4 is reached in every draw.
All inputs are finite; a program needn't handle non-finite values.
Results may differ from a plain program's by a relative error of at most 0.009.
Values may be sent and summed in bfloat16 or wider, within the bound.
No kernel may reach another device: no remote copies, remote signals or barrier semaphores. Data moves between devices by JAX's collectives and lax.ppermute only.
A program may use at most 64 MiB of HBM per device.

v0:
```python
import math

import jax
import jax.numpy as jnp
import numpy as np
from jax import lax
from jax.sharding import PartitionSpec as P

diffusion_nu = 0.01


def padded_2(cells, sides, width):
    for axis, dim in sides:
        count = lax.axis_size(axis)
        head = lax.slice_in_dim(cells, 0, width, axis=dim)
        tail = lax.slice_in_dim(cells, cells.shape[dim] - width, cells.shape[dim], axis=dim)
        cells = jnp.concatenate(
            [
                lax.ppermute(tail, axis, [(i, (i + 1) % count) for i in range(count)]),
                cells,
                lax.ppermute(head, axis, [((i + 1) % count, i) for i in range(count)]),
            ],
            axis=dim,
        )
    return cells


def gll_matrix():
    gll_nodes = np.array([-1.0, -1.0 / math.sqrt(5.0), 1.0 / math.sqrt(5.0), 1.0])
    result = np.zeros((4, 4))
    for row_node in range(4):
        for col_node in range(4):
            if row_node == col_node:
                total = 0.0
                for other_node in range(4):
                    if other_node != row_node:
                        total += 1.0 / (gll_nodes[row_node] - gll_nodes[other_node])
                result[row_node, col_node] = total
            else:
                product_top = 1.0
                product_low = 1.0
                for other_node in range(4):
                    if other_node != col_node:
                        product_low *= gll_nodes[col_node] - gll_nodes[other_node]
                        if other_node != row_node:
                            product_top *= gll_nodes[row_node] - gll_nodes[other_node]
                result[row_node, col_node] = product_top / product_low
    return result


def node_mix(matrix, blocks, axis):
    pieces = [lax.index_in_dim(blocks, node, axis, keepdims=True) for node in range(4)]
    outputs = []
    for row_node in range(4):
        total = float(matrix[row_node, 0]) * pieces[0]
        for col_node in range(1, 4):
            total = total + float(matrix[row_node, col_node]) * pieces[col_node]
        outputs.append(total)
    return jnp.concatenate(outputs, axis=axis)


def local_section(values, metric_x, metric_y):
    elem_rows = values.shape[0] // 4
    elem_cols = values.shape[1] // 4
    features = values.shape[2]
    derivative = gll_matrix()
    blocks = values.astype(jnp.float32).reshape(elem_rows, 4, elem_cols, 4, features)
    scale_x = metric_x.reshape(elem_rows, 4, elem_cols, 4, 1)
    scale_y = metric_y.reshape(elem_rows, 4, elem_cols, 4, 1)
    slope_x = node_mix(derivative, blocks, 1)
    weak_x = node_mix(derivative.T, scale_x * slope_x, 1)
    slope_y = node_mix(derivative, blocks, 3)
    weak_y = node_mix(derivative.T, scale_y * slope_y, 3)
    section_field = blocks - diffusion_nu * (weak_x + weak_y)
    return section_field.reshape(values.shape)


def edge_masks(point_count):
    position = jnp.arange(point_count) % 4
    return ((position == 0).astype(jnp.float32), (position == 3).astype(jnp.float32))


def on_device(
    tracers, metric_x, metric_y, mass_weight, mass_inverse, phys_slot, diff_inverse, span_cost
):
    point_rows, point_cols, features = tracers.shape
    section_field = local_section(tracers, metric_x, metric_y)
    weighted = mass_weight[:, :, None] * section_field
    padded = padded_2(weighted, (("elem", 0), ("sub", 1)), 1)
    first_row, last_row = edge_masks(point_rows)
    along_x = (
        padded[1:-1] + first_row[:, None, None] * padded[:-2] + last_row[:, None, None] * padded[2:]
    )
    first_col, last_col = edge_masks(point_cols)
    summed = (
        along_x[:, 1:-1]
        + first_col[None, :, None] * along_x[:, :-2]
        + last_col[None, :, None] * along_x[:, 2:]
    )
    settled = (mass_inverse[:, :, None] * summed).astype(jnp.bfloat16)
    settled_wide = settled.astype(jnp.float32)
    numerator = (
        (mass_weight[:, :, None] * settled_wide)
        .reshape(point_rows // 2, 2, point_cols // 2, 2, features)
        .sum(axis=(1, 3))
    )
    denominator = mass_weight.reshape(point_rows // 2, 2, point_cols // 2, 2).sum(axis=(1, 3))
    columns = (numerator / denominator[:, :, None]).astype(jnp.bfloat16).reshape(-1, features)
    column_count = columns.shape[0]
    device_count = lax.axis_size(("elem", "sub"))
    capacity = max(1, 2 * column_count // device_count)
    slot_total = device_count * capacity
    target = phys_slot // column_count
    landing = phys_slot % column_count
    column_order = jnp.arange(column_count)
    earlier = (target[None, :] == target[:, None]) & (column_order[None, :] < column_order[:, None])
    position = jnp.sum(earlier.astype(jnp.int32), axis=1)
    dest_row = target * capacity + position
    slot_order = jnp.arange(slot_total)
    send_table = (slot_order[:, None] == dest_row[None, :]).astype(jnp.bfloat16)
    outgoing = jnp.dot(send_table, columns, preferred_element_type=jnp.float32).astype(jnp.bfloat16)
    label_values = jnp.dot(
        send_table.astype(jnp.float32),
        (landing + 1).astype(jnp.float32),
        precision=lax.Precision.HIGHEST,
    )
    labels = label_values.astype(jnp.int32) - 1
    outgoing = outgoing.reshape(device_count, capacity, features)
    labels = labels.reshape(device_count, capacity)
    arrived, arrived_labels = (
        lax.all_to_all(outgoing, ("elem", "sub"), split_axis=0, concat_axis=0, tiled=True),
        lax.all_to_all(labels, ("elem", "sub"), split_axis=0, concat_axis=0, tiled=True),
    )
    arrived = arrived.reshape(-1, features)
    arrived_labels = arrived_labels.reshape(-1)
    place_table = (column_order[:, None] == arrived_labels[None, :]).astype(jnp.bfloat16)
    slot_state = jnp.dot(place_table, arrived, preferred_element_type=jnp.float32).astype(
        jnp.bfloat16
    )
    span_count = span_cost.shape[0]
    levels = diff_inverse.shape[1]
    start_state = slot_state.reshape(span_count, -1, levels)

    def substep(step_index, current):
        updated = jnp.einsum(
            "crm,clm->crl", current, diff_inverse, preferred_element_type=jnp.float32
        ).astype(jnp.bfloat16)
        return jnp.where((step_index < span_cost)[:, None, None], updated, current)

    final_state = lax.fori_loop(0, jnp.max(span_cost), substep, start_state)
    tendency = (
        (final_state.astype(jnp.float32) - start_state.astype(jnp.float32))
        .astype(jnp.bfloat16)
        .reshape(column_count, features)
    )
    reply_table = (arrived_labels[:, None] == column_order[None, :]).astype(jnp.bfloat16)
    replies = jnp.dot(reply_table, tendency, preferred_element_type=jnp.float32).astype(
        jnp.bfloat16
    )
    replies = replies.reshape(device_count, capacity, features)
    returned = lax.all_to_all(replies, ("elem", "sub"), split_axis=0, concat_axis=0, tiled=True)
    returned = returned.reshape(slot_total, features)
    back_table = (dest_row[:, None] == slot_order[None, :]).astype(jnp.bfloat16)
    tend_cols = jnp.dot(back_table, returned, preferred_element_type=jnp.float32)
    tend_grid = tend_cols.reshape(point_rows // 2, point_cols // 2, features)
    spread_back = jnp.broadcast_to(
        tend_grid[:, None, :, None, :], (point_rows // 2, 2, point_cols // 2, 2, features)
    ).reshape(point_rows, point_cols, features)
    return (settled_wide + spread_back).astype(jnp.bfloat16)


def solution(mesh):
    in_specs = (
        P("elem", "sub", None),
        P("elem", "sub"),
        P("elem", "sub"),
        P("elem", "sub"),
        P("elem", "sub"),
        P(("elem", "sub")),
        P(("elem", "sub"), None, None),
        P(("elem", "sub")),
    )
    out_specs = P("elem", "sub", None)
    return jax.shard_map(
        on_device, mesh=mesh, in_specs=in_specs, out_specs=out_specs, check_vma=False
    )
```

profile of v0, /device:TPU:1, one launch (start us, length us, event | category | flops | bytes accessed | tf_op | source)
XLA Modules:
  0.0 176.8 jit_solution(15940209047656506297)
XLA Ops:
  0.0 4.8 %reshape.122 = f32[8,4,8,4,1024]{4,3,2,1,0:T(4,128)} reshape(bf16[32,32,1024]{2,1,0:T(8,128)(2,1)} %param.10) | data formatting | bytes 6291456 | tf_op jit(solution)/shard_map/reshape | solution.py:67
  4.8 11.7 %fusion.24 = (f32[8,4,8,1,1024]{4,3,2,1,0:T(1,128)S(1)}, f32[8,4,8,1,1024]{4,3,2,1,0:T(1,128)S(1)}, f32[8,4,8,1,1024]{4,3,2,1,0:T(1,128)S(1)}, f32[8,4,8,1,1024]{4,3,2,1,0:T(1,128)}) fusion(f32[8,4,8,4,1024]{4,3,2,1,0:T(4,128)} %reshape.122), kind=kLoop, calls=%fused_computation.77 | loop fusion | bytes 8388608 | tf_op jit(solution)/shard_map/slice | solution.py:52
  16.4 2.4 %fusion.25 = (f32[8,1,8,4,1024]{4,3,2,1,0:T(4,128)}, f32[8,1,8,4,1024]{4,3,2,1,0:T(4,128)}, f32[8,1,8,4,1024]{4,3,2,1,0:T(4,128)}, f32[8,1,8,4,1024]{4,3,2,1,0:T(4,128)}) fusion(f32[8,4,8,4,1024]{4,3,2,1,0:T(4,128)S(1)} %copy-done.1), kind=kLoop, calls=%fused_computation.78 | loop fusion | bytes 8388608 | tf_op jit(solution)/shard_map/slice | solution.py:52
  19.2 2.7 %multiply_add_fusion.7 = (f32[8,4,8,1,1024]{4,2,3,1,0:T(8,128)S(1)}, f32[8,4,8,1,1024]{4,2,3,1,0:T(8,128)S(1)}, f32[8,4,8,1,1024]{4,2,3,1,0:T(8,128)S(1)}, f32[8,4,8,1,1024]{4,2,3,1,0:T(8,128)S(1)}) fusion(f32[8,4,8,1,1024]{4,3,2,1,0:T(1,128)} %get-tuple-element.61, f32[8,4,8,1,1024]{4,3,2,1,0:T(1,128)S(1)} %get-tuple-element.59, ...), kind=kLoop, calls=%fused_computation.35 | loop fusion | flops 7340032 | bytes 8388608 | tf_op jit(solution)/shard_map/add | solution.py:57
  22.0 0.4 maximum_multiply_fusion.1
  22.4 1.9 %multiply_add_fusion.3 = (f32[8,4,8,1,1024]{4,2,3,1,0:T(8,128)S(1)}, f32[8,4,8,1,1024]{4,2,3,1,0:T(8,128)S(1)}, f32[8,4,8,1,1024]{4,2,3,1,0:T(8,128)S(1)}, f32[8,4,8,1,1024]{4,2,3,1,0:T(8,128)}) fusion(f32[8,4,8,4,1024]{4,2,3,1,0:T(8,128)S(1)} %maximum_multiply_fusion.1), kind=kLoop, calls=%fused_computation.31 | loop fusion | flops 7340032 | bytes 8388608 | tf_op jit(solution)/shard_map/add | solution.py:57
  24.7 6.3 %multiply_add_fusion.15 = (f32[8,1,8,4,1024]{4,2,3,1,0:T(8,128)S(1)}, f32[8,1,8,4,1024]{4,2,3,1,0:T(8,128)S(1)}, f32[8,1,8,4,1024]{4,2,3,1,0:T(8,128)S(1)}, f32[8,1,8,4,1024]{4,2,3,1,0:T(8,128)S(1)}) fusion(f32[8,1,8,4,1024]{4,3,2,1,0:T(4,128)} %get-tuple-element.71, f32[8,1,8,4,1024]{4,3,2,1,0:T(4,128)} %get-tuple-element.72, ...), kind=kLoop, calls=%fused_computation.43 | loop fusion | flops 7340032 | bytes 8388608 | tf_op jit(solution)/shard_map/add | solution.py:57
  31.0 0.6 maximum_multiply_fusion
  31.6 0.9 multiply_add_fusion.11
  32.9 1.0 fusion.8
  33.9 5.6 %copy.56 = f32[8,4,8,4,1024]{4,3,2,1,0:T(4,128)} copy(f32[8,4,8,4,1024]{4,2,3,1,0:T(8,128)S(1)} %fusion.8) | data formatting | bytes 8388608 | tf_op jit(solution)/shard_map/mul | solution.py:74
  39.4 5.5 %mul.356 = f32[32,32,1024]{2,1,0:T(8,128)} reshape(f32[8,4,8,4,1024]{4,3,2,1,0:T(4,128)} %copy.56) | data formatting | bytes 8388608 | tf_op jit(solution)/shard_map/mul | solution.py:74
  44.9 2.7 %subtract_multiply_fusion = f32[32,32,1024]{2,1,0:T(8,128)S(1)} fusion(f32[32,32,1024]{2,1,0:T(8,128)} %mul.356, f32[32,32]{1,0:T(8,128)S(1)} %copy-done.5, bf16[32,32,1024]{2,1,0:T(8,128)(2,1)S(1)} %copy-done.3), kind=kLoop, calls=%fused_computation.21 | loop fusion | flops 3145728 | bytes 10489856 | tf_op jit(solution)/shard_map/mul | solution.py:88
  47.6 3.1 %collective-permute-start = (f32[1,32,1024]{2,1,0:T(8,128)S(1)}, f32[1,32,1024]{2,1,0:T(8,128)S(1)}, u32[]{:S(2)}, u32[]{:S(2)}) collective-permute-start(f32[1,32,1024]{2,1,0:T(8,128)S(1)} %get-tuple-element.48), channel_id=1, source_target_pairs={{0,4},{4,8},{8,12},{12,16},{16,20},{20,24},{24,28},{28,32},{32,36}... | collective-permute-start | bytes 393224 | tf_op jit(solution)/shard_map/ppermute | solution.py:19
  51.2 1.4 collective-permute-done
  52.7 2.4 %collective-permute-done.1 = f32[1,32,1024]{2,1,0:T(8,128)S(1)} collective-permute-done((f32[1,32,1024]{2,1,0:T(8,128)S(1)}, f32[1,32,1024]{2,1,0:T(8,128)S(1)}, u32[]{:S(2)}, u32[]{:S(2)}) %collective-permute-start.1) | collective-permute-done | bytes 131104 | tf_op jit(solution)/shard_map/ppermute | solution.py:21
  55.4 1.3 collective-permute-start.2
  56.7 1.5 collective-permute-start.3
  58.2 0.7 all_to_all.12
  59.0 9.9 %all-to-all-start = ((s32[128,1,4]{2,1,0:T(1,128)}), s32[128,1,4]{2,1,0:T(1,128)S(1)}, u32[]{:S(2)}, u32[]{:S(2)}) async-start(s32[128,1,4]{2,1,0:T(1,128)} %bitcast.3), calls=%async_computation | async-start | bytes 131072 | tf_op jit(solution)/shard_map/all_to_all | solution.py:132
  69.6 2.8 %pad_maximum_fusion = f32[34,34,1024]{2,1,0:T(8,128)S(1)} fusion(f32[34,1,1024]{2,1,0:T(1,128)S(1)} %copy.60, f32[1,32,1024]{2,1,0:T(8,128)S(1)} %collective-permute-done.1, f32[32,32,1024]{2,1,0:T(8,128)} %copy-done, f32[1,32,1024]{2,1,0:T(8,128)S(1)} %collective-permute-done, f32[34,1,1024]{2,1,0:T(1,128)S(1)} %copy.59), kind=kLoop, calls=%fused_computation.3 | loop fusion | flops 4734976 | bytes 9469952 | tf_op jit(solution)/shard_map/concatenate | solution.py:17
  72.4 2.6 %fusion.1 = f32[32,34,1024]{2,1,0:T(8,128)S(1)} fusion(f32[34,34,1024]{2,1,0:T(8,128)S(1)} %pad_maximum_fusion, f32[32]{0:T(128)S(1)} %get-tuple-element.76, f32[32]{0:T(128)S(1)} %get-tuple-element.77), kind=kLoop, calls=%fused_computation.7 | loop fusion | flops 4456448 | bytes 17826048 | tf_op jit(solution)/shard_map/add | solution.py:92
  75.0 3.0 %convert_multiply_fusion = (f32[32,32,1024]{2,1,0:T(8,128)}, bf16[32,32,1024]{2,1,0:T(8,128)(2,1)S(1)}) fusion(f32[32,32]{1,0:T(8,128)S(1)} %copy-done.5, f32[32,34,1024]{2,1,0:T(8,128)S(1)} %fusion.1, f32[32]{0:T(128)S(1)} %get-tuple-element.76, f32[32]{0:T(128)S(1)} %get-tuple-element.77, f32[32,32]{1,0:T(8,128)S(1)} %copy-done.6), kind=kLoop, calls=%fused_computation.5 | loop fusion | flops 8388608 | bytes 18882816 | tf_op jit(solution)/shard_map/mul | solution.py:103
  78.0 5.9 %reshape.123 = f32[16,2,16,2,1024]{4,3,2,1,0:T(2,128)} reshape(f32[32,32,1024]{2,1,0:T(8,128)} %get-tuple-element.44) | data formatting | bytes 8388608 | tf_op jit(solution)/shard_map/reshape | solution.py:104
  83.8 5.4 %reduce_sum.30 = f32[16,16,1024]{2,1,0:T(8,128)S(1)} reduce(f32[16,2,16,2,1024]{4,3,2,1,0:T(2,128)} %reshape.123, f32[]{:T(128)} %constant.110.clone.1), dimensions={1,3}, to_apply=%region_1.2 | reduce | flops 786432 | bytes 5242884 | tf_op jit(solution)/shard_map/reduce_sum | solution.py:105
  89.9 1.2 reshape.125
  91.1 10.2 %all-to-all-start.1 = ((bf16[128,4,1024]{2,1,0:T(4,128)(2,1)}), bf16[128,4,1024]{2,1,0:T(4,128)(2,1)}, u32[]{:S(2)}, u32[]{:S(2)}) async-start(bf16[128,4,1024]{2,1,0:T(4,128)(2,1)} %reshape.125), calls=%async_computation.1 | async-start | bytes 2097152 | tf_op jit(solution)/shard_map/all_to_all | solution.py:131
  101.3 0.6 reduce_max.9
  102.0 0.6 broadcast.353
  102.5 0.8 reduce.3
  103.5 17.2 %all-to-all-done.1 = bf16[128,4,1024]{2,1,0:T(4,128)(2,1)} async-done(((bf16[128,4,1024]{2,1,0:T(4,128)(2,1)}), bf16[128,4,1024]{2,1,0:T(4,128)(2,1)}, u32[]{:S(2)}, u32[]{:S(2)}) %all-to-all-start.1) | async-done | bytes 1048608 | tf_op jit(solution)/shard_map/all_to_all | solution.py:131
  120.7 2.1 %reshape.126 = bf16[512,1024]{1,0:T(8,128)(2,1)} reshape(bf16[128,4,1024]{2,1,0:T(4,128)(2,1)} %all-to-all-done.1) | data formatting | bytes 2097152 | tf_op jit(solution)/shard_map/reshape | solution.py:134
  122.8 1.7 convolution_convert_fusion.3
  124.5 1.0 reshape.127
  125.5 1.0 copy.106
  126.6 1.7 while.10
  127.2 0.5 fusion.38
  128.3 1.2 subtract_convert_fusion
  129.5 1.0 reshape.128
  130.5 1.5 convolution_convert_fusion.1
  132.0 1.2 reshape.129
  133.2 6.7 %all-to-all-start.2 = ((bf16[128,4,1024]{2,1,0:T(4,128)(2,1)}), bf16[128,4,1024]{2,1,0:T(4,128)(2,1)S(1)}, u32[]{:S(2)}, u32[]{:S(2)}) async-start(bf16[128,4,1024]{2,1,0:T(4,128)(2,1)} %reshape.129), calls=%async_computation.2 | async-start | bytes 2097152 | tf_op jit(solution)/shard_map/all_to_all | solution.py:161
  140.1 19.6 %all-to-all-done.2 = bf16[128,4,1024]{2,1,0:T(4,128)(2,1)S(1)} async-done(((bf16[128,4,1024]{2,1,0:T(4,128)(2,1)}), bf16[128,4,1024]{2,1,0:T(4,128)(2,1)S(1)}, u32[]{:S(2)}, u32[]{:S(2)}) %all-to-all-start.2) | async-done | bytes 1048608 | tf_op jit(solution)/shard_map/all_to_all | solution.py:161
  159.7 1.1 reshape.134
  160.8 1.7 fusion.12
  162.5 3.9 %broadcast_in_dim.7 = f32[16,2,16,2,1024]{4,3,2,1,0:T(2,128)} broadcast(f32[16,16,1024]{2,1,0:T(8,128)S(1)} %fusion.12), dimensions={0,2,4} | broadcast | bytes 5242880 | tf_op jit(solution)/shard_map/broadcast_in_dim | solution.py:166
  166.4 6.1 %reshape.131 = f32[32,32,1024]{2,1,0:T(8,128)} reshape(f32[16,2,16,2,1024]{4,3,2,1,0:T(2,128)} %broadcast_in_dim.7) | data formatting | bytes 8388608 | tf_op jit(solution)/shard_map/reshape | solution.py:168
  172.5 4.3 %fusion.3 = bf16[32,32,1024]{2,1,0:T(8,128)(2,1)} fusion(f32[32,32,1024]{2,1,0:T(8,128)} %reshape.131, bf16[32,32,1024]{2,1,0:T(8,128)(2,1)S(1)} %get-tuple-element.45), kind=kLoop, calls=%fused_computation.10 | loop fusion | flops 3145728 | bytes 8388608 | tf_op jit(solution)/shard_map/convert_element_type | solution.py:169
  (51 shorter events, 3.3 us)
Async XLA Ops:
  4.8 11.7 %copy-start.1 = (f32[8,4,8,4,1024]{4,3,2,1,0:T(4,128)S(1)}, f32[8,4,8,4,1024]{4,3,2,1,0:T(4,128)}, u32[]{:S(2)}) copy-start(f32[8,4,8,4,1024]{4,3,2,1,0:T(4,128)} %reshape.122) | copy-start | bytes 12582916
  16.4 2.5 %copy-start.7 = (f32[32,32]{1,0:T(8,128)S(1)}, f32[32,32]{1,0:T(8,128)}, u32[]{:S(2)}) copy-start(f32[32,32]{1,0:T(8,128)} %param.12) | copy-start | bytes 12292
  22.4 2.0 %copy-start.8 = (f32[32,32]{1,0:T(8,128)S(1)}, f32[32,32]{1,0:T(8,128)}, u32[]{:S(2)}) copy-start(f32[32,32]{1,0:T(8,128)} %param.11) | copy-start | bytes 12292
  31.6 1.2 copy-start.4
  39.4 5.5 %copy-start.3 = (bf16[32,32,1024]{2,1,0:T(8,128)(2,1)S(1)}, bf16[32,32,1024]{2,1,0:T(8,128)(2,1)}, u32[]{:S(2)}) copy-start(bf16[32,32,1024]{2,1,0:T(8,128)(2,1)} %param.10) | copy-start | bytes 6291460
  39.4 5.5 %copy-start.5 = (f32[32,32]{1,0:T(8,128)S(1)}, f32[32,32]{1,0:T(8,128)}, u32[]{:S(2)}) copy-start(f32[32,32]{1,0:T(8,128)} %param.13) | copy-start | bytes 12292
  44.9 5.8 %copy-start.9 = (s32[256]{0:T(256)S(1)}, s32[256]{0:T(256)}, u32[]{:S(2)}) copy-start(s32[256]{0:T(256)} %param.15) | copy-start | bytes 3076
  47.6 7.5 %copy-start = (f32[32,32,1024]{2,1,0:T(8,128)}, f32[32,32,1024]{2,1,0:T(8,128)S(1)}, u32[]{:S(2)}) copy-start(f32[32,32,1024]{2,1,0:T(8,128)S(1)} %subtract_multiply_fusion) | copy-start | bytes 12582916
  47.6 5.0 %collective-permute-start = (f32[1,32,1024]{2,1,0:T(8,128)S(1)}, f32[1,32,1024]{2,1,0:T(8,128)S(1)}, u32[]{:S(2)}, u32[]{:S(2)}) collective-permute-start(f32[1,32,1024]{2,1,0:T(8,128)S(1)} %get-tuple-element.48), channel_id=1, source_target_pairs={{0,4},{4,8},{8,12},{12,16},{16,20},{20,24},{24,28},{28,32},{32,36}... | collective-permute-start | bytes 393224 | tf_op jit(solution)/shard_map/ppermute | solution.py:19
  50.7 4.4 %collective-permute-start.1 = (f32[1,32,1024]{2,1,0:T(8,128)S(1)}, f32[1,32,1024]{2,1,0:T(8,128)S(1)}, u32[]{:S(2)}, u32[]{:S(2)}) collective-permute-start(f32[1,32,1024]{2,1,0:T(8,128)S(1)} %get-tuple-element.49), channel_id=1, source_target_pairs={{4,0},{8,4},{12,8},{16,12},{20,16},{24,20},{28,24},{32,28},{36,32}... | collective-permute-start | bytes 393224 | tf_op jit(solution)/shard_map/ppermute | solution.py:21
  55.4 13.9 %collective-permute-start.2 = (f32[34,1,1024]{2,0,1:T(8,128)S(1)}, f32[34,1,1024]{2,0,1:T(8,128)S(1)}, u32[]{:S(2)}, u32[]{:S(2)}) collective-permute-start(f32[34,1,1024]{2,0,1:T(8,128)S(1)} %copy.57), channel_id=1, source_target_pairs={{0,1},{1,2},{2,3},{3,0},{4,5},{5,6},{6,7},{7,4},{8,9},{9,10},{10,1... | collective-permute-start | bytes 417800 | tf_op jit(solution)/shard_map/ppermute | solution.py:19
  56.7 12.7 %collective-permute-start.3 = (f32[34,1,1024]{2,0,1:T(8,128)S(1)}, f32[34,1,1024]{2,0,1:T(8,128)S(1)}, u32[]{:S(2)}, u32[]{:S(2)}) collective-permute-start(f32[34,1,1024]{2,0,1:T(8,128)S(1)} %copy.58), channel_id=1, source_target_pairs={{1,0},{2,1},{3,2},{0,3},{5,4},{6,5},{7,6},{4,7},{9,8},{10,9},{11,1... | collective-permute-start | bytes 417800 | tf_op jit(solution)/shard_map/ppermute | solution.py:21
  59.0 32.1 %all-to-all-start = ((s32[128,1,4]{2,1,0:T(1,128)}), s32[128,1,4]{2,1,0:T(1,128)S(1)}, u32[]{:S(2)}, u32[]{:S(2)}) async-start(s32[128,1,4]{2,1,0:T(1,128)} %bitcast.3), calls=%async_computation | async-start | bytes 131072 | tf_op jit(solution)/shard_map/all_to_all | solution.py:132
  72.4 2.6 %copy-start.6 = (f32[32,32]{1,0:T(8,128)S(1)}, f32[32,32]{1,0:T(8,128)}, u32[]{:S(2)}) copy-start(f32[32,32]{1,0:T(8,128)} %param.14) | copy-start | bytes 12292
  89.3 12.1 %copy-start.10 = (s32[16]{0:T(128)S(1)}, s32[16]{0:T(128)}, u32[]{:S(2)}) copy-start(s32[16]{0:T(128)} %param.17) | copy-start | bytes 196
  91.1 35.5 %copy-start.2 = (bf16[16,128,128]{2,1,0:T(8,128)(2,1)S(1)}, bf16[16,128,128]{2,1,0:T(8,128)(2,1)}, u32[]{:S(2)}) copy-start(bf16[16,128,128]{2,1,0:T(8,128)(2,1)} %param.16) | copy-start | bytes 1572868
  91.1 29.6 %all-to-all-start.1 = ((bf16[128,4,1024]{2,1,0:T(4,128)(2,1)}), bf16[128,4,1024]{2,1,0:T(4,128)(2,1)}, u32[]{:S(2)}, u32[]{:S(2)}) async-start(bf16[128,4,1024]{2,1,0:T(4,128)(2,1)} %reshape.125), calls=%async_computation.1 | async-start | bytes 2097152 | tf_op jit(solution)/shard_map/all_to_all | solution.py:131
  133.2 26.5 %all-to-all-start.2 = ((bf16[128,4,1024]{2,1,0:T(4,128)(2,1)}), bf16[128,4,1024]{2,1,0:T(4,128)(2,1)S(1)}, u32[]{:S(2)}, u32[]{:S(2)}) async-start(bf16[128,4,1024]{2,1,0:T(4,128)(2,1)} %reshape.129), calls=%async_computation.2 | async-start | bytes 2097152 | tf_op jit(solution)/shard_map/all_to_all | solution.py:161
where the time goes:
time: 178 us; the launch traced here: 177 us
  local copies, waits for them, and re-layouts  57.6 us (32%)
  waiting for transfers between devices  40.7 us (23%)
  other arithmetic  38 us (21%)
  starting transfers between devices  32.8 us (18%)
  matrix products  6.15 us (3%)
    all_to_all x1, waiting for transfers between devices, on_device(): lax.all_to_all(replies, ('elem', 'sub'), split_axis=0, concat_axis=0, til...  19.6 us
    all_to_all x1, waiting for transfers between devices, on_device(): lax.all_to_all(outgoing, ('elem', 'sub'), split_axis=0, concat_axis=0, ti...  17.2 us
    slice x2, local copies, waits for them, and re-layouts, node_mix(): lax.index_in_dim(blocks, node, axis, keepdims=True)  14.1 us
    add x4, other arithmetic, node_mix(): total = total + float(matrix[row_node, col_node]) * pieces[col_node]  11.9 us
    mul x2, local copies, waits for them, and re-layouts, local_section(): section_field = blocks - diffusion_nu * (weak_x + weak_y)  11 us
    all_to_all x1, starting transfers between devices, on_device(): lax.all_to_all(outgoing, ('elem', 'sub'), split_axis=0, concat_axis=0, ti...  10.2 us
    all_to_all x1, starting transfers between devices, on_device(): lax.all_to_all(labels, ('elem', 'sub'), split_axis=0, concat_axis=0, tile...  9.93 us
    all_to_all x1, starting transfers between devices, on_device(): lax.all_to_all(replies, ('elem', 'sub'), split_axis=0, concat_axis=0, til...  6.74 us
  transfers between devices with their start and end apart: 7, of which 4 were waited for; matrix products, arithmetic and copies ran while one was open for 14% of the time, Pallas kernels for 0%

commit v1 on v0

v1 whole, which is shorter than its diff:
```python
import math

import jax
import jax.numpy as jnp
import numpy as np
from jax import lax
from jax.experimental import pallas as pl
from jax.experimental.pallas import tpu as pltpu
from jax.sharding import PartitionSpec as P

diffusion_nu = 0.01
LANES = 128


def gll_matrix():
    gll_nodes = np.array([-1.0, -1.0 / math.sqrt(5.0), 1.0 / math.sqrt(5.0), 1.0])
    result = np.zeros((4, 4))
    for row_node in range(4):
        for col_node in range(4):
            if row_node == col_node:
                total = 0.0
                for other_node in range(4):
                    if other_node != row_node:
                        total += 1.0 / (gll_nodes[row_node] - gll_nodes[other_node])
                result[row_node, col_node] = total
            else:
                product_top = 1.0
                product_low = 1.0
                for other_node in range(4):
                    if other_node != col_node:
                        product_low *= gll_nodes[col_node] - gll_nodes[other_node]
                        if other_node != row_node:
                            product_top *= gll_nodes[row_node] - gll_nodes[other_node]
                result[row_node, col_node] = product_top / product_low
    return result


DERIV = [[float(np.float32(v)) for v in row] for row in gll_matrix()]


def mix(coefs, terms):
    total = coefs[0] * terms[0]
    for c, t in zip(coefs[1:], terms[1:]):
        total = total + c * t
    return total


def section_kernel(q_ref, coef_ref, w_ref, rt_ref, rb_ref, cl_ref, cr_ref, s_ref):
    s_ref[...] = q_ref[...].astype(jnp.float32)
    d = DERIV

    def body(a, carry):
        q = [[s_ref[4 * a + i, pl.ds(j, 8, stride=4), :] for j in range(4)] for i in range(4)]
        mx = [[coef_ref[0, i, j, a] for j in range(4)] for i in range(4)]
        my = [[coef_ref[1, i, j, a] for j in range(4)] for i in range(4)]
        mw = [[coef_ref[2, i, j, a] for j in range(4)] for i in range(4)]
        tx = [
            [mx[k][j] * mix(d[k], [q[m][j] for m in range(4)]) for j in range(4)]
            for k in range(4)
        ]
        ty = [
            [my[i][k] * mix(d[k], [q[i][m] for m in range(4)]) for k in range(4)]
            for i in range(4)
        ]
        for i in range(4):
            for j in range(4):
                wx = mix([d[k][i] for k in range(4)], [tx[k][j] for k in range(4)])
                wy = mix([d[k][j] for k in range(4)], [ty[i][k] for k in range(4)])
                w_ref[i, j, a] = mw[i][j] * (q[i][j] - diffusion_nu * (wx + wy))
        return carry

    lax.fori_loop(0, 8, body, 0)
    for j in range(4):
        rt_ref[j] = w_ref[0, j, 0]
        rb_ref[j] = w_ref[3, j, 7]
    for i in range(4):
        for a in range(8):
            cl_ref[i, pl.ds(a, 1), :] = w_ref[i, 0, a, pl.ds(0, 1), :]
            cr_ref[i, pl.ds(a, 1), :] = w_ref[i, 3, a, pl.ds(7, 1), :]


def settle_kernel(
    w_ref, top_ref, bot_ref, lax_ref, rax_ref, coef_ref, den_ref, st_ref, col_ref, ss_ref
):
    sub = lax.broadcasted_iota(jnp.int32, (8, LANES), 0)

    def body(a, carry):
        x = [[w_ref[i, j, a] for j in range(4)] for i in range(4)]
        up = [
            jnp.where(a == 0, top_ref[j], w_ref[3, j, jnp.maximum(a - 1, 0)]) for j in range(4)
        ]
        dn = [
            jnp.where(a == 7, bot_ref[j], w_ref[0, j, jnp.minimum(a + 1, 7)]) for j in range(4)
        ]
        ax = [
            [x[0][j] + up[j] for j in range(4)],
            x[1],
            x[2],
            [x[3][j] + dn[j] for j in range(4)],
        ]
        settled = [[None] * 4 for _ in range(4)]
        for i in range(4):
            left = lax_ref[i, pl.ds(a, 1), :]
            right = rax_ref[i, pl.ds(a, 1), :]
            prev3 = jnp.where(sub == 0, left, pltpu.roll(ax[i][3], 1, 0))
            next0 = jnp.where(sub == 7, right, pltpu.roll(ax[i][0], 7, 0))
            summed = [ax[i][0] + prev3, ax[i][1], ax[i][2], ax[i][3] + next0]
            for j in range(4):
                value = (coef_ref[1, i, j, a] * summed[j]).astype(jnp.bfloat16)
                settled[i][j] = value.astype(jnp.float32)
                ss_ref[4 * a + i, pl.ds(j, 8, stride=4), :] = settled[i][j]
        for p in range(2):
            for q in range(2):
                num = None
                for i in (2 * p, 2 * p + 1):
                    for j in (2 * q, 2 * q + 1):
                        term = coef_ref[0, i, j, a] * settled[i][j]
                        num = term if num is None else num + term
                col_ref[a, p, q] = num / den_ref[p, q, a]
        return carry

    lax.fori_loop(0, 8, body, 0)
    st_ref[...] = ss_ref[...].astype(st_ref.dtype)


def finish_kernel(st_ref, tend_ref, out_ref, t2_ref):
    def body(r2, carry):
        t = tend_ref[pl.ds(pl.multiple_of(r2 * 16, 16), 16), :]
        t2_ref[pl.ds(0, 16, stride=2), :] = t
        t2_ref[pl.ds(1, 16, stride=2), :] = t
        spread = t2_ref[...]
        for half in range(2):
            row = 2 * r2 + half
            out_ref[row] = (st_ref[row].astype(jnp.float32) + spread).astype(out_ref.dtype)
        return carry

    lax.fori_loop(0, 16, body, 0)


def spec(shape, lane_axis=None):
    nd = len(shape)

    def index(h):
        return tuple(h if d == lane_axis else 0 for d in range(nd))

    return pl.BlockSpec(shape, index)


def run_section(tracers, coef):
    rows, cols, features = tracers.shape
    nb = features // LANES
    return pl.pallas_call(
        section_kernel,
        grid=(nb,),
        in_specs=[
            spec((rows, cols, LANES), 2),
            pl.BlockSpec((3, 4, 4, 8, 8, LANES), lambda h: (0, 0, 0, 0, 0, 0)),
        ],
        out_specs=[
            spec((4, 4, 8, 8, LANES), 4),
            spec((4, 8, LANES), 2),
            spec((4, 8, LANES), 2),
            spec((4, 8, LANES), 2),
            spec((4, 8, LANES), 2),
        ],
        out_shape=[
            jax.ShapeDtypeStruct((4, 4, 8, 8, features), jnp.float32),
            jax.ShapeDtypeStruct((4, 8, features), jnp.float32),
            jax.ShapeDtypeStruct((4, 8, features), jnp.float32),
            jax.ShapeDtypeStruct((4, 8, features), jnp.float32),
            jax.ShapeDtypeStruct((4, 8, features), jnp.float32),
        ],
        scratch_shapes=[pltpu.VMEM((rows, cols, LANES), jnp.float32)],
    )(tracers, coef)


def run_settle(w, top, bot, lax_halo, rax_halo, coef, den):
    features = w.shape[-1]
    nb = features // LANES
    return pl.pallas_call(
        settle_kernel,
        grid=(nb,),
        in_specs=[
            spec((4, 4, 8, 8, LANES), 4),
            spec((4, 8, LANES), 2),
            spec((4, 8, LANES), 2),
            spec((4, 8, LANES), 2),
            spec((4, 8, LANES), 2),
            pl.BlockSpec((2, 4, 4, 8, 8, LANES), lambda h: (1, 0, 0, 0, 0, 0)),
            spec((2, 2, 8, 8, LANES)),
        ],
        out_specs=[
            spec((32, 32, LANES), 2),
            spec((8, 2, 2, 8, LANES), 4),
        ],
        out_shape=[
            jax.ShapeDtypeStruct((32, 32, features), jnp.bfloat16),
            jax.ShapeDtypeStruct((8, 2, 2, 8, features), jnp.float32),
        ],
        scratch_shapes=[pltpu.VMEM((32, 32, LANES), jnp.float32)],
    )(w, top, bot, lax_halo, rax_halo, coef, den)


def run_finish(settled, tend):
    rows, cols, features = settled.shape
    nb = features // LANES
    return pl.pallas_call(
        finish_kernel,
        grid=(nb,),
        in_specs=[spec((rows, cols, LANES), 2), spec((tend.shape[0], LANES), 1)],
        out_specs=spec((rows, cols, LANES), 2),
        out_shape=jax.ShapeDtypeStruct(settled.shape, jnp.bfloat16),
        scratch_shapes=[pltpu.VMEM((cols, LANES), jnp.float32)],
    )(settled, tend)


def deinterleave(field):
    return field.reshape(8, 4, 8, 4).transpose(1, 3, 0, 2)


def shift(x, axis, step):
    count = lax.axis_size(axis)
    return lax.ppermute(x, axis, [(k, (k + step) % count) for k in range(count)])


def shift2(x, step_e, step_s):
    ne = lax.axis_size("elem")
    ns = lax.axis_size("sub")
    pairs = []
    for e in range(ne):
        for s in range(ns):
            pairs.append((e * ns + s, ((e + step_e) % ne) * ns + (s + step_s) % ns))
    return lax.ppermute(x, ("elem", "sub"), pairs)


def on_device(
    tracers, metric_x, metric_y, mass_weight, mass_inverse, phys_slot, diff_inverse, span_cost
):
    point_rows, point_cols, features = tracers.shape
    coef = jnp.broadcast_to(
        jnp.stack(
            [deinterleave(metric_x), deinterleave(metric_y), deinterleave(mass_weight),
             deinterleave(mass_inverse)]
        )[..., None],
        (4, 4, 4, 8, 8, LANES),
    )
    den = mass_weight.reshape(8, 2, 2, 8, 2, 2).sum(axis=(2, 5)).transpose(1, 3, 0, 2)
    den = jnp.broadcast_to(den[..., None], (2, 2, 8, 8, LANES))

    w, rt, rb, cl, cr = run_section(tracers, coef)
    top = shift(rb, "elem", 1)
    bot = shift(rt, "elem", -1)
    left = shift(cr, "sub", 1)
    right = shift(cl, "sub", -1)
    corner_tl = shift2(rb[3, 7], 1, 1)
    corner_tr = shift2(rb[0, 0], 1, -1)
    corner_bl = shift2(rt[3, 7], -1, 1)
    corner_br = shift2(rt[0, 0], -1, -1)

    def along_x(side, above, below):
        first = side[0] + jnp.concatenate([above[None], side[3, :-1]], axis=0)
        last = side[3] + jnp.concatenate([side[0, 1:], below[None]], axis=0)
        return jnp.stack([first, side[1], side[2], last])

    lax_halo = along_x(left, corner_tl, corner_bl)
    rax_halo = along_x(right, corner_tr, corner_br)
    settled, columns = run_settle(w, top, bot, lax_halo, rax_halo, coef, den)
    columns = columns.reshape(-1, features).astype(jnp.bfloat16)

    column_count = columns.shape[0]
    slot_k = phys_slot.reshape(8, 2, 8, 2).transpose(0, 1, 3, 2).reshape(-1)
    device_count = lax.axis_size(("elem", "sub"))
    capacity = max(1, 2 * column_count // device_count)
    slot_total = device_count * capacity
    target = slot_k // column_count
    landing = slot_k % column_count
    column_order = jnp.arange(column_count)
    earlier = (target[None, :] == target[:, None]) & (column_order[None, :] < column_order[:, None])
    position = jnp.sum(earlier.astype(jnp.int32), axis=1)
    dest_row = target * capacity + position
    slot_order = jnp.arange(slot_total)
    send_table = (slot_order[:, None] == dest_row[None, :]).astype(jnp.bfloat16)
    outgoing = jnp.dot(send_table, columns, preferred_element_type=jnp.float32).astype(jnp.bfloat16)
    label_values = jnp.dot(
        send_table.astype(jnp.float32),
        (landing + 1).astype(jnp.float32),
        precision=lax.Precision.HIGHEST,
    )
    labels = label_values.astype(jnp.int32) - 1
    outgoing = outgoing.reshape(device_count, capacity, features)
    labels = labels.reshape(device_count, capacity)
    arrived, arrived_labels = (
        lax.all_to_all(outgoing, ("elem", "sub"), split_axis=0, concat_axis=0, tiled=True),
        lax.all_to_all(labels, ("elem", "sub"), split_axis=0, concat_axis=0, tiled=True),
    )
    arrived = arrived.reshape(-1, features)
    arrived_labels = arrived_labels.reshape(-1)
    place_table = (column_order[:, None] == arrived_labels[None, :]).astype(jnp.bfloat16)
    slot_state = jnp.dot(place_table, arrived, preferred_element_type=jnp.float32).astype(
        jnp.bfloat16
    )
    span_count = span_cost.shape[0]
    levels = diff_inverse.shape[1]
    start_state = slot_state.reshape(span_count, -1, levels)

    def substep(step_index, current):
        updated = jnp.einsum(
            "crm,clm->crl", current, diff_inverse, preferred_element_type=jnp.float32
        ).astype(jnp.bfloat16)
        return jnp.where((step_index < span_cost)[:, None, None], updated, current)

    final_state = lax.fori_loop(0, jnp.max(span_cost), substep, start_state)
    tendency = (
        (final_state.astype(jnp.float32) - start_state.astype(jnp.float32))
        .astype(jnp.bfloat16)
        .reshape(column_count, features)
    )
    reply_table = (arrived_labels[:, None] == column_order[None, :]).astype(jnp.bfloat16)
    replies = jnp.dot(reply_table, tendency, preferred_element_type=jnp.float32).astype(
        jnp.bfloat16
    )
    replies = replies.reshape(device_count, capacity, features)
    returned = lax.all_to_all(replies, ("elem", "sub"), split_axis=0, concat_axis=0, tiled=True)
    returned = returned.reshape(slot_total, features)
    dest_nat = dest_row.reshape(8, 2, 2, 8).transpose(0, 1, 3, 2).reshape(-1)
    back_table = (dest_nat[:, None] == slot_order[None, :]).astype(jnp.bfloat16)
    tend_cols = jnp.dot(back_table, returned, preferred_element_type=jnp.float32)
    return run_finish(settled, tend_cols)


def solution(mesh):
    in_specs = (
        P("elem", "sub", None),
        P("elem", "sub"),
        P("elem", "sub"),
        P("elem", "sub"),
        P("elem", "sub"),
        P(("elem", "sub")),
        P(("elem", "sub"), None, None),
        P(("elem", "sub")),
    )
    out_specs = P("elem", "sub", None)
    return jax.shard_map(
        on_device, mesh=mesh, in_specs=in_specs, out_specs=out_specs, check_vma=False
    )
```

time: 178 us -> 136 us (0.76)
  local copies, waits for them, and re-layouts: 57.6 us -> 14.5 us
  other arithmetic: 38 us -> 4.74 us
  Pallas kernels: 0 us -> 24 us
  waiting for transfers between devices: 40.7 us -> 48 us
  starting transfers between devices: 32.8 us -> 37 us
  matrix products: 6.15 us -> 4.13 us
    pallas_call x0 -> x3, Pallas kernels: none -> 24 us  [the longest x1 9.5 us: run_section(): pl.pallas_call(section_kernel, grid=(nb,), in_specs=[spec((rows, cols, LA...]
    add x5 -> x2, other arithmetic: 14.5 us -> 0.04 us  [along_x(): first = side[0] + jnp.concatenate([above[None], side[3, :-1]], axis=0)]
    slice x5, local copies, waits for them, and re-layouts: 14.2 us -> 0.85 us  [the longest x1 0.82 us: on_device(): corner_tr = shift2(rb[0, 0], 1, -1)]
    reshape x4 -> x8, local copies, waits for them, and re-layouts: 16.9 us -> 4.06 us  [the longest x4 3.23 us: deinterleave(): return field.reshape(8, 4, 8, 4).transpose(1, 3, 0, 2)]
    mul x6 -> x0, local copies, waits for them, and re-layouts: 11.7 us -> none  [the longest x2 11 us: local_section(): section_field = blocks - diffusion_nu * (weak_x + weak_y)]
    ppermute x4 -> x8, starting transfers between devices: 5.9 us -> 15.2 us  [the longest x4 10.1 us: shift2(): return lax.ppermute(x, ('elem', 'sub'), pairs)]
    mul x5 -> x0, other arithmetic: 7.66 us -> none  [the longest x1 2.95 us: on_device(): mass_weight[:, :, None] * settled_wide]
    ppermute x4 -> x8, waiting for transfers between devices: 3.86 us -> 11.2 us  [the longest x4 6.97 us: shift2(): return lax.ppermute(x, ('elem', 'sub'), pairs)]
  transfers between devices with their start and end apart: 7 -> 11, of which waited for: 4 -> 5; matrix products, arithmetic and copies ran while one was open for 14% -> 8% of each run, Pallas kernels for 0% -> 6%
where the time goes in v1:
time: 136 us; the launch traced here: 134 us
  waiting for transfers between devices  48 us (35%)
  starting transfers between devices  37 us (27%)
  Pallas kernels  24 us (18%)
  local copies, waits for them, and re-layouts  14.5 us (11%)
  other arithmetic  4.74 us (3%)
  matrix products  4.13 us (3%)
  loops' own time  1.71 us (1%)
    all_to_all x1, waiting for transfers between devices, on_device(): lax.all_to_all(replies, ('elem', 'sub'), split_axis=0, concat_axis=0, til...  19.1 us
    all_to_all x1, waiting for transfers between devices, on_device(): lax.all_to_all(outgoing, ('elem', 'sub'), split_axis=0, concat_axis=0, ti...  17.7 us
    ppermute x4, starting transfers between devices, shift2(): return lax.ppermute(x, ('elem', 'sub'), pairs)  10.1 us
    pallas_call x1, Pallas kernels, run_section(): pl.pallas_call(section_kernel, grid=(nb,), in_specs=[spec((rows, cols, LA...  9.5 us
    all_to_all x1, starting transfers between devices, on_device(): lax.all_to_all(labels, ('elem', 'sub'), split_axis=0, concat_axis=0, tile...  8.66 us
    pallas_call x1, Pallas kernels, run_settle(): pl.pallas_call(settle_kernel, grid=(nb,), in_specs=[spec((4, 4, 8, 8, LAN...  8.11 us
    all_to_all x1, starting transfers between devices, on_device(): lax.all_to_all(outgoing, ('elem', 'sub'), split_axis=0, concat_axis=0, ti...  8.01 us
    ppermute x4, waiting for transfers between devices, shift2(): return lax.ppermute(x, ('elem', 'sub'), pairs)  6.97 us
  transfers between devices with their start and end apart: 11, of which 5 were waited for; matrix products, arithmetic and copies ran while one was open for 8% of the time, Pallas kernels for 6%

profile of v1, /device:TPU:1, one launch (start us, length us, event | category | flops | bytes accessed | tf_op | source)
XLA Modules:
  0.0 134.3 jit_solution(12652677198255988312)
XLA Ops:
  0.0 0.8 reshape.142
  0.8 0.8 reshape.143
  1.6 0.8 reshape.144
  2.4 0.8 reshape.145
  3.3 0.8 copy.26
  4.1 2.0 %broadcast_in_dim.9.coef_ref = f32[4,4,4,8,8,128]{5,4,3,2,1,0:T(8,128)} broadcast(f32[4,4,4,8,8]{4,3,2,1,0:T(8,128)S(1)} %copy.26), dimensions={0,1,2,3,4} | broadcast | bytes 2113536 | tf_op jit(solution)/shard_map/broadcast_in_dim | solution.py:240
  6.1 9.5 %shard_map.82 = (f32[4,4,8,8,1024]{4,3,2,1,0:T(8,128)}, f32[4,8,1024]{2,1,0:T(8,128)}, f32[4,8,1024]{2,1,0:T(8,128)}, f32[4,8,1024]{2,1,0:T(8,128)}, f32[4,8,1024]{2,1,0:T(8,128)}) custom-call(bf16[32,32,1024]{2,1,0:T(8,128)(2,1)} %q_ref.1, f32[4,4,4,8,8,128]{5,4,3,2,1,0:T(8,128)} %broadcast_in_dim.9.coef_ref), custom_call_target="tpu_custom_call" | custom-call | tf_op jit(solution)/shard_map/pallas_call | solution.py:152
  15.6 3.1 %collective-permute-start = (f32[4,8,1024]{2,1,0:T(8,128)}, f32[4,8,1024]{2,1,0:T(8,128)S(1)}, u32[]{:S(2)}, u32[]{:S(2)}) collective-permute-start(f32[4,8,1024]{2,1,0:T(8,128)} %get-tuple-element.41), channel_id=1, source_target_pairs={{0,4},{4,8},{8,12},{12,16},{16,20},{20,24},{24,28},{28,32},{32,36}... | collective-permute-start | bytes 393224 | tf_op jit(solution)/shard_map/ppermute | solution.py:223
  18.7 0.8 fusion.17
  19.5 4.0 %collective-permute-start.6 = (f32[1024]{0:T(1024)S(1)}, f32[1024]{0:T(1024)S(1)}, u32[]{:S(2)}, u32[]{:S(2)}) collective-permute-start(f32[1024]{0:T(1024)S(1)} %bitcast.71), channel_id=1, source_target_pairs={{0,7},{1,4},{2,5},{3,6},{4,11},{5,8},{6,9},{7,10},{8,15},{9,12},{1... | collective-permute-start | bytes 12296 | tf_op jit(solution)/shard_map/ppermute | solution.py:233
  23.5 3.0 %collective-permute-start.7 = (f32[1024]{0:T(1024)S(1)}, f32[1024]{0:T(1024)S(1)}, u32[]{:S(2)}, u32[]{:S(2)}) collective-permute-start(f32[1024]{0:T(1024)S(1)} %bitcast.70), channel_id=1, source_target_pairs={{0,127},{1,124},{2,125},{3,126},{4,3},{5,0},{6,1},{7,2},{8,7},{9,4... | collective-permute-start | bytes 12296 | tf_op jit(solution)/shard_map/ppermute | solution.py:233
  26.5 0.5 collective-permute-start.5
  27.7 0.3 fusion.1
  28.1 0.8 all_to_all.12
  28.8 8.7 %all-to-all-start = ((s32[128,1,4]{2,1,0:T(1,128)}), s32[128,1,4]{2,1,0:T(1,128)S(1)}, u32[]{:S(2)}, u32[]{:S(2)}) async-start(s32[128,1,4]{2,1,0:T(1,128)} %bitcast.22), calls=%async_computation | async-start | bytes 131072 | tf_op jit(solution)/shard_map/all_to_all | solution.py:294
  37.5 0.4 reshape.146
  38.3 1.4 %collective-permute-start.2 = (f32[4,8,1024]{2,1,0:T(8,128)}, f32[4,8,1024]{2,1,0:T(8,128)S(1)}, u32[]{:S(2)}, u32[]{:S(2)}) collective-permute-start(f32[4,8,1024]{2,1,0:T(8,128)} %get-tuple-element.43), channel_id=1, source_target_pairs={{0,1},{1,2},{2,3},{3,0},{4,5},{5,6},{6,7},{7,4},{8,9},{9,10},{10,1... | collective-permute-start | bytes 393224 | tf_op jit(solution)/shard_map/ppermute | solution.py:223
  39.7 4.2 %collective-permute-done.2 = f32[4,8,1024]{2,1,0:T(8,128)S(1)} collective-permute-done((f32[4,8,1024]{2,1,0:T(8,128)}, f32[4,8,1024]{2,1,0:T(8,128)S(1)}, u32[]{:S(2)}, u32[]{:S(2)}) %collective-permute-start.2) | collective-permute-done | bytes 131104 | tf_op jit(solution)/shard_map/ppermute | solution.py:223
  43.9 1.8 %collective-permute-start.4 = (f32[1024]{0:T(1024)S(1)}, f32[1024]{0:T(1024)S(1)}, u32[]{:S(2)}, u32[]{:S(2)}) collective-permute-start(f32[1024]{0:T(1024)S(1)} %bitcast.69), channel_id=1, source_target_pairs={{0,125},{1,126},{2,127},{3,124},{4,1},{5,2},{6,3},{7,0},{8,5},{9,6... | collective-permute-start | bytes 12296 | tf_op jit(solution)/shard_map/ppermute | solution.py:233
  45.7 1.3 collective-permute-start.3
  47.1 2.2 %collective-permute-done.4 = f32[1024]{0:T(1024)S(1)} collective-permute-done((f32[1024]{0:T(1024)S(1)}, f32[1024]{0:T(1024)S(1)}, u32[]{:S(2)}, u32[]{:S(2)}) %collective-permute-start.4) | collective-permute-done | bytes 4128 | tf_op jit(solution)/shard_map/ppermute | solution.py:233
  49.3 4.7 %collective-permute-done.3 = f32[1024]{0:T(1024)S(1)} collective-permute-done((f32[1024]{0:T(1024)S(1)}, f32[1024]{0:T(1024)S(1)}, u32[]{:S(2)}, u32[]{:S(2)}) %collective-permute-start.3) | collective-permute-done | bytes 4128 | tf_op jit(solution)/shard_map/ppermute | solution.py:233
  54.1 0.7 pad_maximum_fusion.2.rax_ref
  54.7 0.7 pad_maximum_fusion.1.lax_ref
  55.4 0.7 broadcast_in_dim.10.den_ref
  56.2 8.1 %shard_map.83 = (bf16[32,32,1024]{2,1,0:T(8,128)(2,1)}, f32[8,2,2,8,1024]{4,3,2,1,0:T(8,128)}) custom-call(f32[4,4,8,8,1024]{4,3,2,1,0:T(8,128)} %get-tuple-element.40.w_ref, f32[4,8,1024]{2,1,0:T(8,128)} %copy-done.1, f32[4,8,1024]{2,1,0:T(8,128)} %copy-done.2, f32[4,8,1024]{2,1,0:T(8,128)} %pad_maximum_fusion.1.lax_ref, ...), custom_call_target="tpu_custom_call" | custom-call | tf_op jit(solution)/shard_map/pallas_call | solution.py:180
  64.3 1.3 convert_element_type.44
  65.6 0.4 convolution_convert_fusion.2
  66.0 1.2 reshape.149
  67.3 8.0 %all-to-all-start.1 = ((bf16[128,4,1024]{2,1,0:T(4,128)(2,1)}), bf16[128,4,1024]{2,1,0:T(4,128)(2,1)S(1)}, u32[]{:S(2)}, u32[]{:S(2)}) async-start(bf16[128,4,1024]{2,1,0:T(4,128)(2,1)} %reshape.149), calls=%async_computation.1 | async-start | bytes 2097152 | tf_op jit(solution)/shard_map/all_to_all | solution.py:293
  75.3 0.6 reduce_max.9
  75.9 0.6 broadcast.140
  76.5 0.8 reduce.3
  77.4 17.7 %all-to-all-done.1 = bf16[128,4,1024]{2,1,0:T(4,128)(2,1)S(1)} async-done(((bf16[128,4,1024]{2,1,0:T(4,128)(2,1)}), bf16[128,4,1024]{2,1,0:T(4,128)(2,1)S(1)}, u32[]{:S(2)}, u32[]{:S(2)}) %all-to-all-start.1) | async-done | bytes 1048608 | tf_op jit(solution)/shard_map/all_to_all | solution.py:293
  95.1 0.3 reshape.150
  95.4 0.4 convolution_convert_fusion.3
  95.9 0.2 reshape.151
  96.2 0.3 copy-done
  96.5 2.8 %while.10 = (s32[]{:T(128)}, bf16[16,128,128]{2,1,0:T(8,128)(2,1)S(1)}, s32[]{:T(128)}, s32[16]{0:T(128)S(1)}, bf16[16,128,128]{2,1,0:T(8,128)(2,1)S(1)}, /*index=5*/s32[]{:T(128)}) while((s32[]{:T(128)}, bf16[16,128,128]{2,1,0:T(8,128)(2,1)S(1)}, s32[]{:T(128)}, s32[16]{0:T(128)S(1)}, bf16[16,128,128]{2,1,0:T(8,128)(2,1)S(1)}, ...), condition=%wide.region_4.5_spmd, body=%wide.region_3.4_spmd.sunk | while | flops 67633168 | bytes 2621609 | solution.py:312
  97.1 0.5 fusion.33
  98.2 0.5 fusion.33
  99.6 0.5 convolution_convert_fusion.1
  100.1 1.2 reshape.153
  101.3 5.1 %all-to-all-start.2 = ((bf16[128,4,1024]{2,1,0:T(4,128)(2,1)}), bf16[128,4,1024]{2,1,0:T(4,128)(2,1)S(1)}, u32[]{:S(2)}, u32[]{:S(2)}) async-start(bf16[128,4,1024]{2,1,0:T(4,128)(2,1)} %reshape.153), calls=%async_computation.2 | async-start | bytes 2097152 | tf_op jit(solution)/shard_map/all_to_all | solution.py:323
  107.0 19.1 %all-to-all-done.2 = bf16[128,4,1024]{2,1,0:T(4,128)(2,1)S(1)} async-done(((bf16[128,4,1024]{2,1,0:T(4,128)(2,1)}), bf16[128,4,1024]{2,1,0:T(4,128)(2,1)S(1)}, u32[]{:S(2)}, u32[]{:S(2)}) %all-to-all-start.2) | async-done | bytes 1048608 | tf_op jit(solution)/shard_map/all_to_all | solution.py:323
  126.2 0.3 reshape.154
  126.4 1.5 %fusion.2.tend_ref = f32[256,1024]{1,0:T(8,128)} fusion(bf16[512,1024]{1,0:T(8,128)(2,1)S(1)} %reshape.154, s32[256]{0:T(256)S(1)} %eq.74), kind=kOutput, calls=%fused_computation.13 | convolution fusion | flops 268566528 | bytes 2098176 | tf_op jit(solution)/shard_map/dot_general | solution.py:327
  127.9 6.4 %shard_map.84 = bf16[32,32,1024]{2,1,0:T(8,128)(2,1)} custom-call(bf16[32,32,1024]{2,1,0:T(8,128)(2,1)} %get-tuple-element.45.st_ref, f32[256,1024]{1,0:T(8,128)} %fusion.2.tend_ref), custom_call_target="tpu_custom_call" | custom-call | tf_op jit(solution)/shard_map/pallas_call | solution.py:207
  (47 shorter events, 2.3 us)
Async XLA Ops:
  6.1 21.0 %copy-start.4 = (s32[256]{0:T(256)S(1)}, s32[256]{0:T(256)}, u32[]{:S(2)}) copy-start(s32[256]{0:T(256)} %param.15) | copy-start | bytes 3076
  6.1 31.4 %copy-start.3 = (f32[32,32]{1,0:T(8,128)S(1)}, f32[32,32]{1,0:T(8,128)}, u32[]{:S(2)}) copy-start(f32[32,32]{1,0:T(8,128)} %param.13) | copy-start | bytes 12292
  15.6 39.8 %collective-permute-start = (f32[4,8,1024]{2,1,0:T(8,128)}, f32[4,8,1024]{2,1,0:T(8,128)S(1)}, u32[]{:S(2)}, u32[]{:S(2)}) collective-permute-start(f32[4,8,1024]{2,1,0:T(8,128)} %get-tuple-element.41), channel_id=1, source_target_pairs={{0,4},{4,8},{8,12},{12,16},{16,20},{20,24},{24,28},{28,32},{32,36}... | collective-permute-start | bytes 393224 | tf_op jit(solution)/shard_map/ppermute | solution.py:223
  18.7 36.7 %collective-permute-start.1 = (f32[4,8,1024]{2,1,0:T(8,128)}, f32[4,8,1024]{2,1,0:T(8,128)S(1)}, u32[]{:S(2)}, u32[]{:S(2)}) collective-permute-start(f32[4,8,1024]{2,1,0:T(8,128)} %get-tuple-element.42), channel_id=1, source_target_pairs={{0,124},{4,0},{8,4},{12,8},{16,12},{20,16},{24,20},{28,24},{32,28}... | collective-permute-start | bytes 393224 | tf_op jit(solution)/shard_map/ppermute | solution.py:223
  19.5 26.2 %collective-permute-start.6 = (f32[1024]{0:T(1024)S(1)}, f32[1024]{0:T(1024)S(1)}, u32[]{:S(2)}, u32[]{:S(2)}) collective-permute-start(f32[1024]{0:T(1024)S(1)} %bitcast.71), channel_id=1, source_target_pairs={{0,7},{1,4},{2,5},{3,6},{4,11},{5,8},{6,9},{7,10},{8,15},{9,12},{1... | collective-permute-start | bytes 12296 | tf_op jit(solution)/shard_map/ppermute | solution.py:233
  23.5 23.5 %collective-permute-start.7 = (f32[1024]{0:T(1024)S(1)}, f32[1024]{0:T(1024)S(1)}, u32[]{:S(2)}, u32[]{:S(2)}) collective-permute-start(f32[1024]{0:T(1024)S(1)} %bitcast.70), channel_id=1, source_target_pairs={{0,127},{1,124},{2,125},{3,126},{4,3},{5,0},{6,1},{7,2},{8,7},{9,4... | collective-permute-start | bytes 12296 | tf_op jit(solution)/shard_map/ppermute | solution.py:233
  26.5 11.8 %collective-permute-start.5 = (f32[4,8,1024]{2,1,0:T(8,128)}, f32[4,8,1024]{2,1,0:T(8,128)S(1)}, u32[]{:S(2)}, u32[]{:S(2)}) collective-permute-start(f32[4,8,1024]{2,1,0:T(8,128)} %get-tuple-element.44), channel_id=1, source_target_pairs={{0,3},{1,0},{2,1},{3,2},{4,7},{5,4},{6,5},{7,6},{8,11},{9,8},{10,9... | collective-permute-start | bytes 393224 | tf_op jit(solution)/shard_map/ppermute | solution.py:223
  28.8 38.4 %all-to-all-start = ((s32[128,1,4]{2,1,0:T(1,128)}), s32[128,1,4]{2,1,0:T(1,128)S(1)}, u32[]{:S(2)}, u32[]{:S(2)}) async-start(s32[128,1,4]{2,1,0:T(1,128)} %bitcast.22), calls=%async_computation | async-start | bytes 131072 | tf_op jit(solution)/shard_map/all_to_all | solution.py:294
  38.3 5.6 %collective-permute-start.2 = (f32[4,8,1024]{2,1,0:T(8,128)}, f32[4,8,1024]{2,1,0:T(8,128)S(1)}, u32[]{:S(2)}, u32[]{:S(2)}) collective-permute-start(f32[4,8,1024]{2,1,0:T(8,128)} %get-tuple-element.43), channel_id=1, source_target_pairs={{0,1},{1,2},{2,3},{3,0},{4,5},{5,6},{6,7},{7,4},{8,9},{9,10},{10,1... | collective-permute-start | bytes 393224 | tf_op jit(solution)/shard_map/ppermute | solution.py:223
  43.9 5.4 %collective-permute-start.4 = (f32[1024]{0:T(1024)S(1)}, f32[1024]{0:T(1024)S(1)}, u32[]{:S(2)}, u32[]{:S(2)}) collective-permute-start(f32[1024]{0:T(1024)S(1)} %bitcast.69), channel_id=1, source_target_pairs={{0,125},{1,126},{2,127},{3,124},{4,1},{5,2},{6,3},{7,0},{8,5},{9,6... | collective-permute-start | bytes 12296 | tf_op jit(solution)/shard_map/ppermute | solution.py:233
  45.7 8.3 %collective-permute-start.3 = (f32[1024]{0:T(1024)S(1)}, f32[1024]{0:T(1024)S(1)}, u32[]{:S(2)}, u32[]{:S(2)}) collective-permute-start(f32[1024]{0:T(1024)S(1)} %bitcast.68), channel_id=1, source_target_pairs={{0,5},{1,6},{2,7},{3,4},{4,9},{5,10},{6,11},{7,8},{8,13},{9,14},{1... | collective-permute-start | bytes 12296 | tf_op jit(solution)/shard_map/ppermute | solution.py:233
  55.4 0.8 copy-start.1
  55.4 0.8 copy-start.2
  66.0 9.3 %copy-start.5 = (s32[16]{0:T(128)S(1)}, s32[16]{0:T(128)}, u32[]{:S(2)}) copy-start(s32[16]{0:T(128)} %param.17) | copy-start | bytes 196
  67.3 27.9 %all-to-all-start.1 = ((bf16[128,4,1024]{2,1,0:T(4,128)(2,1)}), bf16[128,4,1024]{2,1,0:T(4,128)(2,1)S(1)}, u32[]{:S(2)}, u32[]{:S(2)}) async-start(bf16[128,4,1024]{2,1,0:T(4,128)(2,1)} %reshape.149), calls=%async_computation.1 | async-start | bytes 2097152 | tf_op jit(solution)/shard_map/all_to_all | solution.py:293
  95.4 1.0 copy-start
  101.3 24.9 %all-to-all-start.2 = ((bf16[128,4,1024]{2,1,0:T(4,128)(2,1)}), bf16[128,4,1024]{2,1,0:T(4,128)(2,1)S(1)}, u32[]{:S(2)}, u32[]{:S(2)}) async-start(bf16[128,4,1024]{2,1,0:T(4,128)(2,1)} %reshape.153), calls=%async_computation.2 | async-start | bytes 2097152 | tf_op jit(solution)/shard_map/all_to_all | solution.py:323

commit v2 on v1

--- a/solution.py
+++ b/solution.py
@@ -124,14 +124,20 @@
 
 
 def finish_kernel(st_ref, tend_ref, out_ref, t2_ref):
+    chunks = tend_ref.shape[1] // LANES
+
     def body(r2, carry):
-        t = tend_ref[pl.ds(pl.multiple_of(r2 * 16, 16), 16), :]
-        t2_ref[pl.ds(0, 16, stride=2), :] = t
-        t2_ref[pl.ds(1, 16, stride=2), :] = t
-        spread = t2_ref[...]
-        for half in range(2):
-            row = 2 * r2 + half
-            out_ref[row] = (st_ref[row].astype(jnp.float32) + spread).astype(out_ref.dtype)
+        for h in range(chunks):
+            lanes = pl.ds(h * LANES, LANES)
+            t = tend_ref[pl.ds(pl.multiple_of(r2 * 16, 16), 16), lanes]
+            t2_ref[h, pl.ds(0, 16, stride=2), :] = t
+            t2_ref[h, pl.ds(1, 16, stride=2), :] = t
+            spread = t2_ref[h]
+            for half in range(2):
+                row = 2 * r2 + half
+                out_ref[row, :, lanes] = (
+                    st_ref[row, :, lanes].astype(jnp.float32) + spread
+                ).astype(out_ref.dtype)
         return carry
 
     lax.fori_loop(0, 16, body, 0)
@@ -203,14 +209,15 @@
 
 def run_finish(settled, tend):
     rows, cols, features = settled.shape
-    nb = features // LANES
+    width = 4 * LANES
+    nb = features // width
     return pl.pallas_call(
         finish_kernel,
         grid=(nb,),
-        in_specs=[spec((rows, cols, LANES), 2), spec((tend.shape[0], LANES), 1)],
-        out_specs=spec((rows, cols, LANES), 2),
+        in_specs=[spec((rows, cols, width), 2), spec((tend.shape[0], width), 1)],
+        out_specs=spec((rows, cols, width), 2),
         out_shape=jax.ShapeDtypeStruct(settled.shape, jnp.bfloat16),
-        scratch_shapes=[pltpu.VMEM((cols, LANES), jnp.float32)],
+        scratch_shapes=[pltpu.VMEM((width // LANES, cols, LANES), jnp.float32)],
     )(settled, tend)
 
 
@@ -221,16 +228,6 @@
 def shift(x, axis, step):
     count = lax.axis_size(axis)
     return lax.ppermute(x, axis, [(k, (k + step) % count) for k in range(count)])
-
-
-def shift2(x, step_e, step_s):
-    ne = lax.axis_size("elem")
-    ns = lax.axis_size("sub")
-    pairs = []
-    for e in range(ne):
-        for s in range(ns):
-            pairs.append((e * ns + s, ((e + step_e) % ne) * ns + (s + step_s) % ns))
-    return lax.ppermute(x, ("elem", "sub"), pairs)
 
 
 def on_device(
@@ -250,20 +247,14 @@
     w, rt, rb, cl, cr = run_section(tracers, coef)
     top = shift(rb, "elem", 1)
     bot = shift(rt, "elem", -1)
-    left = shift(cr, "sub", 1)
-    right = shift(cl, "sub", -1)
-    corner_tl = shift2(rb[3, 7], 1, 1)
-    corner_tr = shift2(rb[0, 0], 1, -1)
-    corner_bl = shift2(rt[3, 7], -1, 1)
-    corner_br = shift2(rt[0, 0], -1, -1)
 
     def along_x(side, above, below):
         first = side[0] + jnp.concatenate([above[None], side[3, :-1]], axis=0)
         last = side[3] + jnp.concatenate([side[0, 1:], below[None]], axis=0)
         return jnp.stack([first, side[1], side[2], last])
 
-    lax_halo = along_x(left, corner_tl, corner_bl)
-    rax_halo = along_x(right, corner_tr, corner_br)
+    lax_halo = shift(along_x(cr, top[3, 7], bot[3, 7]), "sub", 1)
+    rax_halo = shift(along_x(cl, top[0, 0], bot[0, 0]), "sub", -1)
     settled, columns = run_settle(w, top, bot, lax_halo, rax_halo, coef, den)
     columns = columns.reshape(-1, features).astype(jnp.bfloat16)
 
@@ -280,21 +271,16 @@
     dest_row = target * capacity + position
     slot_order = jnp.arange(slot_total)
     send_table = (slot_order[:, None] == dest_row[None, :]).astype(jnp.bfloat16)
-    outgoing = jnp.dot(send_table, columns, preferred_element_type=jnp.float32).astype(jnp.bfloat16)
-    label_values = jnp.dot(
-        send_table.astype(jnp.float32),
-        (landing + 1).astype(jnp.float32),
-        precision=lax.Precision.HIGHEST,
-    )
-    labels = label_values.astype(jnp.int32) - 1
-    outgoing = outgoing.reshape(device_count, capacity, features)
-    labels = labels.reshape(device_count, capacity)
-    arrived, arrived_labels = (
-        lax.all_to_all(outgoing, ("elem", "sub"), split_axis=0, concat_axis=0, tiled=True),
-        lax.all_to_all(labels, ("elem", "sub"), split_axis=0, concat_axis=0, tiled=True),
-    )
-    arrived = arrived.reshape(-1, features)
-    arrived_labels = arrived_labels.reshape(-1)
+    label_block = jnp.where(
+        jnp.arange(LANES)[None, :] == 0, (landing + 1)[:, None].astype(jnp.bfloat16), 0
+    ).astype(jnp.bfloat16)
+    payload = jnp.concatenate([columns, label_block], axis=1)
+    outgoing = jnp.dot(send_table, payload, preferred_element_type=jnp.float32).astype(jnp.bfloat16)
+    outgoing = outgoing.reshape(device_count, capacity, features + LANES)
+    arrived = lax.all_to_all(outgoing, ("elem", "sub"), split_axis=0, concat_axis=0, tiled=True)
+    arrived = arrived.reshape(-1, features + LANES)
+    arrived_labels = arrived[:, features].astype(jnp.int32) - 1
+    arrived = arrived[:, :features]
     place_table = (column_order[:, None] == arrived_labels[None, :]).astype(jnp.bfloat16)
     slot_state = jnp.dot(place_table, arrived, preferred_element_type=jnp.float32).astype(
         jnp.bfloat16

time: 136 us -> 114 us (0.84)
  starting transfers between devices: 37 us -> 23.2 us
  waiting for transfers between devices: 48 us -> 44.7 us
  Pallas kernels: 24 us -> 20.8 us
  other arithmetic: 4.74 us -> 2.93 us
    ppermute x4 -> x0, starting transfers between devices: 10.1 us -> none  [shift2(): return lax.ppermute(x, ('elem', 'sub'), pairs)]
    all_to_all x1 -> x0, starting transfers between devices: 8.66 us -> none  [on_device(): lax.all_to_all(labels, ('elem', 'sub'), split_axis=0, concat_axis=0, tile...]
    ppermute x4 -> x0, waiting for transfers between devices: 6.97 us -> none  [shift2(): return lax.ppermute(x, ('elem', 'sub'), pairs)]
    pallas_call x1, Pallas kernels: 6.42 us -> 3.14 us  [run_finish(): pl.pallas_call(finish_kernel, grid=(nb,), in_specs=[spec((rows, cols, wid...]
    all_to_all x1, waiting for transfers between devices: 17.7 us -> 20.4 us  [on_device(): lax.all_to_all(outgoing, ('elem', 'sub'), split_axis=0, concat_axis=0, ti...]
    all_to_all x1, starting transfers between devices: 8.01 us -> 10.4 us  [on_device(): lax.all_to_all(outgoing, ('elem', 'sub'), split_axis=0, concat_axis=0, ti...]
    all_to_all x1, starting transfers between devices: 5.13 us -> 7.1 us  [on_device(): lax.all_to_all(replies, ('elem', 'sub'), split_axis=0, concat_axis=0, til...]
    slice x2, local copies, waits for them, and re-layouts: 0.01 us -> 1.69 us  [along_x(): return jnp.stack([first, side[1], side[2], last])]
  transfers between devices with their start and end apart: 11 -> 6, of which waited for: 5 -> 4; matrix products, arithmetic and copies ran while one was open for 8% -> 5% of each run, Pallas kernels for 6% -> 0%
where the time goes in v2:
time: 114 us; the launch traced here: 112 us
  waiting for transfers between devices  44.7 us (39%)
  starting transfers between devices  23.2 us (20%)
  Pallas kernels  20.8 us (18%)
  local copies, waits for them, and re-layouts  15.8 us (14%)
  matrix products  3.4 us (3%)
  other arithmetic  2.93 us (3%)
  loops' own time  1.28 us (1%)
    all_to_all x1, waiting for transfers between devices, on_device(): lax.all_to_all(outgoing, ('elem', 'sub'), split_axis=0, concat_axis=0, ti...  20.4 us
    all_to_all x1, waiting for transfers between devices, on_device(): lax.all_to_all(replies, ('elem', 'sub'), split_axis=0, concat_axis=0, til...  19.3 us
    all_to_all x1, starting transfers between devices, on_device(): lax.all_to_all(outgoing, ('elem', 'sub'), split_axis=0, concat_axis=0, ti...  10.4 us
    pallas_call x1, Pallas kernels, run_section(): pl.pallas_call(section_kernel, grid=(nb,), in_specs=[spec((rows, cols, LA...  9.5 us
    pallas_call x1, Pallas kernels, run_settle(): pl.pallas_call(settle_kernel, grid=(nb,), in_specs=[spec((4, 4, 8, 8, LAN...  8.12 us
    all_to_all x1, starting transfers between devices, on_device(): lax.all_to_all(replies, ('elem', 'sub'), split_axis=0, concat_axis=0, til...  7.1 us
    ppermute x4, starting transfers between devices, shift(): lax.ppermute(x, axis, [(k, (k + step) % count) for k in range(count)])  5.71 us
    ppermute x4, waiting for transfers between devices, shift(): lax.ppermute(x, axis, [(k, (k + step) % count) for k in range(count)])  5.01 us
  transfers between devices with their start and end apart: 6, of which 4 were waited for; matrix products, arithmetic and copies ran while one was open for 5% of the time, Pallas kernels for 0%

profile of v2, /device:TPU:1, one launch (start us, length us, event | category | flops | bytes accessed | tf_op | source)
XLA Modules:
  0.0 112.4 jit_solution(7735673088921834490)
XLA Ops:
  0.0 0.8 reshape.172
  0.8 0.8 reshape.173
  1.6 0.8 reshape.174
  2.4 0.8 reshape.175
  3.3 0.8 copy.28
  4.1 2.0 %broadcast_in_dim.22.coef_ref = f32[4,4,4,8,8,128]{5,4,3,2,1,0:T(8,128)} broadcast(f32[4,4,4,8,8]{4,3,2,1,0:T(8,128)S(1)} %copy.28), dimensions={0,1,2,3,4} | broadcast | bytes 2113536 | tf_op jit(solution)/shard_map/broadcast_in_dim | solution.py:237
  6.1 9.5 %shard_map.82 = (f32[4,4,8,8,1024]{4,3,2,1,0:T(8,128)}, f32[4,8,1024]{2,1,0:T(8,128)}, f32[4,8,1024]{2,1,0:T(8,128)}, f32[4,8,1024]{2,1,0:T(8,128)}, f32[4,8,1024]{2,1,0:T(8,128)}) custom-call(bf16[32,32,1024]{2,1,0:T(8,128)(2,1)} %q_ref.1, f32[4,4,4,8,8,128]{5,4,3,2,1,0:T(8,128)} %broadcast_in_dim.22.coef_ref), custom_call_target="tpu_custom_call" | custom-call | tf_op jit(solution)/shard_map/pallas_call | solution.py:158
  15.6 3.1 %collective-permute-start = (f32[4,8,1024]{2,1,0:T(8,128)}, f32[4,8,1024]{2,1,0:T(8,128)S(1)}, u32[]{:S(2)}, u32[]{:S(2)}) collective-permute-start(f32[4,8,1024]{2,1,0:T(8,128)} %get-tuple-element.41), channel_id=1, source_target_pairs={{0,4},{4,8},{8,12},{12,16},{16,20},{20,24},{24,28},{28,32},{32,36}... | collective-permute-start | bytes 393224 | tf_op jit(solution)/shard_map/ppermute | solution.py:230
  18.7 0.8 fusion.21
  19.5 0.8 fusion.23
  20.3 0.1 reshape.177
  20.4 0.2 copy.31
  20.8 0.8 slice.62
  21.7 0.8 slice.55
  22.5 0.4 reshape.176
  23.0 0.2 reduce_sum.20
  23.2 0.2 copy.29
  23.3 0.2 convert_reduce_fusion
  23.7 2.5 %collective-permute-start.3 = (f32[4,8,1024]{2,1,0:T(8,128)S(1)}, f32[4,8,1024]{2,1,0:T(8,128)S(1)}, u32[]{:S(2)}, u32[]{:S(2)}) collective-permute-start(f32[4,8,1024]{2,1,0:T(8,128)S(1)} %pad_maximum_fusion.2), channel_id=1, source_target_pairs={{0,3},{1,0},{2,1},{3,2},{4,7},{5,4},{6,5},{7,6},{8,11},{9,8},{10,9... | collective-permute-start | bytes 393224 | tf_op jit(solution)/shard_map/ppermute | solution.py:230
  26.3 1.8 %collective-permute-done.3.rax_ref = f32[4,8,1024]{2,1,0:T(8,128)S(1)} collective-permute-done((f32[4,8,1024]{2,1,0:T(8,128)S(1)}, f32[4,8,1024]{2,1,0:T(8,128)S(1)}, u32[]{:S(2)}, u32[]{:S(2)}) %collective-permute-start.3) | collective-permute-done | bytes 131104 | tf_op jit(solution)/shard_map/ppermute | solution.py:230
  28.2 3.2 %collective-permute-done.2.lax_ref = f32[4,8,1024]{2,1,0:T(8,128)S(1)} collective-permute-done((f32[4,8,1024]{2,1,0:T(8,128)S(1)}, f32[4,8,1024]{2,1,0:T(8,128)S(1)}, u32[]{:S(2)}, u32[]{:S(2)}) %collective-permute-start.2) | collective-permute-done | bytes 131104 | tf_op jit(solution)/shard_map/ppermute | solution.py:230
  31.3 0.7 broadcast_in_dim.30.den_ref
  32.1 8.1 %shard_map.83 = (bf16[32,32,1024]{2,1,0:T(8,128)(2,1)}, f32[8,2,2,8,1024]{4,3,2,1,0:T(8,128)}) custom-call(f32[4,4,8,8,1024]{4,3,2,1,0:T(8,128)} %get-tuple-element.40.w_ref, f32[4,8,1024]{2,1,0:T(8,128)} %copy-done.3, f32[4,8,1024]{2,1,0:T(8,128)} %copy-done.4, f32[4,8,1024]{2,1,0:T(8,128)} %copy-done.6, f32[4,8,1024]{2,1,0:T(8,128)} %copy-done.5, ...), custom_call_target="tpu_custom_call" | custom-call | tf_op jit(solution)/shard_map/pallas_call | solution.py:186
  40.2 1.3 %convert_element_type.54 = bf16[8,2,2,8,1024]{4,3,2,1,0:T(8,128)(2,1)S(1)} convert(f32[8,2,2,8,1024]{4,3,2,1,0:T(8,128)} %get-tuple-element.46) | non-fusion elementwise | flops 262144 | bytes 1572864 | tf_op jit(solution)/shard_map/convert_element_type | solution.py:259
  41.5 0.5 convolution_convert_fusion.1
  42.0 1.2 %reshape.179 = bf16[128,4,1152]{2,1,0:T(4,128)(2,1)} reshape(bf16[512,1152]{1,0:T(8,128)(2,1)S(1)} %convolution_convert_fusion.1) | data formatting | bytes 2359296 | tf_op jit(solution)/shard_map/reshape | solution.py:279
  43.2 10.4 %all-to-all-start = ((bf16[128,4,1152]{2,1,0:T(4,128)(2,1)}), bf16[128,4,1152]{2,1,0:T(4,128)(2,1)S(1)}, u32[]{:S(2)}, u32[]{:S(2)}) async-start(bf16[128,4,1152]{2,1,0:T(4,128)(2,1)} %reshape.179), calls=%async_computation | async-start | bytes 2359296 | tf_op jit(solution)/shard_map/all_to_all | solution.py:280
  53.6 0.7 reduce_max.9
  54.3 20.4 %all-to-all-done = bf16[128,4,1152]{2,1,0:T(4,128)(2,1)S(1)} async-done(((bf16[128,4,1152]{2,1,0:T(4,128)(2,1)}), bf16[128,4,1152]{2,1,0:T(4,128)(2,1)S(1)}, u32[]{:S(2)}, u32[]{:S(2)}) %all-to-all-start) | async-done | bytes 1179680 | tf_op jit(solution)/shard_map/all_to_all | solution.py:280
  74.7 0.3 reshape.180
  75.0 0.1 add_reduce_fusion
  75.2 0.5 convolution_convert_fusion.3
  75.7 0.2 reshape.181
  75.9 0.8 copy-done
  76.7 1.8 %while.10 = (s32[]{:T(128)}, bf16[16,128,128]{2,1,0:T(8,128)(2,1)S(1)}, s32[]{:T(128)}, s32[16]{0:T(128)S(1)}, bf16[16,128,128]{2,1,0:T(8,128)(2,1)S(1)}, /*index=5*/s32[]{:T(128)}) while((s32[]{:T(128)}, bf16[16,128,128]{2,1,0:T(8,128)(2,1)S(1)}, s32[]{:T(128)}, s32[16]{0:T(128)S(1)}, bf16[16,128,128]{2,1,0:T(8,128)(2,1)S(1)}, ...), condition=%wide.region_4.5_spmd, body=%wide.region_3.4_spmd.sunk | while | flops 67633168 | bytes 2621609 | solution.py:298
  77.4 0.5 fusion.33
  78.5 0.1 subtract_convert_fusion
  78.7 0.2 reshape.182
  78.9 0.5 convolution_convert_fusion.2
  79.4 1.2 %reshape.183 = bf16[128,4,1024]{2,1,0:T(4,128)(2,1)} reshape(bf16[512,1024]{1,0:T(8,128)(2,1)S(1)} %convolution_convert_fusion.2) | data formatting | bytes 2097152 | tf_op jit(solution)/shard_map/reshape | solution.py:308
  80.6 7.1 %all-to-all-start.1 = ((bf16[128,4,1024]{2,1,0:T(4,128)(2,1)}), bf16[128,4,1024]{2,1,0:T(4,128)(2,1)S(1)}, u32[]{:S(2)}, u32[]{:S(2)}) async-start(bf16[128,4,1024]{2,1,0:T(4,128)(2,1)} %reshape.183), calls=%async_computation.1 | async-start | bytes 2097152 | tf_op jit(solution)/shard_map/all_to_all | solution.py:309
  87.8 0.2 copy.30
  88.0 0.2 copy.33
  88.2 0.1 eq.85
  88.3 19.3 %all-to-all-done.1 = bf16[128,4,1024]{2,1,0:T(4,128)(2,1)S(1)} async-done(((bf16[128,4,1024]{2,1,0:T(4,128)(2,1)}), bf16[128,4,1024]{2,1,0:T(4,128)(2,1)S(1)}, u32[]{:S(2)}, u32[]{:S(2)}) %all-to-all-start.1) | async-done | bytes 1048608 | tf_op jit(solution)/shard_map/all_to_all | solution.py:309
  107.6 0.3 reshape.184
  107.8 1.5 %fusion.5.tend_ref = f32[256,1024]{1,0:T(8,128)} fusion(bf16[512,1024]{1,0:T(8,128)(2,1)S(1)} %reshape.184, s32[256]{0:T(256)S(1)} %eq.85), kind=kOutput, calls=%fused_computation.16 | convolution fusion | flops 268566528 | bytes 2098176 | tf_op jit(solution)/shard_map/dot_general | solution.py:313
  109.3 3.1 %shard_map.84 = bf16[32,32,1024]{2,1,0:T(8,128)(2,1)} custom-call(bf16[32,32,1024]{2,1,0:T(8,128)(2,1)} %get-tuple-element.45.st_ref, f32[256,1024]{1,0:T(8,128)} %fusion.5.tend_ref), custom_call_target="tpu_custom_call" | custom-call | tf_op jit(solution)/shard_map/pallas_call | solution.py:214
  (39 shorter events, 0.7 us)
Async XLA Ops:
  6.1 14.2 %copy-start.8 = (s32[256]{0:T(256)S(1)}, s32[256]{0:T(256)}, u32[]{:S(2)}) copy-start(s32[256]{0:T(256)} %param.15) | copy-start | bytes 3076
  6.1 16.4 %copy-start.7 = (f32[32,32]{1,0:T(8,128)S(1)}, f32[32,32]{1,0:T(8,128)}, u32[]{:S(2)}) copy-start(f32[32,32]{1,0:T(8,128)} %param.13) | copy-start | bytes 12292
  15.6 8.0 %copy-start.1 = (f32[4,8,1024]{2,1,0:T(8,128)S(1)}, f32[4,8,1024]{2,1,0:T(8,128)}, u32[]{:S(2)}) copy-start(f32[4,8,1024]{2,1,0:T(8,128)} %get-tuple-element.44) | copy-start | bytes 393220
  15.6 8.0 %copy-start.2 = (f32[4,8,1024]{2,1,0:T(8,128)S(1)}, f32[4,8,1024]{2,1,0:T(8,128)}, u32[]{:S(2)}) copy-start(f32[4,8,1024]{2,1,0:T(8,128)} %get-tuple-element.43) | copy-start | bytes 393220
  15.6 7.9 %collective-permute-start = (f32[4,8,1024]{2,1,0:T(8,128)}, f32[4,8,1024]{2,1,0:T(8,128)S(1)}, u32[]{:S(2)}, u32[]{:S(2)}) collective-permute-start(f32[4,8,1024]{2,1,0:T(8,128)} %get-tuple-element.41), channel_id=1, source_target_pairs={{0,4},{4,8},{8,12},{12,16},{16,20},{20,24},{24,28},{28,32},{32,36}... | collective-permute-start | bytes 393224 | tf_op jit(solution)/shard_map/ppermute | solution.py:230
  18.7 4.8 %collective-permute-start.1 = (f32[4,8,1024]{2,1,0:T(8,128)}, f32[4,8,1024]{2,1,0:T(8,128)S(1)}, u32[]{:S(2)}, u32[]{:S(2)}) collective-permute-start(f32[4,8,1024]{2,1,0:T(8,128)} %get-tuple-element.42), channel_id=1, source_target_pairs={{0,124},{4,0},{8,4},{12,8},{16,12},{20,16},{24,20},{28,24},{32,28}... | collective-permute-start | bytes 393224 | tf_op jit(solution)/shard_map/ppermute | solution.py:230
  23.5 8.6 %copy-start.3 = (f32[4,8,1024]{2,1,0:T(8,128)}, f32[4,8,1024]{2,1,0:T(8,128)S(1)}, u32[]{:S(2)}) copy-start(f32[4,8,1024]{2,1,0:T(8,128)S(1)} %collective-permute-done.top_ref) | copy-start | bytes 393220
  23.6 8.5 %copy-start.4 = (f32[4,8,1024]{2,1,0:T(8,128)}, f32[4,8,1024]{2,1,0:T(8,128)S(1)}, u32[]{:S(2)}) copy-start(f32[4,8,1024]{2,1,0:T(8,128)S(1)} %collective-permute-done.1.bot_ref) | copy-start | bytes 393220
  23.7 4.5 %collective-permute-start.3 = (f32[4,8,1024]{2,1,0:T(8,128)S(1)}, f32[4,8,1024]{2,1,0:T(8,128)S(1)}, u32[]{:S(2)}, u32[]{:S(2)}) collective-permute-start(f32[4,8,1024]{2,1,0:T(8,128)S(1)} %pad_maximum_fusion.2), channel_id=1, source_target_pairs={{0,3},{1,0},{2,1},{3,2},{4,7},{5,4},{6,5},{7,6},{8,11},{9,8},{10,9... | collective-permute-start | bytes 393224 | tf_op jit(solution)/shard_map/ppermute | solution.py:230
  26.2 5.1 %collective-permute-start.2 = (f32[4,8,1024]{2,1,0:T(8,128)S(1)}, f32[4,8,1024]{2,1,0:T(8,128)S(1)}, u32[]{:S(2)}, u32[]{:S(2)}) collective-permute-start(f32[4,8,1024]{2,1,0:T(8,128)S(1)} %pad_maximum_fusion.1), channel_id=1, source_target_pairs={{0,1},{1,2},{2,3},{3,0},{4,5},{5,6},{6,7},{7,4},{8,9},{9,10},{10,1... | collective-permute-start | bytes 393224 | tf_op jit(solution)/shard_map/ppermute | solution.py:230
  28.2 3.9 %copy-start.5 = (f32[4,8,1024]{2,1,0:T(8,128)}, f32[4,8,1024]{2,1,0:T(8,128)S(1)}, u32[]{:S(2)}) copy-start(f32[4,8,1024]{2,1,0:T(8,128)S(1)} %collective-permute-done.3.rax_ref) | copy-start | bytes 393220
  31.3 0.8 copy-start.6
  43.2 10.4 %copy-start.9 = (s32[16]{0:T(128)S(1)}, s32[16]{0:T(128)}, u32[]{:S(2)}) copy-start(s32[16]{0:T(128)} %param.17) | copy-start | bytes 196
  43.2 31.5 %all-to-all-start = ((bf16[128,4,1152]{2,1,0:T(4,128)(2,1)}), bf16[128,4,1152]{2,1,0:T(4,128)(2,1)S(1)}, u32[]{:S(2)}, u32[]{:S(2)}) async-start(bf16[128,4,1152]{2,1,0:T(4,128)(2,1)} %reshape.179), calls=%async_computation | async-start | bytes 2359296 | tf_op jit(solution)/shard_map/all_to_all | solution.py:280
  75.6 1.0 copy-start
  80.6 27.0 %all-to-all-start.1 = ((bf16[128,4,1024]{2,1,0:T(4,128)(2,1)}), bf16[128,4,1024]{2,1,0:T(4,128)(2,1)S(1)}, u32[]{:S(2)}, u32[]{:S(2)}) async-start(bf16[128,4,1024]{2,1,0:T(4,128)(2,1)} %reshape.183), calls=%async_computation.1 | async-start | bytes 2097152 | tf_op jit(solution)/shard_map/all_to_all | solution.py:309

commit v3 on v2

--- a/solution.py
+++ b/solution.py
@@ -51,9 +51,11 @@
 
     def body(a, carry):
         q = [[s_ref[4 * a + i, pl.ds(j, 8, stride=4), :] for j in range(4)] for i in range(4)]
-        mx = [[coef_ref[0, i, j, a] for j in range(4)] for i in range(4)]
-        my = [[coef_ref[1, i, j, a] for j in range(4)] for i in range(4)]
-        mw = [[coef_ref[2, i, j, a] for j in range(4)] for i in range(4)]
+        mx, my, mw = (
+            [[coef_ref[kind, 4 * a + i, pl.ds(j, 8, stride=4), :] for j in range(4)]
+             for i in range(4)]
+            for kind in range(3)
+        )
         tx = [
             [mx[k][j] * mix(d[k], [q[m][j] for m in range(4)]) for j in range(4)]
             for k in range(4)
@@ -79,13 +81,13 @@
             cr_ref[i, pl.ds(a, 1), :] = w_ref[i, 3, a, pl.ds(7, 1), :]
 
 
-def settle_kernel(
-    w_ref, top_ref, bot_ref, lax_ref, rax_ref, coef_ref, den_ref, st_ref, col_ref, ss_ref
-):
+def settle_kernel(w_ref, top_ref, bot_ref, lax_ref, rax_ref, coef_ref, st_ref, col_ref, ss_ref):
     sub = lax.broadcasted_iota(jnp.int32, (8, LANES), 0)
 
     def body(a, carry):
         x = [[w_ref[i, j, a] for j in range(4)] for i in range(4)]
+        mw = [[coef_ref[0, 4 * a + i, pl.ds(j, 8, stride=4), :] for j in range(4)] for i in range(4)]
+        mi = [[coef_ref[1, 4 * a + i, pl.ds(j, 8, stride=4), :] for j in range(4)] for i in range(4)]
         up = [
             jnp.where(a == 0, top_ref[j], w_ref[3, j, jnp.maximum(a - 1, 0)]) for j in range(4)
         ]
@@ -106,17 +108,22 @@
             next0 = jnp.where(sub == 7, right, pltpu.roll(ax[i][0], 7, 0))
             summed = [ax[i][0] + prev3, ax[i][1], ax[i][2], ax[i][3] + next0]
             for j in range(4):
-                value = (coef_ref[1, i, j, a] * summed[j]).astype(jnp.bfloat16)
+                value = (mi[i][j] * summed[j]).astype(jnp.bfloat16)
                 settled[i][j] = value.astype(jnp.float32)
                 ss_ref[4 * a + i, pl.ds(j, 8, stride=4), :] = settled[i][j]
         for p in range(2):
+            pair = []
             for q in range(2):
                 num = None
+                den = None
                 for i in (2 * p, 2 * p + 1):
                     for j in (2 * q, 2 * q + 1):
-                        term = coef_ref[0, i, j, a] * settled[i][j]
+                        term = mw[i][j] * settled[i][j]
                         num = term if num is None else num + term
-                col_ref[a, p, q] = num / den_ref[p, q, a]
+                        den = mw[i][j] if den is None else den + mw[i][j]
+                pair.append(num / den)
+            row = pl.multiple_of((a * 2 + p) * 16, 16)
+            col_ref[pl.ds(row, 16), :] = jnp.concatenate(pair, axis=0).astype(col_ref.dtype)
         return carry
 
     lax.fori_loop(0, 8, body, 0)
@@ -160,7 +167,7 @@
         grid=(nb,),
         in_specs=[
             spec((rows, cols, LANES), 2),
-            pl.BlockSpec((3, 4, 4, 8, 8, LANES), lambda h: (0, 0, 0, 0, 0, 0)),
+            pl.BlockSpec((3, rows, cols, LANES), lambda h: (0, 0, 0, 0)),
         ],
         out_specs=[
             spec((4, 4, 8, 8, LANES), 4),
@@ -180,7 +187,7 @@
     )(tracers, coef)
 
 
-def run_settle(w, top, bot, lax_halo, rax_halo, coef, den):
+def run_settle(w, top, bot, lax_halo, rax_halo, coef):
     features = w.shape[-1]
     nb = features // LANES
     return pl.pallas_call(
@@ -192,19 +199,18 @@
             spec((4, 8, LANES), 2),
             spec((4, 8, LANES), 2),
             spec((4, 8, LANES), 2),
-            pl.BlockSpec((2, 4, 4, 8, 8, LANES), lambda h: (1, 0, 0, 0, 0, 0)),
-            spec((2, 2, 8, 8, LANES)),
+            pl.BlockSpec((2, 32, 32, LANES), lambda h: (1, 0, 0, 0)),
         ],
         out_specs=[
             spec((32, 32, LANES), 2),
-            spec((8, 2, 2, 8, LANES), 4),
+            spec((256, LANES), 1),
         ],
         out_shape=[
             jax.ShapeDtypeStruct((32, 32, features), jnp.bfloat16),
-            jax.ShapeDtypeStruct((8, 2, 2, 8, features), jnp.float32),
+            jax.ShapeDtypeStruct((256, features), jnp.bfloat16),
         ],
         scratch_shapes=[pltpu.VMEM((32, 32, LANES), jnp.float32)],
-    )(w, top, bot, lax_halo, rax_halo, coef, den)
+    )(w, top, bot, lax_halo, rax_halo, coef)
 
 
 def run_finish(settled, tend):
@@ -221,10 +227,6 @@
     )(settled, tend)
 
 
-def deinterleave(field):
-    return field.reshape(8, 4, 8, 4).transpose(1, 3, 0, 2)
-
-
 def shift(x, axis, step):
     count = lax.axis_size(axis)
     return lax.ppermute(x, axis, [(k, (k + step) % count) for k in range(count)])
@@ -235,14 +237,9 @@
 ):
     point_rows, point_cols, features = tracers.shape
     coef = jnp.broadcast_to(
-        jnp.stack(
-            [deinterleave(metric_x), deinterleave(metric_y), deinterleave(mass_weight),
-             deinterleave(mass_inverse)]
-        )[..., None],
-        (4, 4, 4, 8, 8, LANES),
-    )
-    den = mass_weight.reshape(8, 2, 2, 8, 2, 2).sum(axis=(2, 5)).transpose(1, 3, 0, 2)
-    den = jnp.broadcast_to(den[..., None], (2, 2, 8, 8, LANES))
+        jnp.stack([metric_x, metric_y, mass_weight, mass_inverse])[..., None],
+        (4, point_rows, point_cols, LANES),
+    )
 
     w, rt, rb, cl, cr = run_section(tracers, coef)
     top = shift(rb, "elem", 1)
@@ -255,8 +252,7 @@
 
     lax_halo = shift(along_x(cr, top[3, 7], bot[3, 7]), "sub", 1)
     rax_halo = shift(along_x(cl, top[0, 0], bot[0, 0]), "sub", -1)
-    settled, columns = run_settle(w, top, bot, lax_halo, rax_halo, coef, den)
-    columns = columns.reshape(-1, features).astype(jnp.bfloat16)
+    settled, columns = run_settle(w, top, bot, lax_halo, rax_halo, coef)
 
     column_count = columns.shape[0]
     slot_k = phys_slot.reshape(8, 2, 8, 2).transpose(0, 1, 3, 2).reshape(-1)

time: 114 us -> 109 us (0.956)
  local copies, waits for them, and re-layouts: 15.8 us -> 11.2 us
  starting transfers between devices: 23.2 us -> 19 us
  matrix products: 3.4 us -> 5.86 us
  loops' own time: 1.28 us -> 3.25 us
    reshape x5 -> x0, local copies, waits for them, and re-layouts: 3.65 us -> none  [the longest x4 3.23 us: deinterleave(): return field.reshape(8, 4, 8, 4).transpose(1, 3, 0, 2)]
    all_to_all x1, starting transfers between devices: 7.1 us -> 3.57 us  [on_device(): lax.all_to_all(replies, ('elem', 'sub'), split_axis=0, concat_axis=0, til...]
    another operation x1, loops' own time: 1.28 us -> 3.25 us  [on_device(): final_state = lax.fori_loop(0, jnp.max(span_cost), substep, start_state)]
    dot_general x1 -> x4, matrix products: 0.48 us -> 1.9 us  [substep(): jnp.einsum('crm,clm->crl', current, diff_inverse, preferred_element_type=...]
    convert_element_type x1 -> x0, other arithmetic: 1.29 us -> none  [on_device(): columns = columns.reshape(-1, features).astype(jnp.bfloat16)]
    broadcast_in_dim x2 -> x1, local copies, waits for them, and re-layouts: 2.7 us -> 1.92 us  [on_device(): jnp.broadcast_to(jnp.stack([metric_x, metric_y, mass_weight, mass_inverse...]
  transfers between devices with their start and end apart: 6 -> 6, of which waited for: 4 -> 5; matrix products, arithmetic and copies ran while one was open for 5% -> 5% of each run, Pallas kernels for 0% -> 0%
where the time goes in v3:
time: 109 us; the launch traced here: 108 us
  waiting for transfers between devices  45.3 us (42%)
  Pallas kernels  20.5 us (19%)
  starting transfers between devices  19 us (17%)
  local copies, waits for them, and re-layouts  11.2 us (10%)
  matrix products  5.86 us (5%)
  loops' own time  3.25 us (3%)
  other arithmetic  3.03 us (3%)
    all_to_all x1, waiting for transfers between devices, on_device(): lax.all_to_all(outgoing, ('elem', 'sub'), split_axis=0, concat_axis=0, ti...  20.4 us
    all_to_all x1, waiting for transfers between devices, on_device(): lax.all_to_all(replies, ('elem', 'sub'), split_axis=0, concat_axis=0, til...  19.3 us
    all_to_all x1, starting transfers between devices, on_device(): lax.all_to_all(outgoing, ('elem', 'sub'), split_axis=0, concat_axis=0, ti...  9.73 us
    pallas_call x1, Pallas kernels, run_section(): pl.pallas_call(section_kernel, grid=(nb,), in_specs=[spec((rows, cols, LA...  9.48 us
    pallas_call x1, Pallas kernels, run_settle(): pl.pallas_call(settle_kernel, grid=(nb,), in_specs=[spec((4, 4, 8, 8, LAN...  7.86 us
    ppermute x4, starting transfers between devices, shift(): lax.ppermute(x, axis, [(k, (k + step) % count) for k in range(count)])  5.71 us
    ppermute x4, waiting for transfers between devices, shift(): lax.ppermute(x, axis, [(k, (k + step) % count) for k in range(count)])  5.59 us
    all_to_all x1, starting transfers between devices, on_device(): lax.all_to_all(replies, ('elem', 'sub'), split_axis=0, concat_axis=0, til...  3.57 us
  transfers between devices with their start and end apart: 6, of which 5 were waited for; matrix products, arithmetic and copies ran while one was open for 5% of the time, Pallas kernels for 0%

profile of v3, /device:TPU:1, one launch (start us, length us, event | category | flops | bytes accessed | tf_op | source)
XLA Modules:
  0.0 108.3 jit_solution(14139097794682590424)
XLA Ops:
  0.0 0.8 pad_maximum_fusion.2
  0.8 1.9 %broadcast_in_dim.27.coef_ref = f32[4,32,32,128]{3,2,1,0:T(8,128)} broadcast(f32[4,32,32]{2,1,0:T(8,128)S(1)} %pad_maximum_fusion.2), dimensions={0,1,2} | broadcast | bytes 2113536 | tf_op jit(solution)/shard_map/broadcast_in_dim | solution.py:239
  2.7 9.5 %shard_map.82 = (f32[4,4,8,8,1024]{4,3,2,1,0:T(8,128)}, f32[4,8,1024]{2,1,0:T(8,128)}, f32[4,8,1024]{2,1,0:T(8,128)}, f32[4,8,1024]{2,1,0:T(8,128)}, f32[4,8,1024]{2,1,0:T(8,128)}) custom-call(bf16[32,32,1024]{2,1,0:T(8,128)(2,1)} %q_ref.1, f32[4,32,32,128]{3,2,1,0:T(8,128)} %broadcast_in_dim.27.coef_ref), custom_call_target="tpu_custom_call" | custom-call | tf_op jit(solution)/shard_map/pallas_call | solution.py:165
  12.2 3.1 %collective-permute-start = (f32[4,8,1024]{2,1,0:T(8,128)}, f32[4,8,1024]{2,1,0:T(8,128)S(1)}, u32[]{:S(2)}, u32[]{:S(2)}) collective-permute-start(f32[4,8,1024]{2,1,0:T(8,128)} %get-tuple-element.41), channel_id=1, source_target_pairs={{0,4},{4,8},{8,12},{12,16},{16,20},{20,24},{24,28},{28,32},{32,36}... | collective-permute-start | bytes 393224 | tf_op jit(solution)/shard_map/ppermute | solution.py:232
  15.3 0.8 fusion.21
  16.1 0.8 fusion.23
  16.8 0.1 reshape.154
  17.0 0.2 copy.17
  17.2 0.1 reshape.155
  17.3 0.1 broadcast_select_fusion
  17.4 0.8 slice.62
  18.2 0.8 slice.55
  19.1 0.2 convert_reduce_fusion
  19.3 0.6 collective-permute-done.1.bot_ref
  19.9 0.9 maximum_add_fusion
  20.8 2.5 %collective-permute-start.3 = (f32[4,8,1024]{2,1,0:T(8,128)S(1)}, f32[4,8,1024]{2,1,0:T(8,128)S(1)}, u32[]{:S(2)}, u32[]{:S(2)}) collective-permute-start(f32[4,8,1024]{2,1,0:T(8,128)S(1)} %pad_maximum_fusion.1), channel_id=1, source_target_pairs={{0,3},{1,0},{2,1},{3,2},{4,7},{5,4},{6,5},{7,6},{8,11},{9,8},{10,9... | collective-permute-start | bytes 393224 | tf_op jit(solution)/shard_map/ppermute | solution.py:232
  23.5 1.8 %collective-permute-done.3.rax_ref = f32[4,8,1024]{2,1,0:T(8,128)S(1)} collective-permute-done((f32[4,8,1024]{2,1,0:T(8,128)S(1)}, f32[4,8,1024]{2,1,0:T(8,128)S(1)}, u32[]{:S(2)}, u32[]{:S(2)}) %collective-permute-start.3) | collective-permute-done | bytes 131104 | tf_op jit(solution)/shard_map/ppermute | solution.py:232
  25.3 3.2 %collective-permute-done.2.lax_ref = f32[4,8,1024]{2,1,0:T(8,128)S(1)} collective-permute-done((f32[4,8,1024]{2,1,0:T(8,128)S(1)}, f32[4,8,1024]{2,1,0:T(8,128)S(1)}, u32[]{:S(2)}, u32[]{:S(2)}) %collective-permute-start.2) | collective-permute-done | bytes 131104 | tf_op jit(solution)/shard_map/ppermute | solution.py:232
  28.5 0.6 copy-done.4
  29.1 7.9 %shard_map.83 = (bf16[32,32,1024]{2,1,0:T(8,128)(2,1)}, bf16[256,1024]{1,0:T(8,128)(2,1)}) custom-call(f32[4,4,8,8,1024]{4,3,2,1,0:T(8,128)} %get-tuple-element.40.w_ref, f32[4,8,1024]{2,1,0:T(8,128)} %copy-done.1, f32[4,8,1024]{2,1,0:T(8,128)} %copy-done.2, f32[4,8,1024]{2,1,0:T(8,128)} %copy-done.4, f32[4,8,1024]{2,1,0:T(8,128)} %copy-done.3, ...), custom_call_target="tpu_custom_call" | custom-call | tf_op jit(solution)/shard_map/pallas_call | solution.py:193
  37.0 1.6 %convolution_convert_fusion.1 = bf16[512,1152]{1,0:T(8,128)(2,1)S(1)} fusion(bf16[256,128]{1,0:T(8,128)(2,1)S(1)} %broadcast_select_fusion, bf16[256,1024]{1,0:T(8,128)(2,1)} %get-tuple-element.46, s32[256]{0:T(256)S(1)} %multiply_add_fusion), kind=kOutput, calls=%fused_computation.3 | convolution fusion | flops 303890432 | bytes 1770496 | tf_op jit(solution)/shard_map/dot_general | solution.py:274
  38.5 1.2 %reshape.156 = bf16[128,4,1152]{2,1,0:T(4,128)(2,1)} reshape(bf16[512,1152]{1,0:T(8,128)(2,1)S(1)} %convolution_convert_fusion.1) | data formatting | bytes 2359296 | tf_op jit(solution)/shard_map/reshape | solution.py:275
  39.7 9.7 %all-to-all-start = ((bf16[128,4,1152]{2,1,0:T(4,128)(2,1)}), bf16[128,4,1152]{2,1,0:T(4,128)(2,1)S(1)}, u32[]{:S(2)}, u32[]{:S(2)}) async-start(bf16[128,4,1152]{2,1,0:T(4,128)(2,1)} %reshape.156), calls=%async_computation | async-start | bytes 2359296 | tf_op jit(solution)/shard_map/all_to_all | solution.py:276
  49.5 0.7 reduce_max.9
  50.2 20.4 %all-to-all-done = bf16[128,4,1152]{2,1,0:T(4,128)(2,1)S(1)} async-done(((bf16[128,4,1152]{2,1,0:T(4,128)(2,1)}), bf16[128,4,1152]{2,1,0:T(4,128)(2,1)S(1)}, u32[]{:S(2)}, u32[]{:S(2)}) %all-to-all-start) | async-done | bytes 1179680 | tf_op jit(solution)/shard_map/all_to_all | solution.py:276
  70.6 0.3 reshape.157
  70.9 0.1 add_reduce_fusion
  71.0 0.5 convolution_convert_fusion.3
  71.5 0.2 reshape.158
  71.8 0.8 copy-done
  72.5 5.3 %while.10 = (s32[]{:T(128)}, bf16[16,128,128]{2,1,0:T(8,128)(2,1)S(1)}, s32[]{:T(128)}, s32[16]{0:T(128)S(1)}, bf16[16,128,128]{2,1,0:T(8,128)(2,1)S(1)}, /*index=5*/s32[]{:T(128)}) while((s32[]{:T(128)}, bf16[16,128,128]{2,1,0:T(8,128)(2,1)S(1)}, s32[]{:T(128)}, s32[16]{0:T(128)S(1)}, bf16[16,128,128]{2,1,0:T(8,128)(2,1)S(1)}, ...), condition=%wide.region_3.4_spmd, body=%wide.region_2.3_spmd.sunk | while | flops 67633168 | bytes 2621609 | solution.py:294
  73.2 0.5 fusion.33
  74.4 0.5 fusion.33
  75.6 0.5 fusion.33
  76.8 0.5 fusion.33
  77.9 0.1 subtract_convert_fusion
  78.0 0.2 reshape.159
  78.3 0.5 convolution_convert_fusion.2
  78.8 1.2 %reshape.160 = bf16[128,4,1024]{2,1,0:T(4,128)(2,1)} reshape(bf16[512,1024]{1,0:T(8,128)(2,1)S(1)} %convolution_convert_fusion.2) | data formatting | bytes 2097152 | tf_op jit(solution)/shard_map/reshape | solution.py:304
  80.0 3.6 %all-to-all-start.1 = ((bf16[128,4,1024]{2,1,0:T(4,128)(2,1)}), bf16[128,4,1024]{2,1,0:T(4,128)(2,1)S(1)}, u32[]{:S(2)}, u32[]{:S(2)}) async-start(bf16[128,4,1024]{2,1,0:T(4,128)(2,1)} %reshape.160), calls=%async_computation.1 | async-start | bytes 2097152 | tf_op jit(solution)/shard_map/all_to_all | solution.py:305
  83.5 0.1 reduce_sum.12
  83.6 0.2 copy.16
  83.8 0.2 copy.19
  84.0 0.1 eq.85
  84.1 19.3 %all-to-all-done.1 = bf16[128,4,1024]{2,1,0:T(4,128)(2,1)S(1)} async-done(((bf16[128,4,1024]{2,1,0:T(4,128)(2,1)}), bf16[128,4,1024]{2,1,0:T(4,128)(2,1)S(1)}, u32[]{:S(2)}, u32[]{:S(2)}) %all-to-all-start.1) | async-done | bytes 1048608 | tf_op jit(solution)/shard_map/all_to_all | solution.py:305
  103.4 0.3 reshape.161
  103.7 1.5 %fusion.5.tend_ref = f32[256,1024]{1,0:T(8,128)} fusion(bf16[512,1024]{1,0:T(8,128)(2,1)S(1)} %reshape.161, s32[256]{0:T(256)S(1)} %eq.85), kind=kOutput, calls=%fused_computation.15 | convolution fusion | flops 268566528 | bytes 2098176 | tf_op jit(solution)/shard_map/dot_general | solution.py:309
  105.1 3.1 %shard_map.84 = bf16[32,32,1024]{2,1,0:T(8,128)(2,1)} custom-call(bf16[32,32,1024]{2,1,0:T(8,128)(2,1)} %get-tuple-element.45.st_ref, f32[256,1024]{1,0:T(8,128)} %fusion.5.tend_ref), custom_call_target="tpu_custom_call" | custom-call | tf_op jit(solution)/shard_map/pallas_call | solution.py:220
  (32 shorter events, 0.4 us)
Async XLA Ops:
  2.7 14.1 %copy-start.5 = (s32[256]{0:T(256)S(1)}, s32[256]{0:T(256)}, u32[]{:S(2)}) copy-start(s32[256]{0:T(256)} %param.15) | copy-start | bytes 3076
  12.2 7.1 %collective-permute-start = (f32[4,8,1024]{2,1,0:T(8,128)}, f32[4,8,1024]{2,1,0:T(8,128)S(1)}, u32[]{:S(2)}, u32[]{:S(2)}) collective-permute-start(f32[4,8,1024]{2,1,0:T(8,128)} %get-tuple-element.41), channel_id=1, source_target_pairs={{0,4},{4,8},{8,12},{12,16},{16,20},{20,24},{24,28},{28,32},{32,36}... | collective-permute-start | bytes 393224 | tf_op jit(solution)/shard_map/ppermute | solution.py:232
  15.3 4.6 %collective-permute-start.1 = (f32[4,8,1024]{2,1,0:T(8,128)}, f32[4,8,1024]{2,1,0:T(8,128)S(1)}, u32[]{:S(2)}, u32[]{:S(2)}) collective-permute-start(f32[4,8,1024]{2,1,0:T(8,128)} %get-tuple-element.42), channel_id=1, source_target_pairs={{0,124},{4,0},{8,4},{12,8},{16,12},{20,16},{24,20},{28,24},{32,28}... | collective-permute-start | bytes 393224 | tf_op jit(solution)/shard_map/ppermute | solution.py:232
  19.3 9.2 %copy-start.1 = (f32[4,8,1024]{2,1,0:T(8,128)}, f32[4,8,1024]{2,1,0:T(8,128)S(1)}, u32[]{:S(2)}) copy-start(f32[4,8,1024]{2,1,0:T(8,128)S(1)} %collective-permute-done.top_ref) | copy-start | bytes 393220
  19.9 8.6 %copy-start.2 = (f32[4,8,1024]{2,1,0:T(8,128)}, f32[4,8,1024]{2,1,0:T(8,128)S(1)}, u32[]{:S(2)}) copy-start(f32[4,8,1024]{2,1,0:T(8,128)S(1)} %collective-permute-done.1.bot_ref) | copy-start | bytes 393220
  20.8 4.5 %collective-permute-start.3 = (f32[4,8,1024]{2,1,0:T(8,128)S(1)}, f32[4,8,1024]{2,1,0:T(8,128)S(1)}, u32[]{:S(2)}, u32[]{:S(2)}) collective-permute-start(f32[4,8,1024]{2,1,0:T(8,128)S(1)} %pad_maximum_fusion.1), channel_id=1, source_target_pairs={{0,3},{1,0},{2,1},{3,2},{4,7},{5,4},{6,5},{7,6},{8,11},{9,8},{10,9... | collective-permute-start | bytes 393224 | tf_op jit(solution)/shard_map/ppermute | solution.py:232
  23.4 5.1 %collective-permute-start.2 = (f32[4,8,1024]{2,1,0:T(8,128)S(1)}, f32[4,8,1024]{2,1,0:T(8,128)S(1)}, u32[]{:S(2)}, u32[]{:S(2)}) collective-permute-start(f32[4,8,1024]{2,1,0:T(8,128)S(1)} %pad_maximum_fusion), channel_id=1, source_target_pairs={{0,1},{1,2},{2,3},{3,0},{4,5},{5,6},{6,7},{7,4},{8,9},{9,10},{10,1... | collective-permute-start | bytes 393224 | tf_op jit(solution)/shard_map/ppermute | solution.py:232
  25.3 3.2 %copy-start.3 = (f32[4,8,1024]{2,1,0:T(8,128)}, f32[4,8,1024]{2,1,0:T(8,128)S(1)}, u32[]{:S(2)}) copy-start(f32[4,8,1024]{2,1,0:T(8,128)S(1)} %collective-permute-done.3.rax_ref) | copy-start | bytes 393220
  28.5 0.6 copy-start.4
  39.7 9.7 %copy-start.6 = (s32[16]{0:T(128)S(1)}, s32[16]{0:T(128)}, u32[]{:S(2)}) copy-start(s32[16]{0:T(128)} %param.17) | copy-start | bytes 196
  39.7 30.9 %all-to-all-start = ((bf16[128,4,1152]{2,1,0:T(4,128)(2,1)}), bf16[128,4,1152]{2,1,0:T(4,128)(2,1)S(1)}, u32[]{:S(2)}, u32[]{:S(2)}) async-start(bf16[128,4,1152]{2,1,0:T(4,128)(2,1)} %reshape.156), calls=%async_computation | async-start | bytes 2359296 | tf_op jit(solution)/shard_map/all_to_all | solution.py:276
  71.5 1.0 copy-start
  80.0 23.4 %all-to-all-start.1 = ((bf16[128,4,1024]{2,1,0:T(4,128)(2,1)}), bf16[128,4,1024]{2,1,0:T(4,128)(2,1)S(1)}, u32[]{:S(2)}, u32[]{:S(2)}) async-start(bf16[128,4,1024]{2,1,0:T(4,128)(2,1)} %reshape.160), calls=%async_computation.1 | async-start | bytes 2097152 | tf_op jit(solution)/shard_map/all_to_all | solution.py:305

commit v4 on v3

--- a/solution.py
+++ b/solution.py
@@ -150,6 +150,71 @@
     lax.fori_loop(0, 16, body, 0)
 
 
+def edge_kernel(cl_ref, cr_ref, top_ref, bot_ref, lsend_ref, rsend_ref):
+    sub = lax.broadcasted_iota(jnp.int32, cl_ref.shape[1:], 0)
+    for side_ref, out_ref, b, j in ((cr_ref, lsend_ref, 7, 3), (cl_ref, rsend_ref, 0, 0)):
+        above = top_ref[j, pl.ds(b, 1), :]
+        below = bot_ref[j, pl.ds(b, 1), :]
+        first = side_ref[0] + jnp.where(sub == 0, above, pltpu.roll(side_ref[3], 1, 0))
+        last = side_ref[3] + jnp.where(sub == 7, below, pltpu.roll(side_ref[0], 7, 0))
+        out_ref[0] = first
+        out_ref[1] = side_ref[1]
+        out_ref[2] = side_ref[2]
+        out_ref[3] = last
+
+
+def run_edges(cl, cr, top, bot):
+    return pl.pallas_call(
+        edge_kernel,
+        out_shape=[jax.ShapeDtypeStruct(cl.shape, cl.dtype)] * 2,
+    )(cl, cr, top, bot)
+
+
+def diffusion_kernel(cost_ref, place_ref, arrived_ref, inv_ref, reply_ref, out_ref, slot_ref, tend_ref):
+    slot_ref[...] = jnp.dot(
+        place_ref[...], arrived_ref[:, pl.ds(0, slot_ref.shape[1])],
+        preferred_element_type=jnp.float32,
+    ).astype(slot_ref.dtype)
+    span_slots = slot_ref.shape[0] // inv_ref.shape[0]
+    steps = 4
+
+    def body(span, carry):
+        rows = pl.ds(pl.multiple_of(span * span_slots, span_slots), span_slots)
+        tracers = slot_ref.shape[1] // LANES
+        start = jnp.concatenate(
+            [slot_ref[rows, pl.ds(t * LANES, LANES)] for t in range(tracers)], axis=0
+        )
+        inverse = inv_ref[span]
+        cost = cost_ref[span]
+        current = start
+        for step in range(steps):
+            updated = lax.dot_general(
+                current, inverse, (((1,), (1,)), ((), ())), preferred_element_type=jnp.float32
+            ).astype(current.dtype)
+            current = jnp.where(step < cost, updated, current)
+        tend = (current.astype(jnp.float32) - start.astype(jnp.float32)).astype(tend_ref.dtype)
+        for t in range(tracers):
+            tend_ref[rows, pl.ds(t * LANES, LANES)] = tend[t * span_slots:(t + 1) * span_slots]
+        return carry
+
+    lax.fori_loop(0, inv_ref.shape[0], body, 0)
+    out_ref[...] = jnp.dot(
+        reply_ref[...], tend_ref[...], preferred_element_type=jnp.float32
+    ).astype(out_ref.dtype)
+
+
+def run_diffusion(span_cost, place, arrived, inverse, reply, features):
+    slots = place.shape[0]
+    vmem = pltpu.VMEM
+    return pl.pallas_call(
+        diffusion_kernel,
+        in_specs=[pl.BlockSpec(memory_space=pltpu.SMEM)] + [pl.BlockSpec(memory_space=vmem)] * 4,
+        out_specs=pl.BlockSpec(memory_space=vmem),
+        out_shape=jax.ShapeDtypeStruct((reply.shape[0], features), jnp.bfloat16),
+        scratch_shapes=[vmem((slots, features), jnp.bfloat16), vmem((slots, features), jnp.bfloat16)],
+    )(span_cost, place, arrived, inverse, reply)
+
+
 def spec(shape, lane_axis=None):
     nd = len(shape)
 
@@ -245,13 +310,9 @@
     top = shift(rb, "elem", 1)
     bot = shift(rt, "elem", -1)
 
-    def along_x(side, above, below):
-        first = side[0] + jnp.concatenate([above[None], side[3, :-1]], axis=0)
-        last = side[3] + jnp.concatenate([side[0, 1:], below[None]], axis=0)
-        return jnp.stack([first, side[1], side[2], last])
-
-    lax_halo = shift(along_x(cr, top[3, 7], bot[3, 7]), "sub", 1)
-    rax_halo = shift(along_x(cl, top[0, 0], bot[0, 0]), "sub", -1)
+    lsend, rsend = run_edges(cl, cr, top, bot)
+    lax_halo = shift(lsend, "sub", 1)
+    rax_halo = shift(rsend, "sub", -1)
     settled, columns = run_settle(w, top, bot, lax_halo, rax_halo, coef)
 
     column_count = columns.shape[0]
@@ -271,36 +332,16 @@
         jnp.arange(LANES)[None, :] == 0, (landing + 1)[:, None].astype(jnp.bfloat16), 0
     ).astype(jnp.bfloat16)
     payload = jnp.concatenate([columns, label_block], axis=1)
-    outgoing = jnp.dot(send_table, payload, preferred_element_type=jnp.float32).astype(jnp.bfloat16)
-    outgoing = outgoing.reshape(device_count, capacity, features + LANES)
+    outgoing = jnp.einsum(
+        "dck,kf->dcf", send_table.reshape(device_count, capacity, column_count), payload,
+        preferred_element_type=jnp.float32,
+    ).astype(jnp.bfloat16)
     arrived = lax.all_to_all(outgoing, ("elem", "sub"), split_axis=0, concat_axis=0, tiled=True)
     arrived = arrived.reshape(-1, features + LANES)
     arrived_labels = arrived[:, features].astype(jnp.int32) - 1
-    arrived = arrived[:, :features]
     place_table = (column_order[:, None] == arrived_labels[None, :]).astype(jnp.bfloat16)
-    slot_state = jnp.dot(place_table, arrived, preferred_element_type=jnp.float32).astype(
-        jnp.bfloat16
-    )
-    span_count = span_cost.shape[0]
-    levels = diff_inverse.shape[1]
-    start_state = slot_state.reshape(span_count, -1, levels)
-
-    def substep(step_index, current):
-        updated = jnp.einsum(
-            "crm,clm->crl", current, diff_inverse, preferred_element_type=jnp.float32
-        ).astype(jnp.bfloat16)
-        return jnp.where((step_index < span_cost)[:, None, None], updated, current)
-
-    final_state = lax.fori_loop(0, jnp.max(span_cost), substep, start_state)
-    tendency = (
-        (final_state.astype(jnp.float32) - start_state.astype(jnp.float32))
-        .astype(jnp.bfloat16)
-        .reshape(column_count, features)
-    )
     reply_table = (arrived_labels[:, None] == column_order[None, :]).astype(jnp.bfloat16)
-    replies = jnp.dot(reply_table, tendency, preferred_element_type=jnp.float32).astype(
-        jnp.bfloat16
-    )
+    replies = run_diffusion(span_cost, place_table, arrived, diff_inverse, reply_table, features)
     replies = replies.reshape(device_count, capacity, features)
     returned = lax.all_to_all(replies, ("elem", "sub"), split_axis=0, concat_axis=0, tiled=True)
     returned = returned.reshape(slot_total, features)

time: 109 us -> 116 us (1.064)
  blocking collectives: 0 us -> 32 us
  waiting for transfers between devices: 45.3 us -> 25.7 us
  Pallas kernels: 20.5 us -> 34 us
  starting transfers between devices: 19 us -> 9.31 us
  loops' own time: 3.25 us -> 0 us
  local copies, waits for them, and re-layouts: 11.2 us -> 7.95 us
  matrix products: 5.86 us -> 3.04 us
    all_to_all x0 -> x1, blocking collectives: none -> 32 us  [on_device(): lax.all_to_all(outgoing, ('elem', 'sub'), split_axis=0, concat_axis=0, ti...]
    all_to_all x1 -> x0, waiting for transfers between devices: 20.4 us -> none  [on_device(): lax.all_to_all(outgoing, ('elem', 'sub'), split_axis=0, concat_axis=0, ti...]
    pallas_call x0 -> x2, Pallas kernels: none -> 13.5 us  [the longest x1 11.7 us: run_diffusion(): pl.pallas_call(diffusion_kernel, in_specs=[pl.BlockSpec(memory_space=pltp...]
    all_to_all x1 -> x0, starting transfers between devices: 9.73 us -> none  [on_device(): lax.all_to_all(outgoing, ('elem', 'sub'), split_axis=0, concat_axis=0, ti...]
    slice x6 -> x0, local copies, waits for them, and re-layouts: 3.27 us -> none  [the longest x2 1.69 us: along_x(): return jnp.stack([first, side[1], side[2], last])]
    another operation x1 -> x0, loops' own time: 3.25 us -> none  [on_device(): final_state = lax.fori_loop(0, jnp.max(span_cost), substep, start_state)]
    dot_general x7 -> x1, matrix products: 4.39 us -> 1.58 us  [on_device(): jnp.einsum('dck,kf->dcf', send_table.reshape(device_count, capacity, colu...]
    convert_element_type x1 -> x2, other arithmetic: 0.14 us -> 1.78 us  [the longest x1 0.93 us: on_device(): (column_order[:, None] == arrived_labels[None, :]).astype(jnp.bfloat16)]
  transfers between devices with their start and end apart: 6 -> 5, of which waited for: 5 -> 4; matrix products, arithmetic and copies ran while one was open for 5% -> 1% of each run, Pallas kernels for 0% -> 0%
where the time goes in v4:
time: 116 us; the launch traced here: 115 us
  Pallas kernels  34 us (29%)
  blocking collectives  32 us (28%)
  waiting for transfers between devices  25.7 us (22%)
  starting transfers between devices  9.31 us (8%)
  local copies, waits for them, and re-layouts  7.95 us (7%)
  matrix products  3.04 us (3%)
  other arithmetic  3.03 us (3%)
    all_to_all x1, blocking collectives, on_device(): lax.all_to_all(outgoing, ('elem', 'sub'), split_axis=0, concat_axis=0, ti...  32 us
    all_to_all x1, waiting for transfers between devices, on_device(): lax.all_to_all(replies, ('elem', 'sub'), split_axis=0, concat_axis=0, til...  19.3 us
    pallas_call x1, Pallas kernels, run_diffusion(): pl.pallas_call(diffusion_kernel, in_specs=[pl.BlockSpec(memory_space=pltp...  11.7 us
    pallas_call x1, Pallas kernels, run_section(): pl.pallas_call(section_kernel, grid=(nb,), in_specs=[spec((rows, cols, LA...  9.51 us
    pallas_call x1, Pallas kernels, run_settle(): pl.pallas_call(settle_kernel, grid=(nb,), in_specs=[spec((4, 4, 8, 8, LAN...  7.86 us
    ppermute x4, waiting for transfers between devices, shift(): lax.ppermute(x, axis, [(k, (k + step) % count) for k in range(count)])  6.42 us
    ppermute x4, starting transfers between devices, shift(): lax.ppermute(x, axis, [(k, (k + step) % count) for k in range(count)])  5.74 us
    all_to_all x1, starting transfers between devices, on_device(): lax.all_to_all(replies, ('elem', 'sub'), split_axis=0, concat_axis=0, til...  3.57 us
  transfers between devices with their start and end apart: 5, of which 4 were waited for; matrix products, arithmetic and copies ran while one was open for 1% of the time, Pallas kernels for 0%

profile of v4, /device:TPU:1, one launch (start us, length us, event | category | flops | bytes accessed | tf_op | source)
XLA Modules:
  0.0 115.1 jit_solution(17559604846221540290)
XLA Ops:
  0.0 0.8 pad_maximum_fusion
  0.8 1.9 %broadcast_in_dim.15.coef_ref = f32[4,32,32,128]{3,2,1,0:T(8,128)} broadcast(f32[4,32,32]{2,1,0:T(8,128)S(1)} %pad_maximum_fusion), dimensions={0,1,2} | broadcast | bytes 2113536 | tf_op jit(solution)/shard_map/broadcast_in_dim | solution.py:304
  2.7 0.0 copy-start.5
  2.7 9.5 %shard_map.82 = (f32[4,4,8,8,1024]{4,3,2,1,0:T(8,128)}, f32[4,8,1024]{2,1,0:T(8,128)}, f32[4,8,1024]{2,1,0:T(8,128)}, f32[4,8,1024]{2,1,0:T(8,128)}, f32[4,8,1024]{2,1,0:T(8,128)}) custom-call(bf16[32,32,1024]{2,1,0:T(8,128)(2,1)} %q_ref.1, f32[4,32,32,128]{3,2,1,0:T(8,128)} %broadcast_in_dim.15.coef_ref), custom_call_target="tpu_custom_call" | custom-call | tf_op jit(solution)/shard_map/pallas_call | solution.py:230
  12.2 3.1 %collective-permute-start = (f32[4,8,1024]{2,1,0:T(8,128)}, f32[4,8,1024]{2,1,0:T(8,128)S(1)}, u32[]{:S(2)}, u32[]{:S(2)}) collective-permute-start(f32[4,8,1024]{2,1,0:T(8,128)} %get-tuple-element.15), channel_id=1, source_target_pairs={{0,4},{4,8},{8,12},{12,16},{16,20},{20,24},{24,28},{28,32},{32,36}... | collective-permute-start | bytes 393224 | tf_op jit(solution)/shard_map/ppermute | solution.py:297
  15.3 0.0 collective-permute-start.1
  15.3 0.0 copy-done.5
  15.3 0.1 reshape.141
  15.4 0.2 copy.20
  15.6 0.1 reshape.142
  15.7 0.1 broadcast_select_fusion
  15.8 0.2 convert_reduce_fusion
  16.0 1.5 %collective-permute-done.top_ref = f32[4,8,1024]{2,1,0:T(8,128)S(1)} collective-permute-done((f32[4,8,1024]{2,1,0:T(8,128)}, f32[4,8,1024]{2,1,0:T(8,128)S(1)}, u32[]{:S(2)}, u32[]{:S(2)}) %collective-permute-start) | collective-permute-done | bytes 131104 | tf_op jit(solution)/shard_map/ppermute | solution.py:297
  17.5 0.0 copy-start.1
  17.5 2.3 %collective-permute-done.1.bot_ref = f32[4,8,1024]{2,1,0:T(8,128)S(1)} collective-permute-done((f32[4,8,1024]{2,1,0:T(8,128)}, f32[4,8,1024]{2,1,0:T(8,128)S(1)}, u32[]{:S(2)}, u32[]{:S(2)}) %collective-permute-start.1) | collective-permute-done | bytes 131104 | tf_op jit(solution)/shard_map/ppermute | solution.py:297
  19.9 0.0 copy-start.2
  19.9 0.0 copy-done.1
  19.9 0.6 copy-done.2
  20.5 1.8 %shard_map.83 = (f32[4,8,1024]{2,1,0:T(8,128)}, f32[4,8,1024]{2,1,0:T(8,128)}) custom-call(f32[4,8,1024]{2,1,0:T(8,128)} %get-tuple-element.17.cl_ref, f32[4,8,1024]{2,1,0:T(8,128)} %get-tuple-element.18.cr_ref, f32[4,8,1024]{2,1,0:T(8,128)} %copy-done.1, f32[4,8,1024]{2,1,0:T(8,128)} %copy-done.2), custom_call_target="tpu_custom_call" | custom-call | tf_op jit(solution)/shard_map/pallas_call | solution.py:167
  22.4 1.2 %collective-permute-start.2 = (f32[4,8,1024]{2,1,0:T(8,128)}, f32[4,8,1024]{2,1,0:T(8,128)S(1)}, u32[]{:S(2)}, u32[]{:S(2)}) collective-permute-start(f32[4,8,1024]{2,1,0:T(8,128)} %get-tuple-element.19), channel_id=1, source_target_pairs={{0,1},{1,2},{2,3},{3,0},{4,5},{5,6},{6,7},{7,4},{8,9},{9,10},{10,1... | collective-permute-start | bytes 393224 | tf_op jit(solution)/shard_map/ppermute | solution.py:297
  23.6 1.5 %collective-permute-start.3 = (f32[4,8,1024]{2,1,0:T(8,128)}, f32[4,8,1024]{2,1,0:T(8,128)S(1)}, u32[]{:S(2)}, u32[]{:S(2)}) collective-permute-start(f32[4,8,1024]{2,1,0:T(8,128)} %get-tuple-element.20), channel_id=1, source_target_pairs={{0,3},{1,0},{2,1},{3,2},{4,7},{5,4},{6,5},{7,6},{8,11},{9,8},{10,9... | collective-permute-start | bytes 393224 | tf_op jit(solution)/shard_map/ppermute | solution.py:297
  25.0 2.6 %collective-permute-done.2.lax_ref = f32[4,8,1024]{2,1,0:T(8,128)S(1)} collective-permute-done((f32[4,8,1024]{2,1,0:T(8,128)}, f32[4,8,1024]{2,1,0:T(8,128)S(1)}, u32[]{:S(2)}, u32[]{:S(2)}) %collective-permute-start.2) | collective-permute-done | bytes 131104 | tf_op jit(solution)/shard_map/ppermute | solution.py:297
  27.6 0.0 copy-start.3
  27.6 0.0 collective-permute-done.3.rax_ref
  27.6 0.0 copy-start.4
  27.6 0.7 copy-done.3
  28.3 0.0 copy-done.4
  28.3 7.9 %shard_map.84 = (bf16[32,32,1024]{2,1,0:T(8,128)(2,1)}, bf16[256,1024]{1,0:T(8,128)(2,1)}) custom-call(f32[4,4,8,8,1024]{4,3,2,1,0:T(8,128)} %get-tuple-element.14.w_ref, f32[4,8,1024]{2,1,0:T(8,128)} %copy-done.1, f32[4,8,1024]{2,1,0:T(8,128)} %copy-done.2, f32[4,8,1024]{2,1,0:T(8,128)} %copy-done.3, f32[4,8,1024]{2,1,0:T(8,128)} %copy-done.4, ...), custom_call_target="tpu_custom_call" | custom-call | tf_op jit(solution)/shard_map/pallas_call | solution.py:258
  36.2 1.6 %convolution_convert_fusion = bf16[128,4,1152]{2,0,1:T(8,128)(2,1)S(1)} fusion(bf16[256,128]{1,0:T(8,128)(2,1)S(1)} %broadcast_select_fusion, bf16[256,1024]{1,0:T(8,128)(2,1)} %get-tuple-element.22, s32[256]{0:T(256)S(1)} %multiply_add_fusion.1, s32[128,4]{0,1:T(4,128)S(1)} %multiply_add_fusion), kind=kOutput, calls=%fused_computation | convolution fusion | flops 303890432 | bytes 1772544 | tf_op jit(solution)/shard_map/dck,kf->dcf/dot_general | solution.py:335
  37.7 0.9 copy.23
  38.7 32.0 %all_to_all.10 = bf16[128,4,1152]{2,1,0:T(4,128)(2,1)S(1)} all-to-all(bf16[128,4,1152]{2,1,0:T(4,128)(2,1)S(1)} %copy.23), channel_id=1, replica_groups=mesh['elem'=32,'sub'=4] {'elem','sub'}, dimensions={0} | all-to-all | bytes 2359296 | tf_op jit(solution)/shard_map/all_to_all | solution.py:339
  70.6 0.3 reshape.143.arrived_ref
  70.9 0.0 copy-start
  70.9 0.1 add_reduce_fusion
  71.1 0.9 fusion.3.place_ref
  72.0 0.8 fusion.4.reply_ref
  72.9 0.0 copy-done
  72.9 11.7 %shard_map.85 = bf16[512,1024]{1,0:T(8,128)(2,1)} custom-call(s32[16]{0:T(128)} %cost_ref.1, bf16[256,512]{1,0:T(8,128)(2,1)} %fusion.3.place_ref, bf16[512,1152]{1,0:T(8,128)(2,1)} %copy-done, bf16[16,128,128]{2,1,0:T(8,128)(2,1)} %inv_ref.1, bf16[512,256]{1,0:T(8,128)(2,1)} %fusion.4.reply_ref), custom_call_target="tpu_custom_call" | custom-call | tf_op jit(solution)/shard_map/pallas_call | solution.py:209
  84.5 2.2 %reshape.144 = bf16[128,4,1024]{2,1,0:T(4,128)(2,1)} reshape(bf16[512,1024]{1,0:T(8,128)(2,1)} %shard_map.85) | data formatting | bytes 2097152 | tf_op jit(solution)/shard_map/reshape | solution.py:345
  86.8 3.6 %all-to-all-start.1 = ((bf16[128,4,1024]{2,1,0:T(4,128)(2,1)}), bf16[128,4,1024]{2,1,0:T(4,128)(2,1)S(1)}, u32[]{:S(2)}, u32[]{:S(2)}) async-start(bf16[128,4,1024]{2,1,0:T(4,128)(2,1)} %reshape.144), calls=%async_computation.1 | async-start | bytes 2097152 | tf_op jit(solution)/shard_map/all_to_all | solution.py:346
  90.4 0.1 reduce_sum.12
  90.5 0.2 copy.19
  90.7 0.2 copy.22
  90.8 0.1 eq.90
  91.0 19.3 %all-to-all-done.1 = bf16[128,4,1024]{2,1,0:T(4,128)(2,1)S(1)} async-done(((bf16[128,4,1024]{2,1,0:T(4,128)(2,1)}), bf16[128,4,1024]{2,1,0:T(4,128)(2,1)S(1)}, u32[]{:S(2)}, u32[]{:S(2)}) %all-to-all-start.1) | async-done | bytes 1048608 | tf_op jit(solution)/shard_map/all_to_all | solution.py:346
  110.2 0.3 reshape.145
  110.5 1.5 %fusion.2.tend_ref = f32[256,1024]{1,0:T(8,128)} fusion(bf16[512,1024]{1,0:T(8,128)(2,1)S(1)} %reshape.145, s32[256]{0:T(256)S(1)} %eq.90), kind=kOutput, calls=%fused_computation.7 | convolution fusion | flops 268566528 | bytes 2098176 | tf_op jit(solution)/shard_map/dot_general | solution.py:350
  112.0 3.1 %shard_map.86 = bf16[32,32,1024]{2,1,0:T(8,128)(2,1)} custom-call(bf16[32,32,1024]{2,1,0:T(8,128)(2,1)} %get-tuple-element.21.st_ref, f32[256,1024]{1,0:T(8,128)} %fusion.2.tend_ref), custom_call_target="tpu_custom_call" | custom-call | tf_op jit(solution)/shard_map/pallas_call | solution.py:285
  (5 shorter events, 0.1 us)
Async XLA Ops:
  2.7 12.6 %copy-start.5 = (s32[256]{0:T(256)S(1)}, s32[256]{0:T(256)}, u32[]{:S(2)}) copy-start(s32[256]{0:T(256)} %param.13) | copy-start | bytes 3076
  12.2 5.3 %collective-permute-start = (f32[4,8,1024]{2,1,0:T(8,128)}, f32[4,8,1024]{2,1,0:T(8,128)S(1)}, u32[]{:S(2)}, u32[]{:S(2)}) collective-permute-start(f32[4,8,1024]{2,1,0:T(8,128)} %get-tuple-element.15), channel_id=1, source_target_pairs={{0,4},{4,8},{8,12},{12,16},{16,20},{20,24},{24,28},{28,32},{32,36}... | collective-permute-start | bytes 393224 | tf_op jit(solution)/shard_map/ppermute | solution.py:297
  15.3 4.6 %collective-permute-start.1 = (f32[4,8,1024]{2,1,0:T(8,128)}, f32[4,8,1024]{2,1,0:T(8,128)S(1)}, u32[]{:S(2)}, u32[]{:S(2)}) collective-permute-start(f32[4,8,1024]{2,1,0:T(8,128)} %get-tuple-element.16), channel_id=1, source_target_pairs={{0,124},{4,0},{8,4},{12,8},{16,12},{20,16},{24,20},{28,24},{32,28}... | collective-permute-start | bytes 393224 | tf_op jit(solution)/shard_map/ppermute | solution.py:297
  17.5 2.3 %copy-start.1 = (f32[4,8,1024]{2,1,0:T(8,128)}, f32[4,8,1024]{2,1,0:T(8,128)S(1)}, u32[]{:S(2)}) copy-start(f32[4,8,1024]{2,1,0:T(8,128)S(1)} %collective-permute-done.top_ref) | copy-start | bytes 393220
  19.9 0.7 copy-start.2
  22.4 5.2 %collective-permute-start.2 = (f32[4,8,1024]{2,1,0:T(8,128)}, f32[4,8,1024]{2,1,0:T(8,128)S(1)}, u32[]{:S(2)}, u32[]{:S(2)}) collective-permute-start(f32[4,8,1024]{2,1,0:T(8,128)} %get-tuple-element.19), channel_id=1, source_target_pairs={{0,1},{1,2},{2,3},{3,0},{4,5},{5,6},{6,7},{7,4},{8,9},{9,10},{10,1... | collective-permute-start | bytes 393224 | tf_op jit(solution)/shard_map/ppermute | solution.py:297
  23.6 4.0 %collective-permute-start.3 = (f32[4,8,1024]{2,1,0:T(8,128)}, f32[4,8,1024]{2,1,0:T(8,128)S(1)}, u32[]{:S(2)}, u32[]{:S(2)}) collective-permute-start(f32[4,8,1024]{2,1,0:T(8,128)} %get-tuple-element.20), channel_id=1, source_target_pairs={{0,3},{1,0},{2,1},{3,2},{4,7},{5,4},{6,5},{7,6},{8,11},{9,8},{10,9... | collective-permute-start | bytes 393224 | tf_op jit(solution)/shard_map/ppermute | solution.py:297
  27.6 0.7 copy-start.3
  27.6 0.7 copy-start.4
  70.9 1.9 %copy-start = (bf16[512,1152]{1,0:T(8,128)(2,1)}, bf16[512,1152]{1,0:T(8,128)(2,1)S(1)}, u32[]{:S(2)}) copy-start(bf16[512,1152]{1,0:T(8,128)(2,1)S(1)} %reshape.143.arrived_ref) | copy-start | bytes 3538948
  86.8 23.4 %all-to-all-start.1 = ((bf16[128,4,1024]{2,1,0:T(4,128)(2,1)}), bf16[128,4,1024]{2,1,0:T(4,128)(2,1)S(1)}, u32[]{:S(2)}, u32[]{:S(2)}) async-start(bf16[128,4,1024]{2,1,0:T(4,128)(2,1)} %reshape.144), calls=%async_computation.1 | async-start | bytes 2097152 | tf_op jit(solution)/shard_map/all_to_all | solution.py:346

commit v5 on v4

--- a/solution.py
+++ b/solution.py
@@ -178,26 +178,36 @@
     span_slots = slot_ref.shape[0] // inv_ref.shape[0]
     steps = 4
 
-    def body(span, carry):
-        rows = pl.ds(pl.multiple_of(span * span_slots, span_slots), span_slots)
-        tracers = slot_ref.shape[1] // LANES
-        start = jnp.concatenate(
-            [slot_ref[rows, pl.ds(t * LANES, LANES)] for t in range(tracers)], axis=0
-        )
-        inverse = inv_ref[span]
-        cost = cost_ref[span]
-        current = start
+    tracers = slot_ref.shape[1] // LANES
+    group = 4
+
+    def body(g, carry):
+        rows, starts, inverses, costs = [], [], [], []
+        for u in range(group):
+            span = g * group + u
+            rows.append(pl.ds(pl.multiple_of(span * span_slots, span_slots), span_slots))
+            starts.append(jnp.concatenate(
+                [slot_ref[rows[u], pl.ds(t * LANES, LANES)] for t in range(tracers)], axis=0
+            ))
+            inverses.append(inv_ref[span])
+            costs.append(cost_ref[span])
+        current = list(starts)
         for step in range(steps):
-            updated = lax.dot_general(
-                current, inverse, (((1,), (1,)), ((), ())), preferred_element_type=jnp.float32
-            ).astype(current.dtype)
-            current = jnp.where(step < cost, updated, current)
-        tend = (current.astype(jnp.float32) - start.astype(jnp.float32)).astype(tend_ref.dtype)
-        for t in range(tracers):
-            tend_ref[rows, pl.ds(t * LANES, LANES)] = tend[t * span_slots:(t + 1) * span_slots]
+            for u in range(group):
+                updated = lax.dot_general(
+                    current[u], inverses[u], (((1,), (1,)), ((), ())),
+                    preferred_element_type=jnp.float32,
+                ).astype(current[u].dtype)
+                current[u] = jnp.where(step < costs[u], updated, current[u])
+        for u in range(group):
+            tend = (current[u].astype(jnp.float32) - starts[u].astype(jnp.float32)).astype(
+                tend_ref.dtype
+            )
+            for t in range(tracers):
+                tend_ref[rows[u], pl.ds(t * LANES, LANES)] = tend[t * span_slots:(t + 1) * span_slots]
         return carry
 
-    lax.fori_loop(0, inv_ref.shape[0], body, 0)
+    lax.fori_loop(0, inv_ref.shape[0] // group, body, 0)
     out_ref[...] = jnp.dot(
         reply_ref[...], tend_ref[...], preferred_element_type=jnp.float32
     ).astype(out_ref.dtype)

time: 116 us -> 110 us (0.948)
  Pallas kernels: 34 us -> 28.1 us
    pallas_call x1, Pallas kernels: 11.7 us -> 5.75 us  [run_diffusion(): pl.pallas_call(diffusion_kernel, in_specs=[pl.BlockSpec(memory_space=pltp...]
where the time goes in v5:
time: 110 us; the launch traced here: 109 us
  blocking collectives  32 us (29%)
  Pallas kernels  28.1 us (26%)
  waiting for transfers between devices  25.7 us (23%)
  starting transfers between devices  9.31 us (8%)
  local copies, waits for them, and re-layouts  7.95 us (7%)
  matrix products  3.05 us (3%)
  other arithmetic  3.03 us (3%)
    all_to_all x1, blocking collectives, on_device(): lax.all_to_all(outgoing, ('elem', 'sub'), split_axis=0, concat_axis=0, ti...  32 us
    all_to_all x1, waiting for transfers between devices, on_device(): lax.all_to_all(replies, ('elem', 'sub'), split_axis=0, concat_axis=0, til...  19.3 us
    pallas_call x1, Pallas kernels, run_section(): pl.pallas_call(section_kernel, grid=(nb,), in_specs=[spec((rows, cols, LA...  9.51 us
    pallas_call x1, Pallas kernels, run_settle(): pl.pallas_call(settle_kernel, grid=(nb,), in_specs=[spec((4, 4, 8, 8, LAN...  7.86 us
    ppermute x4, waiting for transfers between devices, shift(): lax.ppermute(x, axis, [(k, (k + step) % count) for k in range(count)])  6.42 us
    pallas_call x1, Pallas kernels, run_diffusion(): pl.pallas_call(diffusion_kernel, in_specs=[pl.BlockSpec(memory_space=pltp...  5.75 us
    ppermute x4, starting transfers between devices, shift(): lax.ppermute(x, axis, [(k, (k + step) % count) for k in range(count)])  5.74 us
    all_to_all x1, starting transfers between devices, on_device(): lax.all_to_all(replies, ('elem', 'sub'), split_axis=0, concat_axis=0, til...  3.57 us
  transfers between devices with their start and end apart: 5, of which 4 were waited for; matrix products, arithmetic and copies ran while one was open for 1% of the time, Pallas kernels for 0%

profile of v5, /device:TPU:1, one launch (start us, length us, event | category | flops | bytes accessed | tf_op | source)
XLA Modules:
  0.0 109.2 jit_solution(6620853109136594873)
XLA Ops:
  0.0 0.8 pad_maximum_fusion
  0.8 1.9 %broadcast_in_dim.15.coef_ref = f32[4,32,32,128]{3,2,1,0:T(8,128)} broadcast(f32[4,32,32]{2,1,0:T(8,128)S(1)} %pad_maximum_fusion), dimensions={0,1,2} | broadcast | bytes 2113536 | tf_op jit(solution)/shard_map/broadcast_in_dim | solution.py:314
  2.7 0.0 copy-start.5
  2.7 9.5 %shard_map.82 = (f32[4,4,8,8,1024]{4,3,2,1,0:T(8,128)}, f32[4,8,1024]{2,1,0:T(8,128)}, f32[4,8,1024]{2,1,0:T(8,128)}, f32[4,8,1024]{2,1,0:T(8,128)}, f32[4,8,1024]{2,1,0:T(8,128)}) custom-call(bf16[32,32,1024]{2,1,0:T(8,128)(2,1)} %q_ref.1, f32[4,32,32,128]{3,2,1,0:T(8,128)} %broadcast_in_dim.15.coef_ref), custom_call_target="tpu_custom_call" | custom-call | tf_op jit(solution)/shard_map/pallas_call | solution.py:240
  12.2 3.1 %collective-permute-start = (f32[4,8,1024]{2,1,0:T(8,128)}, f32[4,8,1024]{2,1,0:T(8,128)S(1)}, u32[]{:S(2)}, u32[]{:S(2)}) collective-permute-start(f32[4,8,1024]{2,1,0:T(8,128)} %get-tuple-element.15), channel_id=1, source_target_pairs={{0,4},{4,8},{8,12},{12,16},{16,20},{20,24},{24,28},{28,32},{32,36}... | collective-permute-start | bytes 393224 | tf_op jit(solution)/shard_map/ppermute | solution.py:307
  15.3 0.0 collective-permute-start.1
  15.3 0.0 copy-done.5
  15.3 0.1 reshape.141
  15.4 0.2 copy.20
  15.6 0.1 reshape.142
  15.7 0.1 broadcast_select_fusion
  15.8 0.2 convert_reduce_fusion
  16.0 1.5 %collective-permute-done.top_ref = f32[4,8,1024]{2,1,0:T(8,128)S(1)} collective-permute-done((f32[4,8,1024]{2,1,0:T(8,128)}, f32[4,8,1024]{2,1,0:T(8,128)S(1)}, u32[]{:S(2)}, u32[]{:S(2)}) %collective-permute-start) | collective-permute-done | bytes 131104 | tf_op jit(solution)/shard_map/ppermute | solution.py:307
  17.5 0.0 copy-start.1
  17.5 2.3 %collective-permute-done.1.bot_ref = f32[4,8,1024]{2,1,0:T(8,128)S(1)} collective-permute-done((f32[4,8,1024]{2,1,0:T(8,128)}, f32[4,8,1024]{2,1,0:T(8,128)S(1)}, u32[]{:S(2)}, u32[]{:S(2)}) %collective-permute-start.1) | collective-permute-done | bytes 131104 | tf_op jit(solution)/shard_map/ppermute | solution.py:307
  19.9 0.0 copy-start.2
  19.9 0.0 copy-done.1
  19.9 0.6 copy-done.2
  20.5 1.8 %shard_map.83 = (f32[4,8,1024]{2,1,0:T(8,128)}, f32[4,8,1024]{2,1,0:T(8,128)}) custom-call(f32[4,8,1024]{2,1,0:T(8,128)} %get-tuple-element.17.cl_ref, f32[4,8,1024]{2,1,0:T(8,128)} %get-tuple-element.18.cr_ref, f32[4,8,1024]{2,1,0:T(8,128)} %copy-done.1, f32[4,8,1024]{2,1,0:T(8,128)} %copy-done.2), custom_call_target="tpu_custom_call" | custom-call | tf_op jit(solution)/shard_map/pallas_call | solution.py:167
  22.4 1.2 %collective-permute-start.2 = (f32[4,8,1024]{2,1,0:T(8,128)}, f32[4,8,1024]{2,1,0:T(8,128)S(1)}, u32[]{:S(2)}, u32[]{:S(2)}) collective-permute-start(f32[4,8,1024]{2,1,0:T(8,128)} %get-tuple-element.19), channel_id=1, source_target_pairs={{0,1},{1,2},{2,3},{3,0},{4,5},{5,6},{6,7},{7,4},{8,9},{9,10},{10,1... | collective-permute-start | bytes 393224 | tf_op jit(solution)/shard_map/ppermute | solution.py:307
  23.6 1.5 %collective-permute-start.3 = (f32[4,8,1024]{2,1,0:T(8,128)}, f32[4,8,1024]{2,1,0:T(8,128)S(1)}, u32[]{:S(2)}, u32[]{:S(2)}) collective-permute-start(f32[4,8,1024]{2,1,0:T(8,128)} %get-tuple-element.20), channel_id=1, source_target_pairs={{0,3},{1,0},{2,1},{3,2},{4,7},{5,4},{6,5},{7,6},{8,11},{9,8},{10,9... | collective-permute-start | bytes 393224 | tf_op jit(solution)/shard_map/ppermute | solution.py:307
  25.0 2.6 %collective-permute-done.2.lax_ref = f32[4,8,1024]{2,1,0:T(8,128)S(1)} collective-permute-done((f32[4,8,1024]{2,1,0:T(8,128)}, f32[4,8,1024]{2,1,0:T(8,128)S(1)}, u32[]{:S(2)}, u32[]{:S(2)}) %collective-permute-start.2) | collective-permute-done | bytes 131104 | tf_op jit(solution)/shard_map/ppermute | solution.py:307
  27.6 0.0 copy-start.3
  27.6 0.0 collective-permute-done.3.rax_ref
  27.6 0.0 copy-start.4
  27.6 0.7 copy-done.3
  28.3 0.0 copy-done.4
  28.3 7.9 %shard_map.84 = (bf16[32,32,1024]{2,1,0:T(8,128)(2,1)}, bf16[256,1024]{1,0:T(8,128)(2,1)}) custom-call(f32[4,4,8,8,1024]{4,3,2,1,0:T(8,128)} %get-tuple-element.14.w_ref, f32[4,8,1024]{2,1,0:T(8,128)} %copy-done.1, f32[4,8,1024]{2,1,0:T(8,128)} %copy-done.2, f32[4,8,1024]{2,1,0:T(8,128)} %copy-done.3, f32[4,8,1024]{2,1,0:T(8,128)} %copy-done.4, ...), custom_call_target="tpu_custom_call" | custom-call | tf_op jit(solution)/shard_map/pallas_call | solution.py:268
  36.2 1.6 %convolution_convert_fusion = bf16[128,4,1152]{2,0,1:T(8,128)(2,1)S(1)} fusion(bf16[256,128]{1,0:T(8,128)(2,1)S(1)} %broadcast_select_fusion, bf16[256,1024]{1,0:T(8,128)(2,1)} %get-tuple-element.22, s32[256]{0:T(256)S(1)} %multiply_add_fusion.1, s32[128,4]{0,1:T(4,128)S(1)} %multiply_add_fusion), kind=kOutput, calls=%fused_computation | convolution fusion | flops 303890432 | bytes 1772544 | tf_op jit(solution)/shard_map/dck,kf->dcf/dot_general | solution.py:345
  37.7 0.9 copy.23
  38.7 32.0 %all_to_all.10 = bf16[128,4,1152]{2,1,0:T(4,128)(2,1)S(1)} all-to-all(bf16[128,4,1152]{2,1,0:T(4,128)(2,1)S(1)} %copy.23), channel_id=1, replica_groups=mesh['elem'=32,'sub'=4] {'elem','sub'}, dimensions={0} | all-to-all | bytes 2359296 | tf_op jit(solution)/shard_map/all_to_all | solution.py:349
  70.6 0.3 reshape.143.arrived_ref
  70.9 0.0 copy-start
  70.9 0.1 add_reduce_fusion
  71.1 0.9 fusion.3.place_ref
  72.0 0.8 fusion.4.reply_ref
  72.9 0.0 copy-done
  72.9 5.8 %shard_map.85 = bf16[512,1024]{1,0:T(8,128)(2,1)} custom-call(s32[16]{0:T(128)} %cost_ref.1, bf16[256,512]{1,0:T(8,128)(2,1)} %fusion.3.place_ref, bf16[512,1152]{1,0:T(8,128)(2,1)} %copy-done, bf16[16,128,128]{2,1,0:T(8,128)(2,1)} %inv_ref.1, bf16[512,256]{1,0:T(8,128)(2,1)} %fusion.4.reply_ref), custom_call_target="tpu_custom_call" | custom-call | tf_op jit(solution)/shard_map/pallas_call | solution.py:219
  78.6 2.2 %reshape.144 = bf16[128,4,1024]{2,1,0:T(4,128)(2,1)} reshape(bf16[512,1024]{1,0:T(8,128)(2,1)} %shard_map.85) | data formatting | bytes 2097152 | tf_op jit(solution)/shard_map/reshape | solution.py:355
  80.9 3.6 %all-to-all-start.1 = ((bf16[128,4,1024]{2,1,0:T(4,128)(2,1)}), bf16[128,4,1024]{2,1,0:T(4,128)(2,1)S(1)}, u32[]{:S(2)}, u32[]{:S(2)}) async-start(bf16[128,4,1024]{2,1,0:T(4,128)(2,1)} %reshape.144), calls=%async_computation.1 | async-start | bytes 2097152 | tf_op jit(solution)/shard_map/all_to_all | solution.py:356
  84.4 0.1 reduce_sum.12
  84.5 0.2 copy.19
  84.7 0.2 copy.22
  84.9 0.1 eq.90
  85.0 19.3 %all-to-all-done.1 = bf16[128,4,1024]{2,1,0:T(4,128)(2,1)S(1)} async-done(((bf16[128,4,1024]{2,1,0:T(4,128)(2,1)}), bf16[128,4,1024]{2,1,0:T(4,128)(2,1)S(1)}, u32[]{:S(2)}, u32[]{:S(2)}) %all-to-all-start.1) | async-done | bytes 1048608 | tf_op jit(solution)/shard_map/all_to_all | solution.py:356
  104.3 0.3 reshape.145
  104.6 1.5 %fusion.2.tend_ref = f32[256,1024]{1,0:T(8,128)} fusion(bf16[512,1024]{1,0:T(8,128)(2,1)S(1)} %reshape.145, s32[256]{0:T(256)S(1)} %eq.90), kind=kOutput, calls=%fused_computation.7 | convolution fusion | flops 268566528 | bytes 2098176 | tf_op jit(solution)/shard_map/dot_general | solution.py:360
  106.0 3.1 %shard_map.86 = bf16[32,32,1024]{2,1,0:T(8,128)(2,1)} custom-call(bf16[32,32,1024]{2,1,0:T(8,128)(2,1)} %get-tuple-element.21.st_ref, f32[256,1024]{1,0:T(8,128)} %fusion.2.tend_ref), custom_call_target="tpu_custom_call" | custom-call | tf_op jit(solution)/shard_map/pallas_call | solution.py:295
  (5 shorter events, 0.1 us)
Async XLA Ops:
  2.7 12.6 %copy-start.5 = (s32[256]{0:T(256)S(1)}, s32[256]{0:T(256)}, u32[]{:S(2)}) copy-start(s32[256]{0:T(256)} %param.13) | copy-start | bytes 3076
  12.2 5.3 %collective-permute-start = (f32[4,8,1024]{2,1,0:T(8,128)}, f32[4,8,1024]{2,1,0:T(8,128)S(1)}, u32[]{:S(2)}, u32[]{:S(2)}) collective-permute-start(f32[4,8,1024]{2,1,0:T(8,128)} %get-tuple-element.15), channel_id=1, source_target_pairs={{0,4},{4,8},{8,12},{12,16},{16,20},{20,24},{24,28},{28,32},{32,36}... | collective-permute-start | bytes 393224 | tf_op jit(solution)/shard_map/ppermute | solution.py:307
  15.3 4.6 %collective-permute-start.1 = (f32[4,8,1024]{2,1,0:T(8,128)}, f32[4,8,1024]{2,1,0:T(8,128)S(1)}, u32[]{:S(2)}, u32[]{:S(2)}) collective-permute-start(f32[4,8,1024]{2,1,0:T(8,128)} %get-tuple-element.16), channel_id=1, source_target_pairs={{0,124},{4,0},{8,4},{12,8},{16,12},{20,16},{24,20},{28,24},{32,28}... | collective-permute-start | bytes 393224 | tf_op jit(solution)/shard_map/ppermute | solution.py:307
  17.5 2.3 %copy-start.1 = (f32[4,8,1024]{2,1,0:T(8,128)}, f32[4,8,1024]{2,1,0:T(8,128)S(1)}, u32[]{:S(2)}) copy-start(f32[4,8,1024]{2,1,0:T(8,128)S(1)} %collective-permute-done.top_ref) | copy-start | bytes 393220
  19.9 0.7 copy-start.2
  22.4 5.2 %collective-permute-start.2 = (f32[4,8,1024]{2,1,0:T(8,128)}, f32[4,8,1024]{2,1,0:T(8,128)S(1)}, u32[]{:S(2)}, u32[]{:S(2)}) collective-permute-start(f32[4,8,1024]{2,1,0:T(8,128)} %get-tuple-element.19), channel_id=1, source_target_pairs={{0,1},{1,2},{2,3},{3,0},{4,5},{5,6},{6,7},{7,4},{8,9},{9,10},{10,1... | collective-permute-start | bytes 393224 | tf_op jit(solution)/shard_map/ppermute | solution.py:307
  23.6 4.0 %collective-permute-start.3 = (f32[4,8,1024]{2,1,0:T(8,128)}, f32[4,8,1024]{2,1,0:T(8,128)S(1)}, u32[]{:S(2)}, u32[]{:S(2)}) collective-permute-start(f32[4,8,1024]{2,1,0:T(8,128)} %get-tuple-element.20), channel_id=1, source_target_pairs={{0,3},{1,0},{2,1},{3,2},{4,7},{5,4},{6,5},{7,6},{8,11},{9,8},{10,9... | collective-permute-start | bytes 393224 | tf_op jit(solution)/shard_map/ppermute | solution.py:307
  27.6 0.7 copy-start.3
  27.6 0.7 copy-start.4
  70.9 1.9 %copy-start = (bf16[512,1152]{1,0:T(8,128)(2,1)}, bf16[512,1152]{1,0:T(8,128)(2,1)S(1)}, u32[]{:S(2)}) copy-start(bf16[512,1152]{1,0:T(8,128)(2,1)S(1)} %reshape.143.arrived_ref) | copy-start | bytes 3538948
  80.9 23.4 %all-to-all-start.1 = ((bf16[128,4,1024]{2,1,0:T(4,128)(2,1)}), bf16[128,4,1024]{2,1,0:T(4,128)(2,1)S(1)}, u32[]{:S(2)}, u32[]{:S(2)}) async-start(bf16[128,4,1024]{2,1,0:T(4,128)(2,1)} %reshape.144), calls=%async_computation.1 | async-start | bytes 2097152 | tf_op jit(solution)/shard_map/all_to_all | solution.py:356

commit v6 on v3

--- a/solution.py
+++ b/solution.py
@@ -130,8 +130,9 @@
     st_ref[...] = ss_ref[...].astype(st_ref.dtype)
 
 
-def finish_kernel(st_ref, tend_ref, out_ref, t2_ref):
-    chunks = tend_ref.shape[1] // LANES
+def finish_kernel(st_ref, back_ref, ret_ref, out_ref, tend_ref, t2_ref):
+    chunks = ret_ref.shape[1] // LANES
+    tend_ref[...] = jnp.dot(back_ref[...], ret_ref[...], preferred_element_type=jnp.float32)
 
     def body(r2, carry):
         for h in range(chunks):
@@ -150,6 +151,26 @@
     lax.fori_loop(0, 16, body, 0)
 
 
+def edge_kernel(cl_ref, cr_ref, top_ref, bot_ref, lsend_ref, rsend_ref):
+    sub = lax.broadcasted_iota(jnp.int32, cl_ref.shape[1:], 0)
+    for side_ref, out_ref, b, j in ((cr_ref, lsend_ref, 7, 3), (cl_ref, rsend_ref, 0, 0)):
+        above = top_ref[j, pl.ds(b, 1), :]
+        below = bot_ref[j, pl.ds(b, 1), :]
+        first = side_ref[0] + jnp.where(sub == 0, above, pltpu.roll(side_ref[3], 1, 0))
+        last = side_ref[3] + jnp.where(sub == 7, below, pltpu.roll(side_ref[0], 7, 0))
+        out_ref[0] = first
+        out_ref[1] = side_ref[1]
+        out_ref[2] = side_ref[2]
+        out_ref[3] = last
+
+
+def run_edges(cl, cr, top, bot):
+    return pl.pallas_call(
+        edge_kernel,
+        out_shape=[jax.ShapeDtypeStruct(cl.shape, cl.dtype)] * 2,
+    )(cl, cr, top, bot)
+
+
 def spec(shape, lane_axis=None):
     nd = len(shape)
 
@@ -213,18 +234,25 @@
     )(w, top, bot, lax_halo, rax_halo, coef)
 
 
-def run_finish(settled, tend):
+def run_finish(settled, back_table, returned):
     rows, cols, features = settled.shape
     width = 4 * LANES
     nb = features // width
     return pl.pallas_call(
         finish_kernel,
         grid=(nb,),
-        in_specs=[spec((rows, cols, width), 2), spec((tend.shape[0], width), 1)],
+        in_specs=[
+            spec((rows, cols, width), 2),
+            spec(back_table.shape),
+            spec((returned.shape[0], width), 1),
+        ],
         out_specs=spec((rows, cols, width), 2),
         out_shape=jax.ShapeDtypeStruct(settled.shape, jnp.bfloat16),
-        scratch_shapes=[pltpu.VMEM((width // LANES, cols, LANES), jnp.float32)],
-    )(settled, tend)
+        scratch_shapes=[
+            pltpu.VMEM((back_table.shape[0], width), jnp.float32),
+            pltpu.VMEM((width // LANES, cols, LANES), jnp.float32),
+        ],
+    )(settled, back_table, returned)
 
 
 def shift(x, axis, step):
@@ -245,13 +273,9 @@
     top = shift(rb, "elem", 1)
     bot = shift(rt, "elem", -1)
 
-    def along_x(side, above, below):
-        first = side[0] + jnp.concatenate([above[None], side[3, :-1]], axis=0)
-        last = side[3] + jnp.concatenate([side[0, 1:], below[None]], axis=0)
-        return jnp.stack([first, side[1], side[2], last])
-
-    lax_halo = shift(along_x(cr, top[3, 7], bot[3, 7]), "sub", 1)
-    rax_halo = shift(along_x(cl, top[0, 0], bot[0, 0]), "sub", -1)
+    lsend, rsend = run_edges(cl, cr, top, bot)
+    lax_halo = shift(lsend, "sub", 1)
+    rax_halo = shift(rsend, "sub", -1)
     settled, columns = run_settle(w, top, bot, lax_halo, rax_halo, coef)
 
     column_count = columns.shape[0]
@@ -271,16 +295,17 @@
         jnp.arange(LANES)[None, :] == 0, (landing + 1)[:, None].astype(jnp.bfloat16), 0
     ).astype(jnp.bfloat16)
     payload = jnp.concatenate([columns, label_block], axis=1)
-    outgoing = jnp.dot(send_table, payload, preferred_element_type=jnp.float32).astype(jnp.bfloat16)
-    outgoing = outgoing.reshape(device_count, capacity, features + LANES)
+    outgoing = jnp.einsum(
+        "dck,kf->dcf", send_table.reshape(device_count, capacity, column_count), payload,
+        preferred_element_type=jnp.float32,
+    ).astype(jnp.bfloat16)
     arrived = lax.all_to_all(outgoing, ("elem", "sub"), split_axis=0, concat_axis=0, tiled=True)
     arrived = arrived.reshape(-1, features + LANES)
     arrived_labels = arrived[:, features].astype(jnp.int32) - 1
-    arrived = arrived[:, :features]
     place_table = (column_order[:, None] == arrived_labels[None, :]).astype(jnp.bfloat16)
-    slot_state = jnp.dot(place_table, arrived, preferred_element_type=jnp.float32).astype(
-        jnp.bfloat16
-    )
+    slot_state = jnp.dot(
+        place_table, arrived[:, :features], preferred_element_type=jnp.float32
+    ).astype(jnp.bfloat16)
     span_count = span_cost.shape[0]
     levels = diff_inverse.shape[1]
     start_state = slot_state.reshape(span_count, -1, levels)
@@ -306,8 +331,7 @@
     returned = returned.reshape(slot_total, features)
     dest_nat = dest_row.reshape(8, 2, 2, 8).transpose(0, 1, 3, 2).reshape(-1)
     back_table = (dest_nat[:, None] == slot_order[None, :]).astype(jnp.bfloat16)
-    tend_cols = jnp.dot(back_table, returned, preferred_element_type=jnp.float32)
-    return run_finish(settled, tend_cols)
+    return run_finish(settled, back_table, returned)
 
 
 def solution(mesh):

time: 109 us -> 110 us (level)
  starting transfers between devices: 19 us -> 22.4 us
  Pallas kernels: 20.5 us -> 23.2 us
  matrix products: 5.86 us -> 3.45 us
  loops' own time: 3.25 us -> 1.94 us
    slice x6 -> x0, local copies, waits for them, and re-layouts: 3.27 us -> none  [the longest x2 1.69 us: along_x(): return jnp.stack([first, side[1], side[2], last])]
    all_to_all x1, starting transfers between devices: 3.57 us -> 5.64 us  [on_device(): lax.all_to_all(replies, ('elem', 'sub'), split_axis=0, concat_axis=0, til...]
    convert_element_type x0 -> x1, local copies, waits for them, and re-layouts: none -> 1.93 us  [on_device(): outgoing = jnp.einsum('dck,kf->dcf', send_table.reshape(device_count, cap...]
    pallas_call x0 -> x1, Pallas kernels: none -> 1.82 us  [run_edges(): pl.pallas_call(edge_kernel, out_shape=[jax.ShapeDtypeStruct(cl.shape, cl....]
    dot_general x3 -> x2, matrix products: 3.48 us -> 2.03 us  [the longest x1 1.58 us: on_device(): jnp.einsum('dck,kf->dcf', send_table.reshape(device_count, capacity, colu...]
    another operation x1, loops' own time: 3.25 us -> 1.94 us  [on_device(): final_state = lax.fori_loop(0, jnp.max(span_cost), substep, start_state)]
    all_to_all x1, starting transfers between devices: 9.73 us -> 11 us  [on_device(): lax.all_to_all(outgoing, ('elem', 'sub'), split_axis=0, concat_axis=0, ti...]
    reshape x1 -> x0, local copies, waits for them, and re-layouts: 1.17 us -> none  [on_device(): outgoing = outgoing.reshape(device_count, capacity, features + LANES)]
  transfers between devices with their start and end apart: 6 -> 6, of which waited for: 5 -> 5; matrix products, arithmetic and copies ran while one was open for 5% -> 3% of each run, Pallas kernels for 0% -> 0%
where the time goes in v6:
time: 110 us; the launch traced here: 109 us
  waiting for transfers between devices  45.1 us (41%)
  Pallas kernels  23.2 us (21%)
  starting transfers between devices  22.4 us (20%)
  local copies, waits for them, and re-layouts  10.1 us (9%)
  matrix products  3.45 us (3%)
  other arithmetic  2.93 us (3%)
  loops' own time  1.94 us (2%)
    all_to_all x1, waiting for transfers between devices, on_device(): lax.all_to_all(outgoing, ('elem', 'sub'), split_axis=0, concat_axis=0, ti...  20.4 us
    all_to_all x1, waiting for transfers between devices, on_device(): lax.all_to_all(replies, ('elem', 'sub'), split_axis=0, concat_axis=0, til...  18.3 us
    all_to_all x1, starting transfers between devices, on_device(): lax.all_to_all(outgoing, ('elem', 'sub'), split_axis=0, concat_axis=0, ti...  11 us
    pallas_call x1, Pallas kernels, run_section(): pl.pallas_call(section_kernel, grid=(nb,), in_specs=[spec((rows, cols, LA...  9.48 us
    pallas_call x1, Pallas kernels, run_settle(): pl.pallas_call(settle_kernel, grid=(nb,), in_specs=[spec((4, 4, 8, 8, LAN...  7.86 us
    ppermute x4, waiting for transfers between devices, shift(): lax.ppermute(x, axis, [(k, (k + step) % count) for k in range(count)])  6.42 us
    ppermute x4, starting transfers between devices, shift(): lax.ppermute(x, axis, [(k, (k + step) % count) for k in range(count)])  5.76 us
    all_to_all x1, starting transfers between devices, on_device(): lax.all_to_all(replies, ('elem', 'sub'), split_axis=0, concat_axis=0, til...  5.64 us
  transfers between devices with their start and end apart: 6, of which 5 were waited for; matrix products, arithmetic and copies ran while one was open for 3% of the time, Pallas kernels for 0%

profile of v6, /device:TPU:1, one launch (start us, length us, event | category | flops | bytes accessed | tf_op | source)
XLA Modules:
  0.0 109.3 jit_solution(16326342209672356158)
XLA Ops:
  0.0 0.8 pad_maximum_fusion
  0.8 1.9 %broadcast_in_dim.27.coef_ref = f32[4,32,32,128]{3,2,1,0:T(8,128)} broadcast(f32[4,32,32]{2,1,0:T(8,128)S(1)} %pad_maximum_fusion), dimensions={0,1,2} | broadcast | bytes 2113536 | tf_op jit(solution)/shard_map/broadcast_in_dim | solution.py:267
  2.7 9.5 %shard_map.82 = (f32[4,4,8,8,1024]{4,3,2,1,0:T(8,128)}, f32[4,8,1024]{2,1,0:T(8,128)}, f32[4,8,1024]{2,1,0:T(8,128)}, f32[4,8,1024]{2,1,0:T(8,128)}, f32[4,8,1024]{2,1,0:T(8,128)}) custom-call(bf16[32,32,1024]{2,1,0:T(8,128)(2,1)} %q_ref.1, f32[4,32,32,128]{3,2,1,0:T(8,128)} %broadcast_in_dim.27.coef_ref), custom_call_target="tpu_custom_call" | custom-call | tf_op jit(solution)/shard_map/pallas_call | solution.py:186
  12.2 3.1 %collective-permute-start = (f32[4,8,1024]{2,1,0:T(8,128)}, f32[4,8,1024]{2,1,0:T(8,128)S(1)}, u32[]{:S(2)}, u32[]{:S(2)}) collective-permute-start(f32[4,8,1024]{2,1,0:T(8,128)} %get-tuple-element.43), channel_id=1, source_target_pairs={{0,4},{4,8},{8,12},{12,16},{16,20},{20,24},{24,28},{28,32},{32,36}... | collective-permute-start | bytes 393224 | tf_op jit(solution)/shard_map/ppermute | solution.py:260
  15.3 0.0 collective-permute-start.1
  15.3 0.1 reshape.150
  15.4 0.2 copy.19
  15.6 0.1 reshape.151
  15.7 0.1 broadcast_select_fusion
  15.8 0.2 convert_reduce_fusion
  16.0 1.5 %collective-permute-done.top_ref = f32[4,8,1024]{2,1,0:T(8,128)S(1)} collective-permute-done((f32[4,8,1024]{2,1,0:T(8,128)}, f32[4,8,1024]{2,1,0:T(8,128)S(1)}, u32[]{:S(2)}, u32[]{:S(2)}) %collective-permute-start) | collective-permute-done | bytes 131104 | tf_op jit(solution)/shard_map/ppermute | solution.py:260
  17.5 2.3 %collective-permute-done.1.bot_ref = f32[4,8,1024]{2,1,0:T(8,128)S(1)} collective-permute-done((f32[4,8,1024]{2,1,0:T(8,128)}, f32[4,8,1024]{2,1,0:T(8,128)S(1)}, u32[]{:S(2)}, u32[]{:S(2)}) %collective-permute-start.1) | collective-permute-done | bytes 131104 | tf_op jit(solution)/shard_map/ppermute | solution.py:260
  19.9 0.6 copy-done.2
  20.5 1.8 %shard_map.83 = (f32[4,8,1024]{2,1,0:T(8,128)}, f32[4,8,1024]{2,1,0:T(8,128)}) custom-call(f32[4,8,1024]{2,1,0:T(8,128)} %get-tuple-element.45.cl_ref, f32[4,8,1024]{2,1,0:T(8,128)} %get-tuple-element.46.cr_ref, f32[4,8,1024]{2,1,0:T(8,128)} %copy-done.1, f32[4,8,1024]{2,1,0:T(8,128)} %copy-done.2), custom_call_target="tpu_custom_call" | custom-call | tf_op jit(solution)/shard_map/pallas_call | solution.py:168
  22.4 1.2 %collective-permute-start.2 = (f32[4,8,1024]{2,1,0:T(8,128)}, f32[4,8,1024]{2,1,0:T(8,128)S(1)}, u32[]{:S(2)}, u32[]{:S(2)}) collective-permute-start(f32[4,8,1024]{2,1,0:T(8,128)} %get-tuple-element.47), channel_id=1, source_target_pairs={{0,1},{1,2},{2,3},{3,0},{4,5},{5,6},{6,7},{7,4},{8,9},{9,10},{10,1... | collective-permute-start | bytes 393224 | tf_op jit(solution)/shard_map/ppermute | solution.py:260
  23.6 1.5 %collective-permute-start.3 = (f32[4,8,1024]{2,1,0:T(8,128)}, f32[4,8,1024]{2,1,0:T(8,128)S(1)}, u32[]{:S(2)}, u32[]{:S(2)}) collective-permute-start(f32[4,8,1024]{2,1,0:T(8,128)} %get-tuple-element.48), channel_id=1, source_target_pairs={{0,3},{1,0},{2,1},{3,2},{4,7},{5,4},{6,5},{7,6},{8,11},{9,8},{10,9... | collective-permute-start | bytes 393224 | tf_op jit(solution)/shard_map/ppermute | solution.py:260
  25.0 2.6 %collective-permute-done.2.lax_ref = f32[4,8,1024]{2,1,0:T(8,128)S(1)} collective-permute-done((f32[4,8,1024]{2,1,0:T(8,128)}, f32[4,8,1024]{2,1,0:T(8,128)S(1)}, u32[]{:S(2)}, u32[]{:S(2)}) %collective-permute-start.2) | collective-permute-done | bytes 131104 | tf_op jit(solution)/shard_map/ppermute | solution.py:260
  27.6 0.0 collective-permute-done.3.rax_ref
  27.6 0.6 copy-done.3
  28.2 0.1 copy-done.4
  28.3 7.9 %shard_map.84 = (bf16[32,32,1024]{2,1,0:T(8,128)(2,1)}, bf16[256,1024]{1,0:T(8,128)(2,1)}) custom-call(f32[4,4,8,8,1024]{4,3,2,1,0:T(8,128)} %get-tuple-element.42.w_ref, f32[4,8,1024]{2,1,0:T(8,128)} %copy-done.1, f32[4,8,1024]{2,1,0:T(8,128)} %copy-done.2, f32[4,8,1024]{2,1,0:T(8,128)} %copy-done.3, f32[4,8,1024]{2,1,0:T(8,128)} %copy-done.4, ...), custom_call_target="tpu_custom_call" | custom-call | tf_op jit(solution)/shard_map/pallas_call | solution.py:214
  36.2 1.6 %convolution_convert_fusion.1 = bf16[128,4,1152]{2,0,1:T(8,128)(2,1)S(1)} fusion(bf16[256,128]{1,0:T(8,128)(2,1)S(1)} %broadcast_select_fusion, bf16[256,1024]{1,0:T(8,128)(2,1)} %get-tuple-element.50, s32[256]{0:T(256)S(1)} %multiply_add_fusion.1, s32[128,4]{0,1:T(4,128)S(1)} %multiply_add_fusion), kind=kOutput, calls=%fused_computation.3 | convolution fusion | flops 303890432 | bytes 1772544 | tf_op jit(solution)/shard_map/dck,kf->dcf/dot_general | solution.py:298
  37.8 1.9 %copy.22 = bf16[128,4,1152]{2,1,0:T(4,128)(2,1)} copy(bf16[128,4,1152]{2,0,1:T(8,128)(2,1)S(1)} %convolution_convert_fusion.1) | data formatting | bytes 2359296 | tf_op jit(solution)/shard_map/convert_element_type | solution.py:301
  39.7 11.0 %all-to-all-start = ((bf16[128,4,1152]{2,1,0:T(4,128)(2,1)}), bf16[128,4,1152]{2,1,0:T(4,128)(2,1)S(1)}, u32[]{:S(2)}, u32[]{:S(2)}) async-start(bf16[128,4,1152]{2,1,0:T(4,128)(2,1)} %copy.22), calls=%async_computation | async-start | bytes 2359296 | tf_op jit(solution)/shard_map/all_to_all | solution.py:302
  50.7 0.7 reduce_max.9
  51.4 20.4 %all-to-all-done = bf16[128,4,1152]{2,1,0:T(4,128)(2,1)S(1)} async-done(((bf16[128,4,1152]{2,1,0:T(4,128)(2,1)}), bf16[128,4,1152]{2,1,0:T(4,128)(2,1)S(1)}, u32[]{:S(2)}, u32[]{:S(2)}) %all-to-all-start) | async-done | bytes 1179680 | tf_op jit(solution)/shard_map/all_to_all | solution.py:302
  71.8 0.3 reshape.152
  72.1 0.1 add_reduce_fusion
  72.3 0.5 convolution_convert_fusion.3
  72.7 0.0 copy-start
  72.7 0.2 reshape.153
  73.0 0.8 copy-done
  73.8 3.0 %while.10 = (s32[]{:T(128)}, bf16[16,128,128]{2,1,0:T(8,128)(2,1)S(1)}, s32[]{:T(128)}, s32[16]{0:T(128)S(1)}, bf16[16,128,128]{2,1,0:T(8,128)(2,1)S(1)}, /*index=5*/s32[]{:T(128)}) while((s32[]{:T(128)}, bf16[16,128,128]{2,1,0:T(8,128)(2,1)S(1)}, s32[]{:T(128)}, s32[16]{0:T(128)S(1)}, bf16[16,128,128]{2,1,0:T(8,128)(2,1)S(1)}, ...), condition=%wide.region_3.4_spmd, body=%wide.region_2.3_spmd.sunk | while | flops 67633168 | bytes 2621609 | solution.py:319
  74.5 0.5 fusion.28
  75.7 0.5 fusion.28
  76.8 0.1 subtract_convert_fusion
  76.9 0.2 reshape.154
  77.1 0.5 convolution_convert_fusion.2
  77.6 1.2 %reshape.155 = bf16[128,4,1024]{2,1,0:T(4,128)(2,1)} reshape(bf16[512,1024]{1,0:T(8,128)(2,1)S(1)} %convolution_convert_fusion.2) | data formatting | bytes 2097152 | tf_op jit(solution)/shard_map/reshape | solution.py:329
  78.8 5.6 %all-to-all-start.1 = ((bf16[128,4,1024]{2,1,0:T(4,128)(2,1)}), bf16[128,4,1024]{2,1,0:T(4,128)(2,1)S(1)}, u32[]{:S(2)}, u32[]{:S(2)}) async-start(bf16[128,4,1024]{2,1,0:T(4,128)(2,1)} %reshape.155), calls=%async_computation.1 | async-start | bytes 2097152 | tf_op jit(solution)/shard_map/all_to_all | solution.py:330
  84.5 0.1 reduce_sum.12
  84.6 0.2 copy.18
  84.8 0.2 copy.21
  84.9 0.1 eq.92
  85.1 0.8 fusion.4.back_ref
  85.9 18.3 %all-to-all-done.1 = bf16[128,4,1024]{2,1,0:T(4,128)(2,1)S(1)} async-done(((bf16[128,4,1024]{2,1,0:T(4,128)(2,1)}), bf16[128,4,1024]{2,1,0:T(4,128)(2,1)S(1)}, u32[]{:S(2)}, u32[]{:S(2)}) %all-to-all-start.1) | async-done | bytes 1048608 | tf_op jit(solution)/shard_map/all_to_all | solution.py:330
  104.2 1.1 reshape.156.ret_ref
  105.3 4.0 %shard_map.85 = bf16[32,32,1024]{2,1,0:T(8,128)(2,1)} custom-call(bf16[32,32,1024]{2,1,0:T(8,128)(2,1)} %get-tuple-element.49.st_ref, bf16[256,512]{1,0:T(8,128)(2,1)} %fusion.4.back_ref, bf16[512,1024]{1,0:T(8,128)(2,1)} %reshape.156.ret_ref), custom_call_target="tpu_custom_call" | custom-call | tf_op jit(solution)/shard_map/pallas_call | solution.py:241
  (19 shorter events, 0.2 us)
Async XLA Ops:
  2.7 12.6 %copy-start.5 = (s32[256]{0:T(256)S(1)}, s32[256]{0:T(256)}, u32[]{:S(2)}) copy-start(s32[256]{0:T(256)} %param.15) | copy-start | bytes 3076
  12.2 5.3 %collective-permute-start = (f32[4,8,1024]{2,1,0:T(8,128)}, f32[4,8,1024]{2,1,0:T(8,128)S(1)}, u32[]{:S(2)}, u32[]{:S(2)}) collective-permute-start(f32[4,8,1024]{2,1,0:T(8,128)} %get-tuple-element.43), channel_id=1, source_target_pairs={{0,4},{4,8},{8,12},{12,16},{16,20},{20,24},{24,28},{28,32},{32,36}... | collective-permute-start | bytes 393224 | tf_op jit(solution)/shard_map/ppermute | solution.py:260
  15.3 4.6 %collective-permute-start.1 = (f32[4,8,1024]{2,1,0:T(8,128)}, f32[4,8,1024]{2,1,0:T(8,128)S(1)}, u32[]{:S(2)}, u32[]{:S(2)}) collective-permute-start(f32[4,8,1024]{2,1,0:T(8,128)} %get-tuple-element.44), channel_id=1, source_target_pairs={{0,124},{4,0},{8,4},{12,8},{16,12},{20,16},{24,20},{28,24},{32,28}... | collective-permute-start | bytes 393224 | tf_op jit(solution)/shard_map/ppermute | solution.py:260
  17.5 2.3 %copy-start.1 = (f32[4,8,1024]{2,1,0:T(8,128)}, f32[4,8,1024]{2,1,0:T(8,128)S(1)}, u32[]{:S(2)}) copy-start(f32[4,8,1024]{2,1,0:T(8,128)S(1)} %collective-permute-done.top_ref) | copy-start | bytes 393220
  19.9 0.6 copy-start.2
  22.4 5.2 %collective-permute-start.2 = (f32[4,8,1024]{2,1,0:T(8,128)}, f32[4,8,1024]{2,1,0:T(8,128)S(1)}, u32[]{:S(2)}, u32[]{:S(2)}) collective-permute-start(f32[4,8,1024]{2,1,0:T(8,128)} %get-tuple-element.47), channel_id=1, source_target_pairs={{0,1},{1,2},{2,3},{3,0},{4,5},{5,6},{6,7},{7,4},{8,9},{9,10},{10,1... | collective-permute-start | bytes 393224 | tf_op jit(solution)/shard_map/ppermute | solution.py:260
  23.6 4.0 %collective-permute-start.3 = (f32[4,8,1024]{2,1,0:T(8,128)}, f32[4,8,1024]{2,1,0:T(8,128)S(1)}, u32[]{:S(2)}, u32[]{:S(2)}) collective-permute-start(f32[4,8,1024]{2,1,0:T(8,128)} %get-tuple-element.48), channel_id=1, source_target_pairs={{0,3},{1,0},{2,1},{3,2},{4,7},{5,4},{6,5},{7,6},{8,11},{9,8},{10,9... | collective-permute-start | bytes 393224 | tf_op jit(solution)/shard_map/ppermute | solution.py:260
  27.6 0.7 copy-start.3
  27.6 0.7 copy-start.4
  39.7 11.0 %copy-start.6 = (s32[16]{0:T(128)S(1)}, s32[16]{0:T(128)}, u32[]{:S(2)}) copy-start(s32[16]{0:T(128)} %param.17) | copy-start | bytes 196
  39.7 32.1 %all-to-all-start = ((bf16[128,4,1152]{2,1,0:T(4,128)(2,1)}), bf16[128,4,1152]{2,1,0:T(4,128)(2,1)S(1)}, u32[]{:S(2)}, u32[]{:S(2)}) async-start(bf16[128,4,1152]{2,1,0:T(4,128)(2,1)} %copy.22), calls=%async_computation | async-start | bytes 2359296 | tf_op jit(solution)/shard_map/all_to_all | solution.py:302
  72.7 1.0 copy-start
  78.8 25.4 %all-to-all-start.1 = ((bf16[128,4,1024]{2,1,0:T(4,128)(2,1)}), bf16[128,4,1024]{2,1,0:T(4,128)(2,1)S(1)}, u32[]{:S(2)}, u32[]{:S(2)}) async-start(bf16[128,4,1024]{2,1,0:T(4,128)(2,1)} %reshape.155), calls=%async_computation.1 | async-start | bytes 2097152 | tf_op jit(solution)/shard_map/all_to_all | solution.py:330

commit v7 on v6

--- a/solution.py
+++ b/solution.py
@@ -45,16 +45,28 @@
     return total
 
 
-def section_kernel(q_ref, coef_ref, w_ref, rt_ref, rb_ref, cl_ref, cr_ref, s_ref):
+def split_coefficients(coef_ref, cs_ref):
+    @pl.when(pl.program_id(0) == 0)
+    def _():
+        def fill(a, carry):
+            for kind in range(cs_ref.shape[0]):
+                for i in range(4):
+                    for j in range(4):
+                        cs_ref[kind, i, j, a] = coef_ref[kind, 4 * a + i, pl.ds(j, 8, stride=4), :]
+            return carry
+
+        lax.fori_loop(0, 8, fill, 0)
+
+
+def section_kernel(q_ref, coef_ref, w_ref, rt_ref, rb_ref, cl_ref, cr_ref, s_ref, cs_ref):
+    split_coefficients(coef_ref, cs_ref)
     s_ref[...] = q_ref[...].astype(jnp.float32)
     d = DERIV
 
     def body(a, carry):
         q = [[s_ref[4 * a + i, pl.ds(j, 8, stride=4), :] for j in range(4)] for i in range(4)]
         mx, my, mw = (
-            [[coef_ref[kind, 4 * a + i, pl.ds(j, 8, stride=4), :] for j in range(4)]
-             for i in range(4)]
-            for kind in range(3)
+            [[cs_ref[kind, i, j, a] for j in range(4)] for i in range(4)] for kind in range(3)
         )
         tx = [
             [mx[k][j] * mix(d[k], [q[m][j] for m in range(4)]) for j in range(4)]
@@ -81,13 +93,16 @@
             cr_ref[i, pl.ds(a, 1), :] = w_ref[i, 3, a, pl.ds(7, 1), :]
 
 
-def settle_kernel(w_ref, top_ref, bot_ref, lax_ref, rax_ref, coef_ref, st_ref, col_ref, ss_ref):
+def settle_kernel(
+    w_ref, top_ref, bot_ref, lax_ref, rax_ref, coef_ref, st_ref, col_ref, ss_ref, cs_ref
+):
+    split_coefficients(coef_ref, cs_ref)
     sub = lax.broadcasted_iota(jnp.int32, (8, LANES), 0)
 
     def body(a, carry):
         x = [[w_ref[i, j, a] for j in range(4)] for i in range(4)]
-        mw = [[coef_ref[0, 4 * a + i, pl.ds(j, 8, stride=4), :] for j in range(4)] for i in range(4)]
-        mi = [[coef_ref[1, 4 * a + i, pl.ds(j, 8, stride=4), :] for j in range(4)] for i in range(4)]
+        mw = [[cs_ref[0, i, j, a] for j in range(4)] for i in range(4)]
+        mi = [[cs_ref[1, i, j, a] for j in range(4)] for i in range(4)]
         up = [
             jnp.where(a == 0, top_ref[j], w_ref[3, j, jnp.maximum(a - 1, 0)]) for j in range(4)
         ]
@@ -204,7 +219,11 @@
             jax.ShapeDtypeStruct((4, 8, features), jnp.float32),
             jax.ShapeDtypeStruct((4, 8, features), jnp.float32),
         ],
-        scratch_shapes=[pltpu.VMEM((rows, cols, LANES), jnp.float32)],
+        scratch_shapes=[
+            pltpu.VMEM((rows, cols, LANES), jnp.float32),
+            pltpu.VMEM((3, 4, 4, 8, 8, LANES), jnp.float32),
+        ],
+        compiler_params=pltpu.CompilerParams(dimension_semantics=("arbitrary",)),
     )(tracers, coef)
 
 
@@ -230,7 +249,11 @@
             jax.ShapeDtypeStruct((32, 32, features), jnp.bfloat16),
             jax.ShapeDtypeStruct((256, features), jnp.bfloat16),
         ],
-        scratch_shapes=[pltpu.VMEM((32, 32, LANES), jnp.float32)],
+        scratch_shapes=[
+            pltpu.VMEM((32, 32, LANES), jnp.float32),
+            pltpu.VMEM((2, 4, 4, 8, 8, LANES), jnp.float32),
+        ],
+        compiler_params=pltpu.CompilerParams(dimension_semantics=("arbitrary",)),
     )(w, top, bot, lax_halo, rax_halo, coef)
 
 

time: 110 us -> 111 us (level)
  no operation moved by 1% of the time
where the time goes in v7:
time: 111 us; the launch traced here: 110 us
  waiting for transfers between devices  45.1 us (41%)
  Pallas kernels  23.7 us (21%)
  starting transfers between devices  23.5 us (21%)
  local copies, waits for them, and re-layouts  10.1 us (9%)
  matrix products  2.98 us (3%)
  other arithmetic  2.93 us (3%)
  loops' own time  1.28 us (1%)
    all_to_all x1, waiting for transfers between devices, on_device(): lax.all_to_all(outgoing, ('elem', 'sub'), split_axis=0, concat_axis=0, ti...  20.4 us
    all_to_all x1, waiting for transfers between devices, on_device(): lax.all_to_all(replies, ('elem', 'sub'), split_axis=0, concat_axis=0, til...  18.3 us
    all_to_all x1, starting transfers between devices, on_device(): lax.all_to_all(outgoing, ('elem', 'sub'), split_axis=0, concat_axis=0, ti...  11 us
    pallas_call x1, Pallas kernels, run_section(): pl.pallas_call(section_kernel, grid=(nb,), in_specs=[spec((rows, cols, LA...  9.7 us
    pallas_call x1, Pallas kernels, run_settle(): pl.pallas_call(settle_kernel, grid=(nb,), in_specs=[spec((4, 4, 8, 8, LAN...  8.12 us
    all_to_all x1, starting transfers between devices, on_device(): lax.all_to_all(replies, ('elem', 'sub'), split_axis=0, concat_axis=0, til...  6.69 us
    ppermute x4, waiting for transfers between devices, shift(): lax.ppermute(x, axis, [(k, (k + step) % count) for k in range(count)])  6.42 us
    ppermute x4, starting transfers between devices, shift(): lax.ppermute(x, axis, [(k, (k + step) % count) for k in range(count)])  5.76 us
  transfers between devices with their start and end apart: 6, of which 5 were waited for; matrix products, arithmetic and copies ran while one was open for 3% of the time, Pallas kernels for 0%

profile of v7, /device:TPU:1, one launch (start us, length us, event | category | flops | bytes accessed | tf_op | source)
XLA Modules:
  0.0 109.7 jit_solution(2865176135908659719)
XLA Ops:
  0.0 0.8 pad_maximum_fusion
  0.8 1.9 %broadcast_in_dim.27.coef_ref = f32[4,32,32,128]{3,2,1,0:T(8,128)} broadcast(f32[4,32,32]{2,1,0:T(8,128)S(1)} %pad_maximum_fusion), dimensions={0,1,2} | broadcast | bytes 2113536 | tf_op jit(solution)/shard_map/broadcast_in_dim | solution.py:290
  2.7 9.7 %shard_map.82 = (f32[4,4,8,8,1024]{4,3,2,1,0:T(8,128)}, f32[4,8,1024]{2,1,0:T(8,128)}, f32[4,8,1024]{2,1,0:T(8,128)}, f32[4,8,1024]{2,1,0:T(8,128)}, f32[4,8,1024]{2,1,0:T(8,128)}) custom-call(bf16[32,32,1024]{2,1,0:T(8,128)(2,1)} %q_ref.1, f32[4,32,32,128]{3,2,1,0:T(8,128)} %broadcast_in_dim.27.coef_ref), custom_call_target="tpu_custom_call" | custom-call | tf_op jit(solution)/shard_map/pallas_call | solution.py:201
  12.4 3.1 %collective-permute-start = (f32[4,8,1024]{2,1,0:T(8,128)}, f32[4,8,1024]{2,1,0:T(8,128)S(1)}, u32[]{:S(2)}, u32[]{:S(2)}) collective-permute-start(f32[4,8,1024]{2,1,0:T(8,128)} %get-tuple-element.43), channel_id=1, source_target_pairs={{0,4},{4,8},{8,12},{12,16},{16,20},{20,24},{24,28},{28,32},{32,36}... | collective-permute-start | bytes 393224 | tf_op jit(solution)/shard_map/ppermute | solution.py:283
  15.5 0.0 collective-permute-start.1
  15.5 0.0 copy-done.5
  15.5 0.1 reshape.150
  15.6 0.2 copy.19
  15.8 0.1 reshape.151
  15.9 0.1 broadcast_select_fusion
  16.0 0.2 convert_reduce_fusion
  16.2 1.5 %collective-permute-done.top_ref = f32[4,8,1024]{2,1,0:T(8,128)S(1)} collective-permute-done((f32[4,8,1024]{2,1,0:T(8,128)}, f32[4,8,1024]{2,1,0:T(8,128)S(1)}, u32[]{:S(2)}, u32[]{:S(2)}) %collective-permute-start) | collective-permute-done | bytes 131104 | tf_op jit(solution)/shard_map/ppermute | solution.py:283
  17.8 2.3 %collective-permute-done.1.bot_ref = f32[4,8,1024]{2,1,0:T(8,128)S(1)} collective-permute-done((f32[4,8,1024]{2,1,0:T(8,128)}, f32[4,8,1024]{2,1,0:T(8,128)S(1)}, u32[]{:S(2)}, u32[]{:S(2)}) %collective-permute-start.1) | collective-permute-done | bytes 131104 | tf_op jit(solution)/shard_map/ppermute | solution.py:283
  20.1 0.6 copy-done.2
  20.7 1.8 %shard_map.83 = (f32[4,8,1024]{2,1,0:T(8,128)}, f32[4,8,1024]{2,1,0:T(8,128)}) custom-call(f32[4,8,1024]{2,1,0:T(8,128)} %get-tuple-element.45.cl_ref, f32[4,8,1024]{2,1,0:T(8,128)} %get-tuple-element.46.cr_ref, f32[4,8,1024]{2,1,0:T(8,128)} %copy-done.1, f32[4,8,1024]{2,1,0:T(8,128)} %copy-done.2), custom_call_target="tpu_custom_call" | custom-call | tf_op jit(solution)/shard_map/pallas_call | solution.py:183
  22.6 1.2 %collective-permute-start.2 = (f32[4,8,1024]{2,1,0:T(8,128)}, f32[4,8,1024]{2,1,0:T(8,128)S(1)}, u32[]{:S(2)}, u32[]{:S(2)}) collective-permute-start(f32[4,8,1024]{2,1,0:T(8,128)} %get-tuple-element.47), channel_id=1, source_target_pairs={{0,1},{1,2},{2,3},{3,0},{4,5},{5,6},{6,7},{7,4},{8,9},{9,10},{10,1... | collective-permute-start | bytes 393224 | tf_op jit(solution)/shard_map/ppermute | solution.py:283
  23.8 1.5 %collective-permute-start.3 = (f32[4,8,1024]{2,1,0:T(8,128)}, f32[4,8,1024]{2,1,0:T(8,128)S(1)}, u32[]{:S(2)}, u32[]{:S(2)}) collective-permute-start(f32[4,8,1024]{2,1,0:T(8,128)} %get-tuple-element.48), channel_id=1, source_target_pairs={{0,3},{1,0},{2,1},{3,2},{4,7},{5,4},{6,5},{7,6},{8,11},{9,8},{10,9... | collective-permute-start | bytes 393224 | tf_op jit(solution)/shard_map/ppermute | solution.py:283
  25.3 2.6 %collective-permute-done.2.lax_ref = f32[4,8,1024]{2,1,0:T(8,128)S(1)} collective-permute-done((f32[4,8,1024]{2,1,0:T(8,128)}, f32[4,8,1024]{2,1,0:T(8,128)S(1)}, u32[]{:S(2)}, u32[]{:S(2)}) %collective-permute-start.2) | collective-permute-done | bytes 131104 | tf_op jit(solution)/shard_map/ppermute | solution.py:283
  27.8 0.0 collective-permute-done.3.rax_ref
  27.8 0.6 copy-done.3
  28.5 0.1 copy-done.4
  28.5 8.1 %shard_map.84 = (bf16[32,32,1024]{2,1,0:T(8,128)(2,1)}, bf16[256,1024]{1,0:T(8,128)(2,1)}) custom-call(f32[4,4,8,8,1024]{4,3,2,1,0:T(8,128)} %get-tuple-element.42.w_ref, f32[4,8,1024]{2,1,0:T(8,128)} %copy-done.1, f32[4,8,1024]{2,1,0:T(8,128)} %copy-done.2, f32[4,8,1024]{2,1,0:T(8,128)} %copy-done.3, f32[4,8,1024]{2,1,0:T(8,128)} %copy-done.4, ...), custom_call_target="tpu_custom_call" | custom-call | tf_op jit(solution)/shard_map/pallas_call | solution.py:233
  36.6 1.6 %convolution_convert_fusion.1 = bf16[128,4,1152]{2,0,1:T(8,128)(2,1)S(1)} fusion(bf16[256,128]{1,0:T(8,128)(2,1)S(1)} %broadcast_select_fusion, bf16[256,1024]{1,0:T(8,128)(2,1)} %get-tuple-element.50, s32[256]{0:T(256)S(1)} %multiply_add_fusion.1, s32[128,4]{0,1:T(4,128)S(1)} %multiply_add_fusion), kind=kOutput, calls=%fused_computation.3 | convolution fusion | flops 303890432 | bytes 1772544 | tf_op jit(solution)/shard_map/dck,kf->dcf/dot_general | solution.py:321
  38.2 1.9 %copy.22 = bf16[128,4,1152]{2,1,0:T(4,128)(2,1)} copy(bf16[128,4,1152]{2,0,1:T(8,128)(2,1)S(1)} %convolution_convert_fusion.1) | data formatting | bytes 2359296 | tf_op jit(solution)/shard_map/convert_element_type | solution.py:324
  40.2 11.0 %all-to-all-start = ((bf16[128,4,1152]{2,1,0:T(4,128)(2,1)}), bf16[128,4,1152]{2,1,0:T(4,128)(2,1)S(1)}, u32[]{:S(2)}, u32[]{:S(2)}) async-start(bf16[128,4,1152]{2,1,0:T(4,128)(2,1)} %copy.22), calls=%async_computation | async-start | bytes 2359296 | tf_op jit(solution)/shard_map/all_to_all | solution.py:325
  51.2 0.7 reduce_max.9
  51.9 20.4 %all-to-all-done = bf16[128,4,1152]{2,1,0:T(4,128)(2,1)S(1)} async-done(((bf16[128,4,1152]{2,1,0:T(4,128)(2,1)}), bf16[128,4,1152]{2,1,0:T(4,128)(2,1)S(1)}, u32[]{:S(2)}, u32[]{:S(2)}) %all-to-all-start) | async-done | bytes 1179680 | tf_op jit(solution)/shard_map/all_to_all | solution.py:325
  72.3 0.3 reshape.152
  72.6 0.1 add_reduce_fusion
  72.7 0.5 convolution_convert_fusion.3
  73.2 0.0 copy-start
  73.2 0.2 reshape.153
  73.5 0.8 copy-done
  74.3 1.8 %while.10 = (s32[]{:T(128)}, bf16[16,128,128]{2,1,0:T(8,128)(2,1)S(1)}, s32[]{:T(128)}, s32[16]{0:T(128)S(1)}, bf16[16,128,128]{2,1,0:T(8,128)(2,1)S(1)}, /*index=5*/s32[]{:T(128)}) while((s32[]{:T(128)}, bf16[16,128,128]{2,1,0:T(8,128)(2,1)S(1)}, s32[]{:T(128)}, s32[16]{0:T(128)S(1)}, bf16[16,128,128]{2,1,0:T(8,128)(2,1)S(1)}, ...), condition=%wide.region_3.4_spmd, body=%wide.region_2.3_spmd.sunk | while | flops 67633168 | bytes 2621609 | solution.py:342
  74.9 0.5 fusion.28
  76.1 0.1 subtract_convert_fusion
  76.2 0.2 reshape.154
  76.4 0.5 convolution_convert_fusion.2
  76.9 1.2 %reshape.155 = bf16[128,4,1024]{2,1,0:T(4,128)(2,1)} reshape(bf16[512,1024]{1,0:T(8,128)(2,1)S(1)} %convolution_convert_fusion.2) | data formatting | bytes 2097152 | tf_op jit(solution)/shard_map/reshape | solution.py:352
  78.1 6.7 %all-to-all-start.1 = ((bf16[128,4,1024]{2,1,0:T(4,128)(2,1)}), bf16[128,4,1024]{2,1,0:T(4,128)(2,1)S(1)}, u32[]{:S(2)}, u32[]{:S(2)}) async-start(bf16[128,4,1024]{2,1,0:T(4,128)(2,1)} %reshape.155), calls=%async_computation.1 | async-start | bytes 2097152 | tf_op jit(solution)/shard_map/all_to_all | solution.py:353
  84.8 0.1 reduce_sum.12
  84.9 0.2 copy.18
  85.1 0.2 copy.21
  85.3 0.1 eq.92
  85.4 0.8 fusion.4.back_ref
  86.3 18.3 %all-to-all-done.1 = bf16[128,4,1024]{2,1,0:T(4,128)(2,1)S(1)} async-done(((bf16[128,4,1024]{2,1,0:T(4,128)(2,1)}), bf16[128,4,1024]{2,1,0:T(4,128)(2,1)S(1)}, u32[]{:S(2)}, u32[]{:S(2)}) %all-to-all-start.1) | async-done | bytes 1048608 | tf_op jit(solution)/shard_map/all_to_all | solution.py:353
  104.6 1.1 reshape.156.ret_ref
  105.7 4.0 %shard_map.85 = bf16[32,32,1024]{2,1,0:T(8,128)(2,1)} custom-call(bf16[32,32,1024]{2,1,0:T(8,128)(2,1)} %get-tuple-element.49.st_ref, bf16[256,512]{1,0:T(8,128)(2,1)} %fusion.4.back_ref, bf16[512,1024]{1,0:T(8,128)(2,1)} %reshape.156.ret_ref), custom_call_target="tpu_custom_call" | custom-call | tf_op jit(solution)/shard_map/pallas_call | solution.py:264
  (16 shorter events, 0.2 us)
Async XLA Ops:
  2.7 12.8 %copy-start.5 = (s32[256]{0:T(256)S(1)}, s32[256]{0:T(256)}, u32[]{:S(2)}) copy-start(s32[256]{0:T(256)} %param.15) | copy-start | bytes 3076
  12.4 5.3 %collective-permute-start = (f32[4,8,1024]{2,1,0:T(8,128)}, f32[4,8,1024]{2,1,0:T(8,128)S(1)}, u32[]{:S(2)}, u32[]{:S(2)}) collective-permute-start(f32[4,8,1024]{2,1,0:T(8,128)} %get-tuple-element.43), channel_id=1, source_target_pairs={{0,4},{4,8},{8,12},{12,16},{16,20},{20,24},{24,28},{28,32},{32,36}... | collective-permute-start | bytes 393224 | tf_op jit(solution)/shard_map/ppermute | solution.py:283
  15.5 4.6 %collective-permute-start.1 = (f32[4,8,1024]{2,1,0:T(8,128)}, f32[4,8,1024]{2,1,0:T(8,128)S(1)}, u32[]{:S(2)}, u32[]{:S(2)}) collective-permute-start(f32[4,8,1024]{2,1,0:T(8,128)} %get-tuple-element.44), channel_id=1, source_target_pairs={{0,124},{4,0},{8,4},{12,8},{16,12},{20,16},{24,20},{28,24},{32,28}... | collective-permute-start | bytes 393224 | tf_op jit(solution)/shard_map/ppermute | solution.py:283
  17.8 2.3 %copy-start.1 = (f32[4,8,1024]{2,1,0:T(8,128)}, f32[4,8,1024]{2,1,0:T(8,128)S(1)}, u32[]{:S(2)}) copy-start(f32[4,8,1024]{2,1,0:T(8,128)S(1)} %collective-permute-done.top_ref) | copy-start | bytes 393220
  20.1 0.6 copy-start.2
  22.6 5.2 %collective-permute-start.2 = (f32[4,8,1024]{2,1,0:T(8,128)}, f32[4,8,1024]{2,1,0:T(8,128)S(1)}, u32[]{:S(2)}, u32[]{:S(2)}) collective-permute-start(f32[4,8,1024]{2,1,0:T(8,128)} %get-tuple-element.47), channel_id=1, source_target_pairs={{0,1},{1,2},{2,3},{3,0},{4,5},{5,6},{6,7},{7,4},{8,9},{9,10},{10,1... | collective-permute-start | bytes 393224 | tf_op jit(solution)/shard_map/ppermute | solution.py:283
  23.8 4.0 %collective-permute-start.3 = (f32[4,8,1024]{2,1,0:T(8,128)}, f32[4,8,1024]{2,1,0:T(8,128)S(1)}, u32[]{:S(2)}, u32[]{:S(2)}) collective-permute-start(f32[4,8,1024]{2,1,0:T(8,128)} %get-tuple-element.48), channel_id=1, source_target_pairs={{0,3},{1,0},{2,1},{3,2},{4,7},{5,4},{6,5},{7,6},{8,11},{9,8},{10,9... | collective-permute-start | bytes 393224 | tf_op jit(solution)/shard_map/ppermute | solution.py:283
  27.8 0.7 copy-start.3
  27.8 0.7 copy-start.4
  40.2 11.0 %copy-start.6 = (s32[16]{0:T(128)S(1)}, s32[16]{0:T(128)}, u32[]{:S(2)}) copy-start(s32[16]{0:T(128)} %param.17) | copy-start | bytes 196
  40.2 32.1 %all-to-all-start = ((bf16[128,4,1152]{2,1,0:T(4,128)(2,1)}), bf16[128,4,1152]{2,1,0:T(4,128)(2,1)S(1)}, u32[]{:S(2)}, u32[]{:S(2)}) async-start(bf16[128,4,1152]{2,1,0:T(4,128)(2,1)} %copy.22), calls=%async_computation | async-start | bytes 2359296 | tf_op jit(solution)/shard_map/all_to_all | solution.py:325
  73.2 1.0 copy-start
  78.1 26.4 %all-to-all-start.1 = ((bf16[128,4,1024]{2,1,0:T(4,128)(2,1)}), bf16[128,4,1024]{2,1,0:T(4,128)(2,1)S(1)}, u32[]{:S(2)}, u32[]{:S(2)}) async-start(bf16[128,4,1024]{2,1,0:T(4,128)(2,1)} %reshape.155), calls=%async_computation.1 | async-start | bytes 2097152 | tf_op jit(solution)/shard_map/all_to_all | solution.py:353

commit v8 on v7

--- a/solution.py
+++ b/solution.py
@@ -45,6 +45,14 @@
     return total
 
 
+def interleave_matrix(dtype, inverse=False):
+    c = lax.broadcasted_iota(jnp.int32, (32, 32), 0)
+    k = lax.broadcasted_iota(jnp.int32, (32, 32), 1)
+    if inverse:
+        c, k = k, c
+    return (k == (c % 4) * 8 + c // 4).astype(dtype)
+
+
 def split_coefficients(coef_ref, cs_ref):
     @pl.when(pl.program_id(0) == 0)
     def _():
@@ -58,13 +66,16 @@
         lax.fori_loop(0, 8, fill, 0)
 
 
-def section_kernel(q_ref, coef_ref, w_ref, rt_ref, rb_ref, cl_ref, cr_ref, s_ref, cs_ref):
+def section_kernel(q_ref, coef_ref, w_ref, rt_ref, rb_ref, cl_ref, cr_ref, cs_ref):
     split_coefficients(coef_ref, cs_ref)
-    s_ref[...] = q_ref[...].astype(jnp.float32)
     d = DERIV
+    split = interleave_matrix(q_ref.dtype, inverse=True)
 
     def body(a, carry):
-        q = [[s_ref[4 * a + i, pl.ds(j, 8, stride=4), :] for j in range(4)] for i in range(4)]
+        q = []
+        for i in range(4):
+            rows = jnp.dot(split, q_ref[4 * a + i], preferred_element_type=jnp.float32)
+            q.append([rows[8 * j:8 * (j + 1)] for j in range(4)])
         mx, my, mw = (
             [[cs_ref[kind, i, j, a] for j in range(4)] for i in range(4)] for kind in range(3)
         )
@@ -93,11 +104,10 @@
             cr_ref[i, pl.ds(a, 1), :] = w_ref[i, 3, a, pl.ds(7, 1), :]
 
 
-def settle_kernel(
-    w_ref, top_ref, bot_ref, lax_ref, rax_ref, coef_ref, st_ref, col_ref, ss_ref, cs_ref
-):
+def settle_kernel(w_ref, top_ref, bot_ref, lax_ref, rax_ref, coef_ref, st_ref, col_ref, cs_ref):
     split_coefficients(coef_ref, cs_ref)
     sub = lax.broadcasted_iota(jnp.int32, (8, LANES), 0)
+    merge = interleave_matrix(jnp.float32)
 
     def body(a, carry):
         x = [[w_ref[i, j, a] for j in range(4)] for i in range(4)]
@@ -125,7 +135,10 @@
             for j in range(4):
                 value = (mi[i][j] * summed[j]).astype(jnp.bfloat16)
                 settled[i][j] = value.astype(jnp.float32)
-                ss_ref[4 * a + i, pl.ds(j, 8, stride=4), :] = settled[i][j]
+            natural = jnp.dot(
+                merge, jnp.concatenate(settled[i], axis=0), preferred_element_type=jnp.float32
+            )
+            st_ref[4 * a + i] = natural.astype(st_ref.dtype)
         for p in range(2):
             pair = []
             for q in range(2):
@@ -142,7 +155,6 @@
         return carry
 
     lax.fori_loop(0, 8, body, 0)
-    st_ref[...] = ss_ref[...].astype(st_ref.dtype)
 
 
 def finish_kernel(st_ref, back_ref, ret_ref, out_ref, tend_ref, t2_ref):
@@ -219,10 +231,7 @@
             jax.ShapeDtypeStruct((4, 8, features), jnp.float32),
             jax.ShapeDtypeStruct((4, 8, features), jnp.float32),
         ],
-        scratch_shapes=[
-            pltpu.VMEM((rows, cols, LANES), jnp.float32),
-            pltpu.VMEM((3, 4, 4, 8, 8, LANES), jnp.float32),
-        ],
+        scratch_shapes=[pltpu.VMEM((3, 4, 4, 8, 8, LANES), jnp.float32)],
         compiler_params=pltpu.CompilerParams(dimension_semantics=("arbitrary",)),
     )(tracers, coef)
 
@@ -249,10 +258,7 @@
             jax.ShapeDtypeStruct((32, 32, features), jnp.bfloat16),
             jax.ShapeDtypeStruct((256, features), jnp.bfloat16),
         ],
-        scratch_shapes=[
-            pltpu.VMEM((32, 32, LANES), jnp.float32),
-            pltpu.VMEM((2, 4, 4, 8, 8, LANES), jnp.float32),
-        ],
+        scratch_shapes=[pltpu.VMEM((2, 4, 4, 8, 8, LANES), jnp.float32)],
         compiler_params=pltpu.CompilerParams(dimension_semantics=("arbitrary",)),
     )(w, top, bot, lax_halo, rax_halo, coef)
 

time: 111 us -> 121 us (1.090)
  Pallas kernels: 23.7 us -> 34.1 us
  starting transfers between devices: 23.5 us -> 20.3 us
  loops' own time: 1.28 us -> 3.25 us
  matrix products: 2.98 us -> 4.41 us
    pallas_call x1, Pallas kernels: 9.7 us -> 15.7 us  [run_section(): pl.pallas_call(section_kernel, grid=(nb,), in_specs=[spec((rows, cols, LA...]
    pallas_call x1, Pallas kernels: 8.12 us -> 12.6 us  [run_settle(): pl.pallas_call(settle_kernel, grid=(nb,), in_specs=[spec((4, 4, 8, 8, LAN...]
    all_to_all x1, starting transfers between devices: 6.69 us -> 3.57 us  [on_device(): lax.all_to_all(replies, ('elem', 'sub'), split_axis=0, concat_axis=0, til...]
    another operation x1, loops' own time: 1.28 us -> 3.25 us  [on_device(): final_state = lax.fori_loop(0, jnp.max(span_cost), substep, start_state)]
    dot_general x1 -> x4, matrix products: 0.48 us -> 1.91 us  [substep(): jnp.einsum('crm,clm->crl', current, diff_inverse, preferred_element_type=...]
  transfers between devices with their start and end apart: 6 -> 6, of which waited for: 5 -> 5; matrix products, arithmetic and copies ran while one was open for 3% -> 2% of each run, Pallas kernels for 0% -> 0%
where the time goes in v8:
time: 121 us
  waiting for transfers between devices  45.3 us (37%)
  Pallas kernels  34.1 us (28%)
  starting transfers between devices  20.3 us (17%)
  local copies, waits for them, and re-layouts  10.2 us (8%)
  matrix products  4.41 us (4%)
  loops' own time  3.25 us (3%)
  other arithmetic  2.94 us (2%)
    all_to_all x1, waiting for transfers between devices, on_device(): lax.all_to_all(outgoing, ('elem', 'sub'), split_axis=0, concat_axis=0, ti...  20.4 us
    all_to_all x1, waiting for transfers between devices, on_device(): lax.all_to_all(replies, ('elem', 'sub'), split_axis=0, concat_axis=0, til...  18.4 us
    pallas_call x1, Pallas kernels, run_section(): pl.pallas_call(section_kernel, grid=(nb,), in_specs=[spec((rows, cols, LA...  15.7 us
    pallas_call x1, Pallas kernels, run_settle(): pl.pallas_call(settle_kernel, grid=(nb,), in_specs=[spec((4, 4, 8, 8, LAN...  12.6 us
    all_to_all x1, starting transfers between devices, on_device(): lax.all_to_all(outgoing, ('elem', 'sub'), split_axis=0, concat_axis=0, ti...  11 us
    ppermute x4, waiting for transfers between devices, shift(): lax.ppermute(x, axis, [(k, (k + step) % count) for k in range(count)])  6.42 us
    ppermute x4, starting transfers between devices, shift(): lax.ppermute(x, axis, [(k, (k + step) % count) for k in range(count)])  5.76 us
    pallas_call x1, Pallas kernels, run_finish(): pl.pallas_call(finish_kernel, grid=(nb,), in_specs=[spec((rows, cols, wid...  4.03 us
  transfers between devices with their start and end apart: 6, of which 5 were waited for; matrix products, arithmetic and copies ran while one was open for 2% of the time, Pallas kernels for 0%

profile of v8, /device:TPU:1, one launch (start us, length us, event | category | flops | bytes accessed | tf_op | source)
XLA Modules:
  0.0 120.7 jit_solution(15832522257801710016)
XLA Ops:
  0.0 0.8 pad_maximum_fusion
  0.8 1.9 %broadcast_in_dim.27.coef_ref = f32[4,32,32,128]{3,2,1,0:T(8,128)} broadcast(f32[4,32,32]{2,1,0:T(8,128)S(1)} %pad_maximum_fusion), dimensions={0,1,2} | broadcast | bytes 2113536 | tf_op jit(solution)/shard_map/broadcast_in_dim | solution.py:296
  2.7 15.7 %shard_map.82 = (f32[4,4,8,8,1024]{4,3,2,1,0:T(8,128)}, f32[4,8,1024]{2,1,0:T(8,128)}, f32[4,8,1024]{2,1,0:T(8,128)}, f32[4,8,1024]{2,1,0:T(8,128)}, f32[4,8,1024]{2,1,0:T(8,128)}) custom-call(bf16[32,32,1024]{2,1,0:T(8,128)(2,1)} %q_ref.1, f32[4,32,32,128]{3,2,1,0:T(8,128)} %broadcast_in_dim.27.coef_ref), custom_call_target="tpu_custom_call" | custom-call | tf_op jit(solution)/shard_map/pallas_call | solution.py:213
  18.4 3.1 %collective-permute-start = (f32[4,8,1024]{2,1,0:T(8,128)}, f32[4,8,1024]{2,1,0:T(8,128)S(1)}, u32[]{:S(2)}, u32[]{:S(2)}) collective-permute-start(f32[4,8,1024]{2,1,0:T(8,128)} %get-tuple-element.43), channel_id=1, source_target_pairs={{0,4},{4,8},{8,12},{12,16},{16,20},{20,24},{24,28},{28,32},{32,36}... | collective-permute-start | bytes 393224 | tf_op jit(solution)/shard_map/ppermute | solution.py:289
  21.5 0.1 reshape.150
  21.6 0.2 copy.19
  21.8 0.1 reshape.151
  21.9 0.1 broadcast_select_fusion
  22.0 0.2 convert_reduce_fusion
  22.2 1.5 %collective-permute-done.top_ref = f32[4,8,1024]{2,1,0:T(8,128)S(1)} collective-permute-done((f32[4,8,1024]{2,1,0:T(8,128)}, f32[4,8,1024]{2,1,0:T(8,128)S(1)}, u32[]{:S(2)}, u32[]{:S(2)}) %collective-permute-start) | collective-permute-done | bytes 131104 | tf_op jit(solution)/shard_map/ppermute | solution.py:289
  23.7 2.3 %collective-permute-done.1.bot_ref = f32[4,8,1024]{2,1,0:T(8,128)S(1)} collective-permute-done((f32[4,8,1024]{2,1,0:T(8,128)}, f32[4,8,1024]{2,1,0:T(8,128)S(1)}, u32[]{:S(2)}, u32[]{:S(2)}) %collective-permute-start.1) | collective-permute-done | bytes 131104 | tf_op jit(solution)/shard_map/ppermute | solution.py:289
  26.1 0.6 copy-done.2
  26.7 1.8 %shard_map.83 = (f32[4,8,1024]{2,1,0:T(8,128)}, f32[4,8,1024]{2,1,0:T(8,128)}) custom-call(f32[4,8,1024]{2,1,0:T(8,128)} %get-tuple-element.45.cl_ref, f32[4,8,1024]{2,1,0:T(8,128)} %get-tuple-element.46.cr_ref, f32[4,8,1024]{2,1,0:T(8,128)} %copy-done.1, f32[4,8,1024]{2,1,0:T(8,128)} %copy-done.2), custom_call_target="tpu_custom_call" | custom-call | tf_op jit(solution)/shard_map/pallas_call | solution.py:195
  28.5 1.2 %collective-permute-start.2 = (f32[4,8,1024]{2,1,0:T(8,128)}, f32[4,8,1024]{2,1,0:T(8,128)S(1)}, u32[]{:S(2)}, u32[]{:S(2)}) collective-permute-start(f32[4,8,1024]{2,1,0:T(8,128)} %get-tuple-element.47), channel_id=1, source_target_pairs={{0,1},{1,2},{2,3},{3,0},{4,5},{5,6},{6,7},{7,4},{8,9},{9,10},{10,1... | collective-permute-start | bytes 393224 | tf_op jit(solution)/shard_map/ppermute | solution.py:289
  29.7 1.5 %collective-permute-start.3 = (f32[4,8,1024]{2,1,0:T(8,128)}, f32[4,8,1024]{2,1,0:T(8,128)S(1)}, u32[]{:S(2)}, u32[]{:S(2)}) collective-permute-start(f32[4,8,1024]{2,1,0:T(8,128)} %get-tuple-element.48), channel_id=1, source_target_pairs={{0,3},{1,0},{2,1},{3,2},{4,7},{5,4},{6,5},{7,6},{8,11},{9,8},{10,9... | collective-permute-start | bytes 393224 | tf_op jit(solution)/shard_map/ppermute | solution.py:289
  31.2 2.6 %collective-permute-done.2.lax_ref = f32[4,8,1024]{2,1,0:T(8,128)S(1)} collective-permute-done((f32[4,8,1024]{2,1,0:T(8,128)}, f32[4,8,1024]{2,1,0:T(8,128)S(1)}, u32[]{:S(2)}, u32[]{:S(2)}) %collective-permute-start.2) | collective-permute-done | bytes 131104 | tf_op jit(solution)/shard_map/ppermute | solution.py:289
  33.8 0.6 copy-done.3
  34.4 0.1 copy-done.4
  34.5 12.6 %shard_map.84 = (bf16[32,32,1024]{2,1,0:T(8,128)(2,1)}, bf16[256,1024]{1,0:T(8,128)(2,1)}) custom-call(f32[4,4,8,8,1024]{4,3,2,1,0:T(8,128)} %get-tuple-element.42.w_ref, f32[4,8,1024]{2,1,0:T(8,128)} %copy-done.1, f32[4,8,1024]{2,1,0:T(8,128)} %copy-done.2, f32[4,8,1024]{2,1,0:T(8,128)} %copy-done.3, f32[4,8,1024]{2,1,0:T(8,128)} %copy-done.4, ...), custom_call_target="tpu_custom_call" | custom-call | tf_op jit(solution)/shard_map/pallas_call | solution.py:242
  47.0 1.6 %convolution_convert_fusion.1 = bf16[128,4,1152]{2,0,1:T(8,128)(2,1)S(1)} fusion(bf16[256,128]{1,0:T(8,128)(2,1)S(1)} %broadcast_select_fusion, bf16[256,1024]{1,0:T(8,128)(2,1)} %get-tuple-element.50, s32[256]{0:T(256)S(1)} %multiply_add_fusion.1, s32[128,4]{0,1:T(4,128)S(1)} %multiply_add_fusion), kind=kOutput, calls=%fused_computation.3 | convolution fusion | flops 303890432 | bytes 1772544 | tf_op jit(solution)/shard_map/dck,kf->dcf/dot_general | solution.py:327
  48.6 1.9 %copy.22 = bf16[128,4,1152]{2,1,0:T(4,128)(2,1)} copy(bf16[128,4,1152]{2,0,1:T(8,128)(2,1)S(1)} %convolution_convert_fusion.1) | data formatting | bytes 2359296 | tf_op jit(solution)/shard_map/convert_element_type | solution.py:330
  50.6 11.0 %all-to-all-start = ((bf16[128,4,1152]{2,1,0:T(4,128)(2,1)}), bf16[128,4,1152]{2,1,0:T(4,128)(2,1)S(1)}, u32[]{:S(2)}, u32[]{:S(2)}) async-start(bf16[128,4,1152]{2,1,0:T(4,128)(2,1)} %copy.22), calls=%async_computation | async-start | bytes 2359296 | tf_op jit(solution)/shard_map/all_to_all | solution.py:331
  61.6 0.7 reduce_max.9
  62.3 20.4 %all-to-all-done = bf16[128,4,1152]{2,1,0:T(4,128)(2,1)S(1)} async-done(((bf16[128,4,1152]{2,1,0:T(4,128)(2,1)}), bf16[128,4,1152]{2,1,0:T(4,128)(2,1)S(1)}, u32[]{:S(2)}, u32[]{:S(2)}) %all-to-all-start) | async-done | bytes 1179680 | tf_op jit(solution)/shard_map/all_to_all | solution.py:331
  82.7 0.3 reshape.152
  83.0 0.1 add_reduce_fusion
  83.1 0.5 convolution_convert_fusion.3
  83.6 0.0 copy-start
  83.6 0.2 reshape.153
  83.9 0.8 copy-done
  84.7 5.4 %while.10 = (s32[]{:T(128)}, bf16[16,128,128]{2,1,0:T(8,128)(2,1)S(1)}, s32[]{:T(128)}, s32[16]{0:T(128)S(1)}, bf16[16,128,128]{2,1,0:T(8,128)(2,1)S(1)}, /*index=5*/s32[]{:T(128)}) while((s32[]{:T(128)}, bf16[16,128,128]{2,1,0:T(8,128)(2,1)S(1)}, s32[]{:T(128)}, s32[16]{0:T(128)S(1)}, bf16[16,128,128]{2,1,0:T(8,128)(2,1)S(1)}, ...), condition=%wide.region_3.4_spmd, body=%wide.region_2.3_spmd.sunk | while | flops 67633168 | bytes 2621609 | solution.py:348
  85.4 0.5 fusion.28
  86.5 0.5 fusion.28
  87.7 0.5 fusion.28
  88.9 0.5 fusion.28
  90.0 0.1 subtract_convert_fusion
  90.2 0.2 reshape.154
  90.4 0.5 convolution_convert_fusion.2
  90.9 1.2 %reshape.155 = bf16[128,4,1024]{2,1,0:T(4,128)(2,1)} reshape(bf16[512,1024]{1,0:T(8,128)(2,1)S(1)} %convolution_convert_fusion.2) | data formatting | bytes 2097152 | tf_op jit(solution)/shard_map/reshape | solution.py:358
  92.1 3.6 %all-to-all-start.1 = ((bf16[128,4,1024]{2,1,0:T(4,128)(2,1)}), bf16[128,4,1024]{2,1,0:T(4,128)(2,1)S(1)}, u32[]{:S(2)}, u32[]{:S(2)}) async-start(bf16[128,4,1024]{2,1,0:T(4,128)(2,1)} %reshape.155), calls=%async_computation.1 | async-start | bytes 2097152 | tf_op jit(solution)/shard_map/all_to_all | solution.py:359
  95.7 0.1 reduce_sum.12
  95.8 0.2 copy.18
  96.0 0.2 copy.21
  96.1 0.1 eq.92
  96.3 0.8 fusion.4.back_ref
  97.1 18.4 %all-to-all-done.1 = bf16[128,4,1024]{2,1,0:T(4,128)(2,1)S(1)} async-done(((bf16[128,4,1024]{2,1,0:T(4,128)(2,1)}), bf16[128,4,1024]{2,1,0:T(4,128)(2,1)S(1)}, u32[]{:S(2)}, u32[]{:S(2)}) %all-to-all-start.1) | async-done | bytes 1048608 | tf_op jit(solution)/shard_map/all_to_all | solution.py:359
  115.5 1.1 reshape.156.ret_ref
  116.6 4.0 %shard_map.85 = bf16[32,32,1024]{2,1,0:T(8,128)(2,1)} custom-call(bf16[32,32,1024]{2,1,0:T(8,128)(2,1)} %get-tuple-element.49.st_ref, bf16[256,512]{1,0:T(8,128)(2,1)} %fusion.4.back_ref, bf16[512,1024]{1,0:T(8,128)(2,1)} %reshape.156.ret_ref), custom_call_target="tpu_custom_call" | custom-call | tf_op jit(solution)/shard_map/pallas_call | solution.py:270
  (25 shorter events, 0.3 us)
Async XLA Ops:
  2.7 18.8 %copy-start.5 = (s32[256]{0:T(256)S(1)}, s32[256]{0:T(256)}, u32[]{:S(2)}) copy-start(s32[256]{0:T(256)} %param.15) | copy-start | bytes 3076
  18.4 5.3 %collective-permute-start = (f32[4,8,1024]{2,1,0:T(8,128)}, f32[4,8,1024]{2,1,0:T(8,128)S(1)}, u32[]{:S(2)}, u32[]{:S(2)}) collective-permute-start(f32[4,8,1024]{2,1,0:T(8,128)} %get-tuple-element.43), channel_id=1, source_target_pairs={{0,4},{4,8},{8,12},{12,16},{16,20},{20,24},{24,28},{28,32},{32,36}... | collective-permute-start | bytes 393224 | tf_op jit(solution)/shard_map/ppermute | solution.py:289
  21.5 4.6 %collective-permute-start.1 = (f32[4,8,1024]{2,1,0:T(8,128)}, f32[4,8,1024]{2,1,0:T(8,128)S(1)}, u32[]{:S(2)}, u32[]{:S(2)}) collective-permute-start(f32[4,8,1024]{2,1,0:T(8,128)} %get-tuple-element.44), channel_id=1, source_target_pairs={{0,124},{4,0},{8,4},{12,8},{16,12},{20,16},{24,20},{28,24},{32,28}... | collective-permute-start | bytes 393224 | tf_op jit(solution)/shard_map/ppermute | solution.py:289
  23.7 2.3 %copy-start.1 = (f32[4,8,1024]{2,1,0:T(8,128)}, f32[4,8,1024]{2,1,0:T(8,128)S(1)}, u32[]{:S(2)}) copy-start(f32[4,8,1024]{2,1,0:T(8,128)S(1)} %collective-permute-done.top_ref) | copy-start | bytes 393220
  26.1 0.6 copy-start.2
  28.5 5.2 %collective-permute-start.2 = (f32[4,8,1024]{2,1,0:T(8,128)}, f32[4,8,1024]{2,1,0:T(8,128)S(1)}, u32[]{:S(2)}, u32[]{:S(2)}) collective-permute-start(f32[4,8,1024]{2,1,0:T(8,128)} %get-tuple-element.47), channel_id=1, source_target_pairs={{0,1},{1,2},{2,3},{3,0},{4,5},{5,6},{6,7},{7,4},{8,9},{9,10},{10,1... | collective-permute-start | bytes 393224 | tf_op jit(solution)/shard_map/ppermute | solution.py:289
  29.7 4.0 %collective-permute-start.3 = (f32[4,8,1024]{2,1,0:T(8,128)}, f32[4,8,1024]{2,1,0:T(8,128)S(1)}, u32[]{:S(2)}, u32[]{:S(2)}) collective-permute-start(f32[4,8,1024]{2,1,0:T(8,128)} %get-tuple-element.48), channel_id=1, source_target_pairs={{0,3},{1,0},{2,1},{3,2},{4,7},{5,4},{6,5},{7,6},{8,11},{9,8},{10,9... | collective-permute-start | bytes 393224 | tf_op jit(solution)/shard_map/ppermute | solution.py:289
  33.8 0.7 copy-start.3
  33.8 0.7 copy-start.4
  50.6 11.0 %copy-start.6 = (s32[16]{0:T(128)S(1)}, s32[16]{0:T(128)}, u32[]{:S(2)}) copy-start(s32[16]{0:T(128)} %param.17) | copy-start | bytes 196
  50.6 32.1 %all-to-all-start = ((bf16[128,4,1152]{2,1,0:T(4,128)(2,1)}), bf16[128,4,1152]{2,1,0:T(4,128)(2,1)S(1)}, u32[]{:S(2)}, u32[]{:S(2)}) async-start(bf16[128,4,1152]{2,1,0:T(4,128)(2,1)} %copy.22), calls=%async_computation | async-start | bytes 2359296 | tf_op jit(solution)/shard_map/all_to_all | solution.py:331
  83.6 1.0 copy-start
  92.1 23.4 %all-to-all-start.1 = ((bf16[128,4,1024]{2,1,0:T(4,128)(2,1)}), bf16[128,4,1024]{2,1,0:T(4,128)(2,1)S(1)}, u32[]{:S(2)}, u32[]{:S(2)}) async-start(bf16[128,4,1024]{2,1,0:T(4,128)(2,1)} %reshape.155), calls=%async_computation.1 | async-start | bytes 2097152 | tf_op jit(solution)/shard_map/all_to_all | solution.py:359

commit v9 on v7

--- a/solution.py
+++ b/solution.py
@@ -38,6 +38,33 @@
 DERIV = [[float(np.float32(v)) for v in row] for row in gll_matrix()]
 
 
+def split_operator(matrix):
+    table = []
+    for i in range(2):
+        row = matrix[i]
+        table.append(tuple(float(np.float32(v)) for v in (
+            (row[0] + row[3]) / 2, (row[1] + row[2]) / 2, (row[0] - row[3]) / 2, (row[1] - row[2]) / 2
+        )))
+    return table
+
+
+GLL = gll_matrix()
+SLOPE = split_operator(GLL)
+WEAK = split_operator(diffusion_nu * GLL.T)
+
+
+def apply_split(table, t):
+    e0, d0 = t[0] + t[3], t[0] - t[3]
+    e1, d1 = t[1] + t[2], t[1] - t[2]
+    out = [None] * 4
+    for i, (ae, be, ad, bd) in enumerate(table):
+        even = ae * e0 + be * e1
+        odd = ad * d0 + bd * d1
+        out[i] = even + odd
+        out[3 - i] = odd - even
+    return out
+
+
 def mix(coefs, terms):
     total = coefs[0] * terms[0]
     for c, t in zip(coefs[1:], terms[1:]):
@@ -68,19 +95,15 @@
         mx, my, mw = (
             [[cs_ref[kind, i, j, a] for j in range(4)] for i in range(4)] for kind in range(3)
         )
-        tx = [
-            [mx[k][j] * mix(d[k], [q[m][j] for m in range(4)]) for j in range(4)]
-            for k in range(4)
-        ]
-        ty = [
-            [my[i][k] * mix(d[k], [q[i][m] for m in range(4)]) for k in range(4)]
-            for i in range(4)
-        ]
+        sx = [apply_split(SLOPE, [q[m][j] for m in range(4)]) for j in range(4)]
+        tx = [[mx[k][j] * sx[j][k] for k in range(4)] for j in range(4)]
+        wx = [apply_split(WEAK, tx[j]) for j in range(4)]
+        sy = [apply_split(SLOPE, q[i]) for i in range(4)]
+        ty = [[my[i][k] * sy[i][k] for k in range(4)] for i in range(4)]
+        wy = [apply_split(WEAK, ty[i]) for i in range(4)]
         for i in range(4):
             for j in range(4):
-                wx = mix([d[k][i] for k in range(4)], [tx[k][j] for k in range(4)])
-                wy = mix([d[k][j] for k in range(4)], [ty[i][k] for k in range(4)])
-                w_ref[i, j, a] = mw[i][j] * (q[i][j] - diffusion_nu * (wx + wy))
+                w_ref[i, j, a] = mw[i][j] * (q[i][j] - (wx[j][i] + wy[i][j]))
         return carry
 
     lax.fori_loop(0, 8, body, 0)

time: 111 us -> 110 us (level)
  no operation moved by 1% of the time
where the time goes in v9:
time: 110 us; the launch traced here: 109 us
  waiting for transfers between devices  45.1 us (41%)
  starting transfers between devices  23.6 us (21%)
  Pallas kernels  23 us (21%)
  local copies, waits for them, and re-layouts  10.1 us (9%)
  matrix products  2.98 us (3%)
  other arithmetic  2.93 us (3%)
  loops' own time  1.28 us (1%)
    all_to_all x1, waiting for transfers between devices, on_device(): lax.all_to_all(outgoing, ('elem', 'sub'), split_axis=0, concat_axis=0, ti...  20.4 us
    all_to_all x1, waiting for transfers between devices, on_device(): lax.all_to_all(replies, ('elem', 'sub'), split_axis=0, concat_axis=0, til...  18.3 us
    all_to_all x1, starting transfers between devices, on_device(): lax.all_to_all(outgoing, ('elem', 'sub'), split_axis=0, concat_axis=0, ti...  11 us
    pallas_call x1, Pallas kernels, run_section(): pl.pallas_call(section_kernel, grid=(nb,), in_specs=[spec((rows, cols, LA...  9.01 us
    pallas_call x1, Pallas kernels, run_settle(): pl.pallas_call(settle_kernel, grid=(nb,), in_specs=[spec((4, 4, 8, 8, LAN...  8.12 us
    all_to_all x1, starting transfers between devices, on_device(): lax.all_to_all(replies, ('elem', 'sub'), split_axis=0, concat_axis=0, til...  6.81 us
    ppermute x4, waiting for transfers between devices, shift(): lax.ppermute(x, axis, [(k, (k + step) % count) for k in range(count)])  6.42 us
    ppermute x4, starting transfers between devices, shift(): lax.ppermute(x, axis, [(k, (k + step) % count) for k in range(count)])  5.76 us
  transfers between devices with their start and end apart: 6, of which 5 were waited for; matrix products, arithmetic and copies ran while one was open for 3% of the time, Pallas kernels for 0%

profile of v9, /device:TPU:1, one launch (start us, length us, event | category | flops | bytes accessed | tf_op | source)
XLA Modules:
  0.0 109.1 jit_solution(1762849665839771522)
XLA Ops:
  0.0 0.8 pad_maximum_fusion
  0.8 1.9 %broadcast_in_dim.27.coef_ref = f32[4,32,32,128]{3,2,1,0:T(8,128)} broadcast(f32[4,32,32]{2,1,0:T(8,128)S(1)} %pad_maximum_fusion), dimensions={0,1,2} | broadcast | bytes 2113536 | tf_op jit(solution)/shard_map/broadcast_in_dim | solution.py:313
  2.7 9.0 %shard_map.82 = (f32[4,4,8,8,1024]{4,3,2,1,0:T(8,128)}, f32[4,8,1024]{2,1,0:T(8,128)}, f32[4,8,1024]{2,1,0:T(8,128)}, f32[4,8,1024]{2,1,0:T(8,128)}, f32[4,8,1024]{2,1,0:T(8,128)}) custom-call(bf16[32,32,1024]{2,1,0:T(8,128)(2,1)} %q_ref.1, f32[4,32,32,128]{3,2,1,0:T(8,128)} %broadcast_in_dim.27.coef_ref), custom_call_target="tpu_custom_call" | custom-call | tf_op jit(solution)/shard_map/pallas_call | solution.py:224
  11.7 3.1 %collective-permute-start = (f32[4,8,1024]{2,1,0:T(8,128)}, f32[4,8,1024]{2,1,0:T(8,128)S(1)}, u32[]{:S(2)}, u32[]{:S(2)}) collective-permute-start(f32[4,8,1024]{2,1,0:T(8,128)} %get-tuple-element.43), channel_id=1, source_target_pairs={{0,4},{4,8},{8,12},{12,16},{16,20},{20,24},{24,28},{28,32},{32,36}... | collective-permute-start | bytes 393224 | tf_op jit(solution)/shard_map/ppermute | solution.py:306
  14.8 0.0 collective-permute-start.1
  14.8 0.0 copy-done.5
  14.8 0.1 reshape.150
  15.0 0.2 copy.19
  15.1 0.1 reshape.151
  15.2 0.1 broadcast_select_fusion
  15.4 0.2 convert_reduce_fusion
  15.5 1.5 %collective-permute-done.top_ref = f32[4,8,1024]{2,1,0:T(8,128)S(1)} collective-permute-done((f32[4,8,1024]{2,1,0:T(8,128)}, f32[4,8,1024]{2,1,0:T(8,128)S(1)}, u32[]{:S(2)}, u32[]{:S(2)}) %collective-permute-start) | collective-permute-done | bytes 131104 | tf_op jit(solution)/shard_map/ppermute | solution.py:306
  17.1 2.3 %collective-permute-done.1.bot_ref = f32[4,8,1024]{2,1,0:T(8,128)S(1)} collective-permute-done((f32[4,8,1024]{2,1,0:T(8,128)}, f32[4,8,1024]{2,1,0:T(8,128)S(1)}, u32[]{:S(2)}, u32[]{:S(2)}) %collective-permute-start.1) | collective-permute-done | bytes 131104 | tf_op jit(solution)/shard_map/ppermute | solution.py:306
  19.4 0.6 copy-done.2
  20.1 1.8 %shard_map.83 = (f32[4,8,1024]{2,1,0:T(8,128)}, f32[4,8,1024]{2,1,0:T(8,128)}) custom-call(f32[4,8,1024]{2,1,0:T(8,128)} %get-tuple-element.45.cl_ref, f32[4,8,1024]{2,1,0:T(8,128)} %get-tuple-element.46.cr_ref, f32[4,8,1024]{2,1,0:T(8,128)} %copy-done.1, f32[4,8,1024]{2,1,0:T(8,128)} %copy-done.2), custom_call_target="tpu_custom_call" | custom-call | tf_op jit(solution)/shard_map/pallas_call | solution.py:206
  21.9 1.2 %collective-permute-start.2 = (f32[4,8,1024]{2,1,0:T(8,128)}, f32[4,8,1024]{2,1,0:T(8,128)S(1)}, u32[]{:S(2)}, u32[]{:S(2)}) collective-permute-start(f32[4,8,1024]{2,1,0:T(8,128)} %get-tuple-element.47), channel_id=1, source_target_pairs={{0,1},{1,2},{2,3},{3,0},{4,5},{5,6},{6,7},{7,4},{8,9},{9,10},{10,1... | collective-permute-start | bytes 393224 | tf_op jit(solution)/shard_map/ppermute | solution.py:306
  23.1 1.5 %collective-permute-start.3 = (f32[4,8,1024]{2,1,0:T(8,128)}, f32[4,8,1024]{2,1,0:T(8,128)S(1)}, u32[]{:S(2)}, u32[]{:S(2)}) collective-permute-start(f32[4,8,1024]{2,1,0:T(8,128)} %get-tuple-element.48), channel_id=1, source_target_pairs={{0,3},{1,0},{2,1},{3,2},{4,7},{5,4},{6,5},{7,6},{8,11},{9,8},{10,9... | collective-permute-start | bytes 393224 | tf_op jit(solution)/shard_map/ppermute | solution.py:306
  24.6 2.6 %collective-permute-done.2.lax_ref = f32[4,8,1024]{2,1,0:T(8,128)S(1)} collective-permute-done((f32[4,8,1024]{2,1,0:T(8,128)}, f32[4,8,1024]{2,1,0:T(8,128)S(1)}, u32[]{:S(2)}, u32[]{:S(2)}) %collective-permute-start.2) | collective-permute-done | bytes 131104 | tf_op jit(solution)/shard_map/ppermute | solution.py:306
  27.1 0.0 collective-permute-done.3.rax_ref
  27.1 0.6 copy-done.3
  27.8 0.1 copy-done.4
  27.8 8.1 %shard_map.84 = (bf16[32,32,1024]{2,1,0:T(8,128)(2,1)}, bf16[256,1024]{1,0:T(8,128)(2,1)}) custom-call(f32[4,4,8,8,1024]{4,3,2,1,0:T(8,128)} %get-tuple-element.42.w_ref, f32[4,8,1024]{2,1,0:T(8,128)} %copy-done.1, f32[4,8,1024]{2,1,0:T(8,128)} %copy-done.2, f32[4,8,1024]{2,1,0:T(8,128)} %copy-done.3, f32[4,8,1024]{2,1,0:T(8,128)} %copy-done.4, ...), custom_call_target="tpu_custom_call" | custom-call | tf_op jit(solution)/shard_map/pallas_call | solution.py:256
  36.0 1.6 %convolution_convert_fusion.1 = bf16[128,4,1152]{2,0,1:T(8,128)(2,1)S(1)} fusion(bf16[256,128]{1,0:T(8,128)(2,1)S(1)} %broadcast_select_fusion, bf16[256,1024]{1,0:T(8,128)(2,1)} %get-tuple-element.50, s32[256]{0:T(256)S(1)} %multiply_add_fusion.1, s32[128,4]{0,1:T(4,128)S(1)} %multiply_add_fusion), kind=kOutput, calls=%fused_computation.3 | convolution fusion | flops 303890432 | bytes 1772544 | tf_op jit(solution)/shard_map/dck,kf->dcf/dot_general | solution.py:344
  37.5 1.9 %copy.22 = bf16[128,4,1152]{2,1,0:T(4,128)(2,1)} copy(bf16[128,4,1152]{2,0,1:T(8,128)(2,1)S(1)} %convolution_convert_fusion.1) | data formatting | bytes 2359296 | tf_op jit(solution)/shard_map/convert_element_type | solution.py:347
  39.5 11.0 %all-to-all-start = ((bf16[128,4,1152]{2,1,0:T(4,128)(2,1)}), bf16[128,4,1152]{2,1,0:T(4,128)(2,1)S(1)}, u32[]{:S(2)}, u32[]{:S(2)}) async-start(bf16[128,4,1152]{2,1,0:T(4,128)(2,1)} %copy.22), calls=%async_computation | async-start | bytes 2359296 | tf_op jit(solution)/shard_map/all_to_all | solution.py:348
  50.5 0.7 reduce_max.9
  51.2 20.4 %all-to-all-done = bf16[128,4,1152]{2,1,0:T(4,128)(2,1)S(1)} async-done(((bf16[128,4,1152]{2,1,0:T(4,128)(2,1)}), bf16[128,4,1152]{2,1,0:T(4,128)(2,1)S(1)}, u32[]{:S(2)}, u32[]{:S(2)}) %all-to-all-start) | async-done | bytes 1179680 | tf_op jit(solution)/shard_map/all_to_all | solution.py:348
  71.6 0.3 reshape.152
  71.9 0.1 add_reduce_fusion
  72.1 0.5 convolution_convert_fusion.3
  72.5 0.0 copy-start
  72.5 0.2 reshape.153
  72.8 0.8 copy-done
  73.6 1.8 %while.10 = (s32[]{:T(128)}, bf16[16,128,128]{2,1,0:T(8,128)(2,1)S(1)}, s32[]{:T(128)}, s32[16]{0:T(128)S(1)}, bf16[16,128,128]{2,1,0:T(8,128)(2,1)S(1)}, /*index=5*/s32[]{:T(128)}) while((s32[]{:T(128)}, bf16[16,128,128]{2,1,0:T(8,128)(2,1)S(1)}, s32[]{:T(128)}, s32[16]{0:T(128)S(1)}, bf16[16,128,128]{2,1,0:T(8,128)(2,1)S(1)}, ...), condition=%wide.region_3.4_spmd, body=%wide.region_2.3_spmd.sunk | while | flops 67633168 | bytes 2621609 | solution.py:365
  74.3 0.5 fusion.28
  75.4 0.1 subtract_convert_fusion
  75.5 0.2 reshape.154
  75.8 0.5 convolution_convert_fusion.2
  76.2 1.2 %reshape.155 = bf16[128,4,1024]{2,1,0:T(4,128)(2,1)} reshape(bf16[512,1024]{1,0:T(8,128)(2,1)S(1)} %convolution_convert_fusion.2) | data formatting | bytes 2097152 | tf_op jit(solution)/shard_map/reshape | solution.py:375
  77.5 6.8 %all-to-all-start.1 = ((bf16[128,4,1024]{2,1,0:T(4,128)(2,1)}), bf16[128,4,1024]{2,1,0:T(4,128)(2,1)S(1)}, u32[]{:S(2)}, u32[]{:S(2)}) async-start(bf16[128,4,1024]{2,1,0:T(4,128)(2,1)} %reshape.155), calls=%async_computation.1 | async-start | bytes 2097152 | tf_op jit(solution)/shard_map/all_to_all | solution.py:376
  84.3 0.1 reduce_sum.12
  84.4 0.2 copy.18
  84.6 0.2 copy.21
  84.7 0.1 eq.92
  84.9 0.8 fusion.4.back_ref
  85.7 18.3 %all-to-all-done.1 = bf16[128,4,1024]{2,1,0:T(4,128)(2,1)S(1)} async-done(((bf16[128,4,1024]{2,1,0:T(4,128)(2,1)}), bf16[128,4,1024]{2,1,0:T(4,128)(2,1)S(1)}, u32[]{:S(2)}, u32[]{:S(2)}) %all-to-all-start.1) | async-done | bytes 1048608 | tf_op jit(solution)/shard_map/all_to_all | solution.py:376
  104.0 1.1 %reshape.156.ret_ref = bf16[512,1024]{1,0:T(8,128)(2,1)} reshape(bf16[128,4,1024]{2,1,0:T(4,128)(2,1)S(1)} %all-to-all-done.1) | data formatting | bytes 2097152 | tf_op jit(solution)/shard_map/reshape | solution.py:377
  105.1 4.0 %shard_map.85 = bf16[32,32,1024]{2,1,0:T(8,128)(2,1)} custom-call(bf16[32,32,1024]{2,1,0:T(8,128)(2,1)} %get-tuple-element.49.st_ref, bf16[256,512]{1,0:T(8,128)(2,1)} %fusion.4.back_ref, bf16[512,1024]{1,0:T(8,128)(2,1)} %reshape.156.ret_ref), custom_call_target="tpu_custom_call" | custom-call | tf_op jit(solution)/shard_map/pallas_call | solution.py:287
  (16 shorter events, 0.2 us)
Async XLA Ops:
  2.7 12.1 %copy-start.5 = (s32[256]{0:T(256)S(1)}, s32[256]{0:T(256)}, u32[]{:S(2)}) copy-start(s32[256]{0:T(256)} %param.15) | copy-start | bytes 3076
  11.7 5.3 %collective-permute-start = (f32[4,8,1024]{2,1,0:T(8,128)}, f32[4,8,1024]{2,1,0:T(8,128)S(1)}, u32[]{:S(2)}, u32[]{:S(2)}) collective-permute-start(f32[4,8,1024]{2,1,0:T(8,128)} %get-tuple-element.43), channel_id=1, source_target_pairs={{0,4},{4,8},{8,12},{12,16},{16,20},{20,24},{24,28},{28,32},{32,36}... | collective-permute-start | bytes 393224 | tf_op jit(solution)/shard_map/ppermute | solution.py:306
  14.8 4.6 %collective-permute-start.1 = (f32[4,8,1024]{2,1,0:T(8,128)}, f32[4,8,1024]{2,1,0:T(8,128)S(1)}, u32[]{:S(2)}, u32[]{:S(2)}) collective-permute-start(f32[4,8,1024]{2,1,0:T(8,128)} %get-tuple-element.44), channel_id=1, source_target_pairs={{0,124},{4,0},{8,4},{12,8},{16,12},{20,16},{24,20},{28,24},{32,28}... | collective-permute-start | bytes 393224 | tf_op jit(solution)/shard_map/ppermute | solution.py:306
  17.1 2.3 %copy-start.1 = (f32[4,8,1024]{2,1,0:T(8,128)}, f32[4,8,1024]{2,1,0:T(8,128)S(1)}, u32[]{:S(2)}) copy-start(f32[4,8,1024]{2,1,0:T(8,128)S(1)} %collective-permute-done.top_ref) | copy-start | bytes 393220
  19.4 0.6 copy-start.2
  21.9 5.2 %collective-permute-start.2 = (f32[4,8,1024]{2,1,0:T(8,128)}, f32[4,8,1024]{2,1,0:T(8,128)S(1)}, u32[]{:S(2)}, u32[]{:S(2)}) collective-permute-start(f32[4,8,1024]{2,1,0:T(8,128)} %get-tuple-element.47), channel_id=1, source_target_pairs={{0,1},{1,2},{2,3},{3,0},{4,5},{5,6},{6,7},{7,4},{8,9},{9,10},{10,1... | collective-permute-start | bytes 393224 | tf_op jit(solution)/shard_map/ppermute | solution.py:306
  23.1 4.0 %collective-permute-start.3 = (f32[4,8,1024]{2,1,0:T(8,128)}, f32[4,8,1024]{2,1,0:T(8,128)S(1)}, u32[]{:S(2)}, u32[]{:S(2)}) collective-permute-start(f32[4,8,1024]{2,1,0:T(8,128)} %get-tuple-element.48), channel_id=1, source_target_pairs={{0,3},{1,0},{2,1},{3,2},{4,7},{5,4},{6,5},{7,6},{8,11},{9,8},{10,9... | collective-permute-start | bytes 393224 | tf_op jit(solution)/shard_map/ppermute | solution.py:306
  27.1 0.7 copy-start.3
  27.1 0.7 copy-start.4
  39.5 11.0 %copy-start.6 = (s32[16]{0:T(128)S(1)}, s32[16]{0:T(128)}, u32[]{:S(2)}) copy-start(s32[16]{0:T(128)} %param.17) | copy-start | bytes 196
  39.5 32.1 %all-to-all-start = ((bf16[128,4,1152]{2,1,0:T(4,128)(2,1)}), bf16[128,4,1152]{2,1,0:T(4,128)(2,1)S(1)}, u32[]{:S(2)}, u32[]{:S(2)}) async-start(bf16[128,4,1152]{2,1,0:T(4,128)(2,1)} %copy.22), calls=%async_computation | async-start | bytes 2359296 | tf_op jit(solution)/shard_map/all_to_all | solution.py:348
  72.5 1.0 copy-start
  77.5 26.5 %all-to-all-start.1 = ((bf16[128,4,1024]{2,1,0:T(4,128)(2,1)}), bf16[128,4,1024]{2,1,0:T(4,128)(2,1)S(1)}, u32[]{:S(2)}, u32[]{:S(2)}) async-start(bf16[128,4,1024]{2,1,0:T(4,128)(2,1)} %reshape.155), calls=%async_computation.1 | async-start | bytes 2097152 | tf_op jit(solution)/shard_map/all_to_all | solution.py:376

commit v10 on v3

--- a/solution.py
+++ b/solution.py
@@ -38,6 +38,33 @@
 DERIV = [[float(np.float32(v)) for v in row] for row in gll_matrix()]
 
 
+def split_operator(matrix):
+    table = []
+    for i in range(2):
+        row = matrix[i]
+        table.append(tuple(float(np.float32(v)) for v in (
+            (row[0] + row[3]) / 2, (row[1] + row[2]) / 2, (row[0] - row[3]) / 2, (row[1] - row[2]) / 2
+        )))
+    return table
+
+
+GLL = gll_matrix()
+SLOPE = split_operator(GLL)
+WEAK = split_operator(diffusion_nu * GLL.T)
+
+
+def apply_split(table, t):
+    e0, d0 = t[0] + t[3], t[0] - t[3]
+    e1, d1 = t[1] + t[2], t[1] - t[2]
+    out = [None] * 4
+    for i, (ae, be, ad, bd) in enumerate(table):
+        even = ae * e0 + be * e1
+        odd = ad * d0 + bd * d1
+        out[i] = even + odd
+        out[3 - i] = odd - even
+    return out
+
+
 def mix(coefs, terms):
     total = coefs[0] * terms[0]
     for c, t in zip(coefs[1:], terms[1:]):
@@ -56,19 +83,15 @@
              for i in range(4)]
             for kind in range(3)
         )
-        tx = [
-            [mx[k][j] * mix(d[k], [q[m][j] for m in range(4)]) for j in range(4)]
-            for k in range(4)
-        ]
-        ty = [
-            [my[i][k] * mix(d[k], [q[i][m] for m in range(4)]) for k in range(4)]
-            for i in range(4)
-        ]
+        sx = [apply_split(SLOPE, [q[m][j] for m in range(4)]) for j in range(4)]
+        tx = [[mx[k][j] * sx[j][k] for k in range(4)] for j in range(4)]
+        wx = [apply_split(WEAK, tx[j]) for j in range(4)]
+        sy = [apply_split(SLOPE, q[i]) for i in range(4)]
+        ty = [[my[i][k] * sy[i][k] for k in range(4)] for i in range(4)]
+        wy = [apply_split(WEAK, ty[i]) for i in range(4)]
         for i in range(4):
             for j in range(4):
-                wx = mix([d[k][i] for k in range(4)], [tx[k][j] for k in range(4)])
-                wy = mix([d[k][j] for k in range(4)], [ty[i][k] for k in range(4)])
-                w_ref[i, j, a] = mw[i][j] * (q[i][j] - diffusion_nu * (wx + wy))
+                w_ref[i, j, a] = mw[i][j] * (q[i][j] - (wx[j][i] + wy[i][j]))
         return carry
 
     lax.fori_loop(0, 8, body, 0)

time: 109 us -> 108 us (level)
  no operation moved by 1% of the time
where the time goes in v10:
time: 108 us; the launch traced here: 107 us
  waiting for transfers between devices  45.1 us (42%)
  Pallas kernels  19.8 us (18%)
  starting transfers between devices  19.7 us (18%)
  local copies, waits for them, and re-layouts  11.1 us (10%)
  matrix products  5.39 us (5%)
  other arithmetic  3.02 us (3%)
  loops' own time  2.59 us (2%)
    all_to_all x1, waiting for transfers between devices, on_device(): lax.all_to_all(outgoing, ('elem', 'sub'), split_axis=0, concat_axis=0, ti...  20.4 us
    all_to_all x1, waiting for transfers between devices, on_device(): lax.all_to_all(replies, ('elem', 'sub'), split_axis=0, concat_axis=0, til...  19.1 us
    all_to_all x1, starting transfers between devices, on_device(): lax.all_to_all(outgoing, ('elem', 'sub'), split_axis=0, concat_axis=0, ti...  9.74 us
    pallas_call x1, Pallas kernels, run_section(): pl.pallas_call(section_kernel, grid=(nb,), in_specs=[spec((rows, cols, LA...  8.82 us
    pallas_call x1, Pallas kernels, run_settle(): pl.pallas_call(settle_kernel, grid=(nb,), in_specs=[spec((4, 4, 8, 8, LAN...  7.86 us
    ppermute x4, starting transfers between devices, shift(): lax.ppermute(x, axis, [(k, (k + step) % count) for k in range(count)])  5.71 us
    ppermute x4, waiting for transfers between devices, shift(): lax.ppermute(x, axis, [(k, (k + step) % count) for k in range(count)])  5.59 us
    all_to_all x1, starting transfers between devices, on_device(): lax.all_to_all(replies, ('elem', 'sub'), split_axis=0, concat_axis=0, til...  4.24 us
  transfers between devices with their start and end apart: 6, of which 5 were waited for; matrix products, arithmetic and copies ran while one was open for 5% of the time, Pallas kernels for 0%

profile of v10, /device:TPU:1, one launch (start us, length us, event | category | flops | bytes accessed | tf_op | source)
XLA Modules:
  0.0 107.0 jit_solution(5321598643728132582)
XLA Ops:
  0.0 0.8 pad_maximum_fusion.2
  0.8 1.9 %broadcast_in_dim.27.coef_ref = f32[4,32,32,128]{3,2,1,0:T(8,128)} broadcast(f32[4,32,32]{2,1,0:T(8,128)S(1)} %pad_maximum_fusion.2), dimensions={0,1,2} | broadcast | bytes 2113536 | tf_op jit(solution)/shard_map/broadcast_in_dim | solution.py:262
  2.7 8.8 %shard_map.82 = (f32[4,4,8,8,1024]{4,3,2,1,0:T(8,128)}, f32[4,8,1024]{2,1,0:T(8,128)}, f32[4,8,1024]{2,1,0:T(8,128)}, f32[4,8,1024]{2,1,0:T(8,128)}, f32[4,8,1024]{2,1,0:T(8,128)}) custom-call(bf16[32,32,1024]{2,1,0:T(8,128)(2,1)} %q_ref.1, f32[4,32,32,128]{3,2,1,0:T(8,128)} %broadcast_in_dim.27.coef_ref), custom_call_target="tpu_custom_call" | custom-call | tf_op jit(solution)/shard_map/pallas_call | solution.py:188
  11.5 3.1 %collective-permute-start = (f32[4,8,1024]{2,1,0:T(8,128)}, f32[4,8,1024]{2,1,0:T(8,128)S(1)}, u32[]{:S(2)}, u32[]{:S(2)}) collective-permute-start(f32[4,8,1024]{2,1,0:T(8,128)} %get-tuple-element.41), channel_id=1, source_target_pairs={{0,4},{4,8},{8,12},{12,16},{16,20},{20,24},{24,28},{28,32},{32,36}... | collective-permute-start | bytes 393224 | tf_op jit(solution)/shard_map/ppermute | solution.py:255
  14.6 0.8 fusion.21
  15.4 0.8 fusion.23
  16.2 0.1 reshape.154
  16.3 0.2 copy.17
  16.5 0.1 reshape.155
  16.6 0.1 broadcast_select_fusion
  16.7 0.8 slice.62
  17.6 0.8 slice.55
  18.4 0.2 convert_reduce_fusion
  18.6 0.6 collective-permute-done.1.bot_ref
  19.2 0.9 maximum_add_fusion
  20.1 2.5 %collective-permute-start.3 = (f32[4,8,1024]{2,1,0:T(8,128)S(1)}, f32[4,8,1024]{2,1,0:T(8,128)S(1)}, u32[]{:S(2)}, u32[]{:S(2)}) collective-permute-start(f32[4,8,1024]{2,1,0:T(8,128)S(1)} %pad_maximum_fusion.1), channel_id=1, source_target_pairs={{0,3},{1,0},{2,1},{3,2},{4,7},{5,4},{6,5},{7,6},{8,11},{9,8},{10,9... | collective-permute-start | bytes 393224 | tf_op jit(solution)/shard_map/ppermute | solution.py:255
  22.7 0.1 collective-permute-start.2
  22.8 1.8 %collective-permute-done.3.rax_ref = f32[4,8,1024]{2,1,0:T(8,128)S(1)} collective-permute-done((f32[4,8,1024]{2,1,0:T(8,128)S(1)}, f32[4,8,1024]{2,1,0:T(8,128)S(1)}, u32[]{:S(2)}, u32[]{:S(2)}) %collective-permute-start.3) | collective-permute-done | bytes 131104 | tf_op jit(solution)/shard_map/ppermute | solution.py:255
  24.6 3.2 %collective-permute-done.2.lax_ref = f32[4,8,1024]{2,1,0:T(8,128)S(1)} collective-permute-done((f32[4,8,1024]{2,1,0:T(8,128)S(1)}, f32[4,8,1024]{2,1,0:T(8,128)S(1)}, u32[]{:S(2)}, u32[]{:S(2)}) %collective-permute-start.2) | collective-permute-done | bytes 131104 | tf_op jit(solution)/shard_map/ppermute | solution.py:255
  27.8 0.6 copy-done.4
  28.5 7.9 %shard_map.83 = (bf16[32,32,1024]{2,1,0:T(8,128)(2,1)}, bf16[256,1024]{1,0:T(8,128)(2,1)}) custom-call(f32[4,4,8,8,1024]{4,3,2,1,0:T(8,128)} %get-tuple-element.40.w_ref, f32[4,8,1024]{2,1,0:T(8,128)} %copy-done.1, f32[4,8,1024]{2,1,0:T(8,128)} %copy-done.2, f32[4,8,1024]{2,1,0:T(8,128)} %copy-done.4, f32[4,8,1024]{2,1,0:T(8,128)} %copy-done.3, ...), custom_call_target="tpu_custom_call" | custom-call | tf_op jit(solution)/shard_map/pallas_call | solution.py:216
  36.3 1.6 %convolution_convert_fusion.1 = bf16[512,1152]{1,0:T(8,128)(2,1)S(1)} fusion(bf16[256,128]{1,0:T(8,128)(2,1)S(1)} %broadcast_select_fusion, bf16[256,1024]{1,0:T(8,128)(2,1)} %get-tuple-element.46, s32[256]{0:T(256)S(1)} %multiply_add_fusion), kind=kOutput, calls=%fused_computation.3 | convolution fusion | flops 303890432 | bytes 1770496 | tf_op jit(solution)/shard_map/dot_general | solution.py:297
  37.9 1.2 %reshape.156 = bf16[128,4,1152]{2,1,0:T(4,128)(2,1)} reshape(bf16[512,1152]{1,0:T(8,128)(2,1)S(1)} %convolution_convert_fusion.1) | data formatting | bytes 2359296 | tf_op jit(solution)/shard_map/reshape | solution.py:298
  39.1 9.7 %all-to-all-start = ((bf16[128,4,1152]{2,1,0:T(4,128)(2,1)}), bf16[128,4,1152]{2,1,0:T(4,128)(2,1)S(1)}, u32[]{:S(2)}, u32[]{:S(2)}) async-start(bf16[128,4,1152]{2,1,0:T(4,128)(2,1)} %reshape.156), calls=%async_computation | async-start | bytes 2359296 | tf_op jit(solution)/shard_map/all_to_all | solution.py:299
  48.8 0.7 reduce_max.9
  49.5 20.4 %all-to-all-done = bf16[128,4,1152]{2,1,0:T(4,128)(2,1)S(1)} async-done(((bf16[128,4,1152]{2,1,0:T(4,128)(2,1)}), bf16[128,4,1152]{2,1,0:T(4,128)(2,1)S(1)}, u32[]{:S(2)}, u32[]{:S(2)}) %all-to-all-start) | async-done | bytes 1179680 | tf_op jit(solution)/shard_map/all_to_all | solution.py:299
  69.9 0.3 reshape.157
  70.2 0.1 add_reduce_fusion
  70.4 0.5 convolution_convert_fusion.3
  70.9 0.2 reshape.158
  71.1 0.8 copy-done
  71.9 4.2 %while.10 = (s32[]{:T(128)}, bf16[16,128,128]{2,1,0:T(8,128)(2,1)S(1)}, s32[]{:T(128)}, s32[16]{0:T(128)S(1)}, bf16[16,128,128]{2,1,0:T(8,128)(2,1)S(1)}, /*index=5*/s32[]{:T(128)}) while((s32[]{:T(128)}, bf16[16,128,128]{2,1,0:T(8,128)(2,1)S(1)}, s32[]{:T(128)}, s32[16]{0:T(128)S(1)}, bf16[16,128,128]{2,1,0:T(8,128)(2,1)S(1)}, ...), condition=%wide.region_3.4_spmd, body=%wide.region_2.3_spmd.sunk | while | flops 67633168 | bytes 2621609 | solution.py:317
  72.6 0.5 fusion.33
  73.8 0.5 fusion.33
  74.9 0.5 fusion.33
  76.1 0.1 subtract_convert_fusion
  76.2 0.2 reshape.159
  76.4 0.5 convolution_convert_fusion.2
  76.9 1.2 %reshape.160 = bf16[128,4,1024]{2,1,0:T(4,128)(2,1)} reshape(bf16[512,1024]{1,0:T(8,128)(2,1)S(1)} %convolution_convert_fusion.2) | data formatting | bytes 2097152 | tf_op jit(solution)/shard_map/reshape | solution.py:327
  78.1 4.2 %all-to-all-start.1 = ((bf16[128,4,1024]{2,1,0:T(4,128)(2,1)}), bf16[128,4,1024]{2,1,0:T(4,128)(2,1)S(1)}, u32[]{:S(2)}, u32[]{:S(2)}) async-start(bf16[128,4,1024]{2,1,0:T(4,128)(2,1)} %reshape.160), calls=%async_computation.1 | async-start | bytes 2097152 | tf_op jit(solution)/shard_map/all_to_all | solution.py:328
  82.4 0.1 reduce_sum.12
  82.5 0.2 copy.16
  82.7 0.2 copy.19
  82.8 0.1 eq.85
  83.0 19.1 %all-to-all-done.1 = bf16[128,4,1024]{2,1,0:T(4,128)(2,1)S(1)} async-done(((bf16[128,4,1024]{2,1,0:T(4,128)(2,1)}), bf16[128,4,1024]{2,1,0:T(4,128)(2,1)S(1)}, u32[]{:S(2)}, u32[]{:S(2)}) %all-to-all-start.1) | async-done | bytes 1048608 | tf_op jit(solution)/shard_map/all_to_all | solution.py:328
  102.1 0.3 reshape.161
  102.4 1.5 %fusion.5.tend_ref = f32[256,1024]{1,0:T(8,128)} fusion(bf16[512,1024]{1,0:T(8,128)(2,1)S(1)} %reshape.161, s32[256]{0:T(256)S(1)} %eq.85), kind=kOutput, calls=%fused_computation.15 | convolution fusion | flops 268566528 | bytes 2098176 | tf_op jit(solution)/shard_map/dot_general | solution.py:332
  103.8 3.1 %shard_map.84 = bf16[32,32,1024]{2,1,0:T(8,128)(2,1)} custom-call(bf16[32,32,1024]{2,1,0:T(8,128)(2,1)} %get-tuple-element.45.st_ref, f32[256,1024]{1,0:T(8,128)} %fusion.5.tend_ref), custom_call_target="tpu_custom_call" | custom-call | tf_op jit(solution)/shard_map/pallas_call | solution.py:243
  (29 shorter events, 0.3 us)
Async XLA Ops:
  2.7 13.5 %copy-start.5 = (s32[256]{0:T(256)S(1)}, s32[256]{0:T(256)}, u32[]{:S(2)}) copy-start(s32[256]{0:T(256)} %param.15) | copy-start | bytes 3076
  11.5 7.1 %collective-permute-start = (f32[4,8,1024]{2,1,0:T(8,128)}, f32[4,8,1024]{2,1,0:T(8,128)S(1)}, u32[]{:S(2)}, u32[]{:S(2)}) collective-permute-start(f32[4,8,1024]{2,1,0:T(8,128)} %get-tuple-element.41), channel_id=1, source_target_pairs={{0,4},{4,8},{8,12},{12,16},{16,20},{20,24},{24,28},{28,32},{32,36}... | collective-permute-start | bytes 393224 | tf_op jit(solution)/shard_map/ppermute | solution.py:255
  14.6 4.6 %collective-permute-start.1 = (f32[4,8,1024]{2,1,0:T(8,128)}, f32[4,8,1024]{2,1,0:T(8,128)S(1)}, u32[]{:S(2)}, u32[]{:S(2)}) collective-permute-start(f32[4,8,1024]{2,1,0:T(8,128)} %get-tuple-element.42), channel_id=1, source_target_pairs={{0,124},{4,0},{8,4},{12,8},{16,12},{20,16},{24,20},{28,24},{32,28}... | collective-permute-start | bytes 393224 | tf_op jit(solution)/shard_map/ppermute | solution.py:255
  18.6 9.2 %copy-start.1 = (f32[4,8,1024]{2,1,0:T(8,128)}, f32[4,8,1024]{2,1,0:T(8,128)S(1)}, u32[]{:S(2)}) copy-start(f32[4,8,1024]{2,1,0:T(8,128)S(1)} %collective-permute-done.top_ref) | copy-start | bytes 393220
  19.2 8.6 %copy-start.2 = (f32[4,8,1024]{2,1,0:T(8,128)}, f32[4,8,1024]{2,1,0:T(8,128)S(1)}, u32[]{:S(2)}) copy-start(f32[4,8,1024]{2,1,0:T(8,128)S(1)} %collective-permute-done.1.bot_ref) | copy-start | bytes 393220
  20.1 4.5 %collective-permute-start.3 = (f32[4,8,1024]{2,1,0:T(8,128)S(1)}, f32[4,8,1024]{2,1,0:T(8,128)S(1)}, u32[]{:S(2)}, u32[]{:S(2)}) collective-permute-start(f32[4,8,1024]{2,1,0:T(8,128)S(1)} %pad_maximum_fusion.1), channel_id=1, source_target_pairs={{0,3},{1,0},{2,1},{3,2},{4,7},{5,4},{6,5},{7,6},{8,11},{9,8},{10,9... | collective-permute-start | bytes 393224 | tf_op jit(solution)/shard_map/ppermute | solution.py:255
  22.7 5.1 %collective-permute-start.2 = (f32[4,8,1024]{2,1,0:T(8,128)S(1)}, f32[4,8,1024]{2,1,0:T(8,128)S(1)}, u32[]{:S(2)}, u32[]{:S(2)}) collective-permute-start(f32[4,8,1024]{2,1,0:T(8,128)S(1)} %pad_maximum_fusion), channel_id=1, source_target_pairs={{0,1},{1,2},{2,3},{3,0},{4,5},{5,6},{6,7},{7,4},{8,9},{9,10},{10,1... | collective-permute-start | bytes 393224 | tf_op jit(solution)/shard_map/ppermute | solution.py:255
  24.6 3.2 %copy-start.3 = (f32[4,8,1024]{2,1,0:T(8,128)}, f32[4,8,1024]{2,1,0:T(8,128)S(1)}, u32[]{:S(2)}) copy-start(f32[4,8,1024]{2,1,0:T(8,128)S(1)} %collective-permute-done.3.rax_ref) | copy-start | bytes 393220
  27.8 0.6 copy-start.4
  39.1 9.7 %copy-start.6 = (s32[16]{0:T(128)S(1)}, s32[16]{0:T(128)}, u32[]{:S(2)}) copy-start(s32[16]{0:T(128)} %param.17) | copy-start | bytes 196
  39.1 30.9 %all-to-all-start = ((bf16[128,4,1152]{2,1,0:T(4,128)(2,1)}), bf16[128,4,1152]{2,1,0:T(4,128)(2,1)S(1)}, u32[]{:S(2)}, u32[]{:S(2)}) async-start(bf16[128,4,1152]{2,1,0:T(4,128)(2,1)} %reshape.156), calls=%async_computation | async-start | bytes 2359296 | tf_op jit(solution)/shard_map/all_to_all | solution.py:299
  70.8 1.0 copy-start
  78.1 24.0 %all-to-all-start.1 = ((bf16[128,4,1024]{2,1,0:T(4,128)(2,1)}), bf16[128,4,1024]{2,1,0:T(4,128)(2,1)S(1)}, u32[]{:S(2)}, u32[]{:S(2)}) async-start(bf16[128,4,1024]{2,1,0:T(4,128)(2,1)} %reshape.160), calls=%async_computation.1 | async-start | bytes 2097152 | tf_op jit(solution)/shard_map/all_to_all | solution.py:328
